TPU v7x, 256 devices: a whole 4x4x8 slice. The times are simulated.
256 devices in a mesh: grp: 4 (over x), tok: 8 (over z), mdl: 8 (over y, core).
Axes of the slice: x: 4, y: 4, z: 8, core: 2. Of those that a mesh axis runs over, the one named last changes fastest.
Arguments:
- hidden_in: bfloat16 [4, 1024, 5120], P('grp', 'tok', 'mdl'), may hold values from -8 to 8
- seg_ids: int32 [4, 1024], replicated, may hold values from 0 to 3, never falling along the last dimension, each value on 1 to 768 neighbouring positions
- request_prefix: int32 [4, 4], replicated, may hold values from 0 to 1
- page_table: int32 [32], replicated, may hold values from 0 to 31, each once
- prefix_cache: bfloat16 [32, 256, 8, 256], P(('grp', 'mdl'), None, 'tok'), may hold values from -200 to 200
- attn_gain: float32 [5120], P('mdl'), may hold values from 0.1 to 1.9
- w_query: bfloat16 [5120, 5120], P('mdl', 'tok'), may hold values from -0.078125 to 0.078125
- w_key: bfloat16 [5120, 1024], P('mdl', 'tok'), may hold values from -0.25 to 0.25
- w_value: bfloat16 [5120, 1024], P('mdl', 'tok'), may hold values from -0.078125 to 0.078125
- w_out: bfloat16 [5120, 5120], P('tok', 'mdl'), may hold values from -0.078125 to 0.078125
- ffn_gain: float32 [5120], P('mdl'), may hold values from 0.1 to 1.9
- w_gate: bfloat16 [5120, 14336], P('mdl', 'tok'), may hold values from -0.078125 to 0.078125
- w_up: bfloat16 [5120, 14336], P('mdl', 'tok'), may hold values from -0.078125 to 0.078125
- w_down: bfloat16 [14336, 5120], P('tok', 'mdl'), may hold values from -0.046875 to 0.046875
- final_gain: float32 [5120], replicated, may hold values from 0.1 to 1.9
- lm_head: bfloat16 [76800, 5120], P(('grp', 'tok', 'mdl')), may hold values from -0.25 to 0.25
Outputs:
- hidden_out: bfloat16 [4, 1024, 5120], P('grp', 'tok', 'mdl')
- new_kv: bfloat16 [4, 1024, 8, 256], P('grp', 'mdl', 'tok')
- req_norm: float32 [4, 4], P('grp')
- max_logit: float32 [4, 4], replicated
- logits: float32 [16, 76800], P(None, ('grp', 'tok', 'mdl'))
Inputs may be any that keep to these rules, and one draw needn't show every extreme that they name: `seg_ids`: requests of a group are contiguous, in order, and none is empty. `page_table`: each physical slot holds exactly one logical page.
All inputs are finite; a program needn't handle non-finite values.
Results may differ from a plain program's by a relative error of at most 0.024.
Values may be sent and summed in bfloat16 or wider, within the bound.
No kernel may reach another device: no remote copies, remote signals or barrier semaphores. Data moves between devices by JAX's collectives and lax.ppermute only.
A program may use at most 128 MiB of HBM per device.

v0:
```python
import jax
import jax.numpy as jnp
from jax import lax
from jax.sharding import PartitionSpec as P

PREFIX = 4096
PAGE = 256


EPS = 1e-06
THETA = 1000000.0
NEG = -1e30


def rotate(tensor, positions):
    half_dim = tensor.shape[-1] // 2
    frequency = THETA ** (-(jnp.arange(half_dim, dtype=jnp.float32) * 2.0 / tensor.shape[-1]))
    angles = positions.astype(jnp.float32)[:, None] * frequency[None, :]
    cosine = jnp.cos(angles)[:, None, :]
    sine_part = jnp.sin(angles)[:, None, :]
    first_part = tensor[..., :half_dim]
    second = tensor[..., half_dim:]
    return jnp.concatenate(
        [first_part * cosine - second * sine_part, second * cosine + first_part * sine_part], -1
    )


def on_device(
    hidden_in,
    seg_ids,
    request_prefix,
    page_table,
    prefix_cache,
    attn_gain,
    w_query,
    w_key,
    w_value,
    w_out,
    ffn_gain,
    w_gate,
    w_up,
    w_down,
    final_gain,
    lm_head,
):
    groups_total = seg_ids.shape[0]
    seq_len = seg_ids.shape[1]
    req_count = request_prefix.shape[1]
    tok_rows = hidden_in.shape[1]
    feat_dev = hidden_in.shape[2]
    model_width = feat_dev * lax.axis_size("mdl")
    head_dim = prefix_cache.shape[3] // 2
    kv_dev = prefix_cache.shape[2]
    heads_dev = w_query.shape[1] // head_dim
    group_size = heads_dev // kv_dev
    page_len = prefix_cache.shape[1]
    slot_total = page_table.shape[0]
    rows_mdl = seq_len // lax.axis_size("mdl")
    group_idx = lax.axis_index("grp")
    tok_idx = lax.axis_index("tok")
    mdl_idx = lax.axis_index("mdl")
    score_scale = head_dim ** (-0.5)
    tokens = hidden_in[0].astype(jnp.float32)
    squares = lax.psum(jnp.sum(tokens * tokens, -1), "mdl")
    normed = (tokens * lax.rsqrt(squares[:, None] / model_width + EPS) * attn_gain).astype(
        jnp.bfloat16
    )
    w_joined = jnp.concatenate([w_query, w_key, w_value], 1)
    partial_qkv = jnp.dot(
        lax.all_gather(normed, "tok", axis=0, tiled=True),
        w_joined,
        preferred_element_type=jnp.float32,
    )
    qkv_rows = lax.psum_scatter(partial_qkv, "mdl", scatter_dimension=0, tiled=True)
    q_cols = heads_dev * head_dim
    kv_cols = kv_dev * head_dim
    queries = qkv_rows[:, :q_cols].reshape(rows_mdl, heads_dev, head_dim)
    key_rows = qkv_rows[:, q_cols : q_cols + kv_cols].reshape(rows_mdl, kv_dev, head_dim)
    value_rows = qkv_rows[:, q_cols + kv_cols :].reshape(rows_mdl, kv_dev, head_dim)
    seg_row = lax.dynamic_index_in_dim(seg_ids, group_idx, 0, keepdims=False)
    prefix_row = lax.dynamic_index_in_dim(request_prefix, group_idx, 0, keepdims=False)
    requests = jnp.arange(req_count, dtype=jnp.int32)
    member = seg_row[:, None] == requests[None, :]
    counts = jnp.sum(member.astype(jnp.int32), 0)
    offsets = jnp.cumsum(counts) - counts
    row_start = mdl_idx * rows_mdl
    my_rows = row_start + jnp.arange(rows_mdl, dtype=jnp.int32)
    my_seg = lax.dynamic_slice_in_dim(seg_row, row_start, rows_mdl)
    my_member = my_seg[:, None] == requests[None, :]
    positions = PREFIX + my_rows - jnp.sum(jnp.where(my_member, offsets[None, :], 0), 1)
    my_prefix = jnp.sum(jnp.where(my_member, prefix_row[None, :], 0), 1)
    q_rot = (
        rotate(queries, positions)
        .astype(jnp.bfloat16)
        .reshape(rows_mdl, kv_dev, group_size, head_dim)
    )
    k_rot = rotate(key_rows, positions).astype(jnp.bfloat16)
    appended = jnp.concatenate([k_rot, value_rows.astype(jnp.bfloat16)], -1)
    suffix = lax.all_gather(appended, "mdl", axis=0, tiled=True)
    every_row = jnp.arange(seq_len, dtype=jnp.int32)
    suffix_ok = ((seg_row[None, :] == my_seg[:, None]) & (every_row[None, :] <= my_rows[:, None]))[
        :, None, None, :
    ]
    suffix_scores = (
        jnp.einsum(
            "rcgd,tcd->rcgt", q_rot, suffix[..., :head_dim], preferred_element_type=jnp.float32
        )
        * score_scale
    )
    suffix_scores = jnp.where(suffix_ok, suffix_scores, NEG)
    row_max = jnp.max(suffix_scores, -1)
    suffix_weights = jnp.where(suffix_ok, jnp.exp(suffix_scores - row_max[..., None]), 0.0)
    row_total = jnp.sum(suffix_weights, -1)
    mixed = jnp.einsum(
        "rcgt,tcd->rcgd",
        suffix_weights.astype(jnp.bfloat16),
        suffix[..., head_dim:],
        preferred_element_type=jnp.float32,
    )
    slot_ids = jnp.arange(slot_total, dtype=jnp.int32)
    pages_each = PREFIX // PAGE
    slot_prefix = jnp.sum(
        jnp.where(page_table[None, :] == slot_ids[:, None], (slot_ids // pages_each)[None, :], 0), 1
    )
    piece = lax.all_gather(prefix_cache, ("grp", "mdl"), axis=0, tiled=True)
    page_count = piece.shape[0]
    key_prefix = jnp.repeat(slot_prefix, page_len)
    allowed = (my_prefix[:, None] == key_prefix[None, :])[:, None, None, :]
    flat_pages = piece.reshape(page_count * page_len, kv_dev, 2 * head_dim)
    scores = (
        jnp.einsum(
            "rcgd,kcd->rcgk", q_rot, flat_pages[..., :head_dim], preferred_element_type=jnp.float32
        )
        * score_scale
    )
    scores = jnp.where(allowed, scores, NEG)
    new_max = jnp.maximum(row_max, jnp.max(scores, -1))
    factor = jnp.exp(row_max - new_max)
    page_weights = jnp.where(allowed, jnp.exp(scores - new_max[..., None]), 0.0)
    new_total = row_total * factor + jnp.sum(page_weights, -1)
    new_mixed = mixed * factor[..., None] + jnp.einsum(
        "rcgk,kcd->rcgd",
        page_weights.astype(jnp.bfloat16),
        flat_pages[..., head_dim:],
        preferred_element_type=jnp.float32,
    )
    attended = (
        (new_mixed / new_total[..., None])
        .astype(jnp.bfloat16)
        .reshape(rows_mdl, heads_dev * head_dim)
    )
    partial_out = jnp.dot(
        lax.all_gather(attended, "mdl", axis=0, tiled=True),
        w_out,
        preferred_element_type=jnp.float32,
    )
    residual = tokens + lax.psum_scatter(
        partial_out.astype(jnp.bfloat16), "tok", scatter_dimension=0, tiled=True
    ).astype(jnp.float32)
    squares_ffn = lax.psum(jnp.sum(residual * residual, -1), "mdl")
    ffn_input = (residual * lax.rsqrt(squares_ffn[:, None] / model_width + EPS) * ffn_gain).astype(
        jnp.bfloat16
    )
    w_pair = jnp.concatenate([w_gate, w_up], 1)
    ff_dev = w_gate.shape[1]
    partial_ffn = jnp.dot(
        lax.all_gather(ffn_input, "tok", axis=0, tiled=True),
        w_pair,
        preferred_element_type=jnp.float32,
    )
    summed = lax.psum_scatter(
        partial_ffn.astype(jnp.bfloat16), "mdl", scatter_dimension=0, tiled=True
    ).astype(jnp.float32)
    activated = (jax.nn.silu(summed[:, :ff_dev]) * summed[:, ff_dev:]).astype(jnp.bfloat16)
    partial_down = jnp.dot(
        lax.all_gather(activated, "mdl", axis=0, tiled=True),
        w_down,
        preferred_element_type=jnp.float32,
    )
    final_rows = residual + lax.psum_scatter(
        partial_down.astype(jnp.bfloat16), "tok", scatter_dimension=0, tiled=True
    ).astype(jnp.float32)
    tok_start = tok_idx * tok_rows
    my_tok_rows = tok_start + jnp.arange(tok_rows, dtype=jnp.int32)
    tok_seg = lax.dynamic_slice_in_dim(seg_row, tok_start, tok_rows)
    row_squares = jnp.sum(final_rows * final_rows, -1)
    req_squares = jnp.sum(
        jnp.where(tok_seg[:, None] == requests[None, :], row_squares[:, None], 0.0), 0
    )
    ends = offsets + counts - 1
    picked = ends[:, None] == my_tok_rows[None, :]
    last_part = jnp.sum(jnp.where(picked[:, :, None], final_rows[None, :, :], 0.0), 1)
    padded = jnp.zeros((groups_total * req_count, model_width), jnp.float32)
    padded = lax.dynamic_update_slice(
        padded, last_part, (group_idx * req_count, mdl_idx * feat_dev)
    )
    req_total = lax.psum(req_squares, ("tok", "mdl"))
    last_all = lax.psum(padded, ("grp", "tok", "mdl"))
    req_norm = jnp.sqrt(req_total / (counts.astype(jnp.float32) * model_width) + EPS)
    last_normed = (
        last_all * lax.rsqrt(jnp.mean(last_all * last_all, -1, keepdims=True) + EPS) * final_gain
    ).astype(jnp.bfloat16)
    logits = lax.dot_general(
        last_normed, lm_head, (((1,), (1,)), ((), ())), preferred_element_type=jnp.float32
    )
    max_logit = lax.pmax(jnp.max(logits, -1), ("grp", "tok", "mdl")).reshape(
        groups_total, req_count
    )
    return (
        final_rows.astype(jnp.bfloat16)[None],
        appended[None],
        req_norm[None],
        max_logit,
        logits,
    )


def solution(mesh):
    return jax.shard_map(
        on_device,
        mesh=mesh,
        in_specs=(
            P("grp", "tok", "mdl"),
            P(),
            P(),
            P(),
            P(("grp", "mdl"), None, "tok", None),
            P("mdl"),
            P("mdl", "tok"),
            P("mdl", "tok"),
            P("mdl", "tok"),
            P("tok", "mdl"),
            P("mdl"),
            P("mdl", "tok"),
            P("mdl", "tok"),
            P("tok", "mdl"),
            P(),
            P(("grp", "tok", "mdl"), None),
        ),
        out_specs=(
            P("grp", "tok", "mdl"),
            P("grp", "mdl", "tok", None),
            P("grp", None),
            P(),
            P(None, ("grp", "tok", "mdl")),
        ),
        check_vma=False,
    )
```

profile of v0, /device:TPU:1, one launch (start us, length us, event | category | flops | bytes accessed | tf_op | source)
XLA Modules:
  0.0 899.1 jit_solution(10230812188905599163)
XLA Ops:
  9.2 15.0 %psum.28 = f32[128]{0:T(128)S(1)} all-reduce(f32[128]{0:T(128)S(1)} %fusion.44), channel_id=1, replica_groups=mesh['grp'=4,'tok'=8,'mdl'=8] {'mdl'}, use_global_device_ids=true, to_apply=%region_1.0 | all-reduce | flops 128 | bytes 1024 | tf_op jit(solution)/shard_map/psum | solution.py:64
  24.2 1.7 fusion.46
  26.0 35.1 %all-gather.6.cloned.1.call-done = bf16[1024,640]{1,0:T(8,128)(2,1)} async-done(((bf16[128,640]{1,0:T(8,128)(2,1)}), bf16[1024,640]{1,0:T(8,128)(2,1)}) %all-gather.6.cloned.1.call-update) | async-done | bytes 1310736 | tf_op jit(solution)/shard_map/all_gather | solution.py:70
  61.1 5.1 fusion.30
  71.6 1.6 broadcast_compare_fusion
  73.3 34.7 %reduce-scatter.5.cloned.1.call-done = f32[128,896]{0,1:T(8,128)} async-done(((f32[1024,896]{0,1:T(8,128)}), f32[128,896]{0,1:T(8,128)}) %reduce-scatter.5.cloned.1.call-update) | async-done | bytes 458768 | tf_op jit(solution)/shard_map/reduce_scatter | solution.py:74
  110.8 1.8 copy.57
  114.5 16.8 %all_gather.19 = bf16[1024,1,256]{0,2,1:T(8,128)(2,1)} all-gather(bf16[128,1,256]{0,2,1:T(8,128)(2,1)S(1)} %get-tuple-element.23), channel_id=1, replica_groups=mesh['grp'=4,'tok'=8,'mdl'=8] {'mdl'}, dimensions={0}, use_global_device_ids=true | all-gather | bytes 589824 | tf_op jit(solution)/shard_map/all_gather | solution.py:99
  131.3 1.8 subtract_convert_fusion
  133.1 12.9 %fusion = (f32[128,5]{0,1:T(8,128)S(1)}, f32[128,5,8192]{2,0,1:T(8,128)}) fusion(pred[128,8192]{1,0:T(8,128)(4,1)} %broadcast_compare_fusion, bf16[8192,1,256]{2,0,1:T(8,128)(2,1)} %bitcast.150, bf16[128,5,64]{2,0,1:T(8,128)(2,1)} %get-tuple-element.17, bf16[128,5,64]{2,0,1:T(8,128)(2,1)} %get-tuple-element.16), kind=kOutput, calls=%fused_computation.2 | convolution fusion | flops 1358232960 | bytes 24447488 | tf_op jit(solution)/shard_map/rcgd,kcd->rcgk/dot_general | solution.py:131
  146.1 2.2 fusion.10
  148.3 14.2 %fusion.21 = f32[1,128,128,5]{2,1,3,0:T(8,128)} fusion(bf16[8192,1,256]{2,0,1:T(8,128)(2,1)} %bitcast.151, f32[128,5,8192]{2,0,1:T(8,128)} %get-tuple-element.33, f32[128,5]{0,1:T(8,128)S(1)} %max.19, pred[128,8192]{1,0:T(8,128)(4,1)} %broadcast_compare_fusion), kind=kOutput, calls=%fused_computation.28 | convolution fusion | flops 1368391680 | bytes 24447488 | tf_op jit(solution)/shard_map/rcgk,kcd->rcgd/dot_general | solution.py:141
  162.5 10.7 %fusion.1 = f32[128,5]{0,1:T(8,128)S(1)} fusion(f32[128,5,8192]{2,0,1:T(8,128)} %get-tuple-element.33, f32[128,5]{0,1:T(8,128)S(1)} %max.19, pred[128,8192]{1,0:T(8,128)(4,1)} %broadcast_compare_fusion), kind=kLoop, calls=%fused_computation.3 | loop fusion | flops 26213760 | bytes 22025216 | tf_op jit(solution)/shard_map/reduce_sum | solution.py:140
  174.3 1.5 fusion.39
  175.9 27.0 %all-gather.10.cloned.1.call-done = bf16[1024,640]{0,1:T(8,128)(2,1)} async-done(((bf16[128,640]{0,1:T(8,128)(2,1)}), bf16[1024,640]{0,1:T(8,128)(2,1)}) %all-gather.10.cloned.1.call-update) | async-done | bytes 1310736 | tf_op jit(solution)/shard_map/all_gather | solution.py:153
  202.9 4.0 convolution_convert_fusion.2
  206.9 36.2 %reduce-scatter.7.cloned.1.call-done = bf16[128,640]{1,0:T(8,128)(2,1)} async-done(((bf16[1024,640]{1,0:T(8,128)(2,1)}), bf16[128,640]{1,0:T(8,128)(2,1)}) %reduce-scatter.7.cloned.1.call-update) | async-done | bytes 163856 | tf_op jit(solution)/shard_map/reduce_scatter | solution.py:157
  244.2 16.7 %psum.29 = f32[128]{0:T(128)S(1)} all-reduce(f32[128]{0:T(128)S(1)} %multiply_reduce_fusion.2), channel_id=1, replica_groups=mesh['grp'=4,'tok'=8,'mdl'=8] {'mdl'}, use_global_device_ids=true, to_apply=%region_14.15 | all-reduce | flops 128 | bytes 1024 | tf_op jit(solution)/shard_map/psum | solution.py:160
  260.9 1.7 multiply_convert_fusion.1
  262.7 30.4 %all-gather.12.cloned.1.call-done = bf16[1024,640]{1,0:T(8,128)(2,1)} async-done(((bf16[128,640]{1,0:T(8,128)(2,1)}), bf16[1024,640]{1,0:T(8,128)(2,1)}) %all-gather.12.cloned.1.call-update) | async-done | bytes 1310736 | tf_op jit(solution)/shard_map/all_gather | solution.py:167
  293.1 10.5 %convolution_convert_fusion = bf16[1024,3584]{1,0:T(8,128)(2,1)} fusion(bf16[1024,640]{1,0:T(8,128)(2,1)} %all-gather.12.cloned.1.call-done, bf16[640,1792]{1,0:T(8,128)(2,1)} %param.28, bf16[640,1792]{1,0:T(8,128)(2,1)} %param.27), kind=kOutput, calls=%fused_computation.8 | convolution fusion | flops 4710465536 | bytes 13238272 | tf_op jit(solution)/shard_map/dot_general | solution.py:166
  303.6 53.3 %reduce-scatter.9.cloned.1.call-done = bf16[128,3584]{1,0:T(8,128)(2,1)} async-done(((bf16[1024,3584]{1,0:T(8,128)(2,1)}), bf16[128,3584]{1,0:T(8,128)(2,1)}) %reduce-scatter.9.cloned.1.call-update) | async-done | bytes 917520 | tf_op jit(solution)/shard_map/reduce_scatter | solution.py:171
  356.9 1.4 convert_element_type.96
  359.4 33.1 %all-gather.14.cloned.1.call-done = bf16[1024,1792]{1,0:T(8,128)(2,1)} async-done(((bf16[128,1792]{1,0:T(8,128)(2,1)}), bf16[1024,1792]{1,0:T(8,128)(2,1)}) %all-gather.14.cloned.1.call-update) | async-done | bytes 3670032 | tf_op jit(solution)/shard_map/all_gather | solution.py:176
  392.5 6.8 convolution_convert_fusion.1
  399.5 35.1 %reduce-scatter.11.cloned.1.call-done = bf16[128,640]{1,0:T(8,128)(2,1)} async-done(((bf16[1024,640]{1,0:T(8,128)(2,1)}), bf16[128,640]{1,0:T(8,128)(2,1)}) %reduce-scatter.11.cloned.1.call-update) | async-done | bytes 163856 | tf_op jit(solution)/shard_map/reduce_scatter | solution.py:180
  434.6 1.7 multiply_reduce_fusion.1
  437.2 128.3 %psum.30 = f32[4]{0:T(128)S(1)} all-reduce(f32[4]{0:T(128)S(1)} %select_reduce_fusion.2), channel_id=1, replica_groups=mesh['grp'=4,'tok'=8,'mdl'=8] {'tok','mdl'}, use_global_device_ids=true, to_apply=%region_19.20 | all-reduce | flops 4 | bytes 32 | tf_op jit(solution)/shard_map/psum | solution.py:197
  568.2 1.7 convert_bitcast_fusion
  569.9 243.1 %all-reduce.2.cloned.1.call-done = f32[16,5120]{1,0:T(8,128)} async-done(((f32[16,5120]{1,0:T(8,128)}), f32[16,5120]{1,0:T(8,128)}) %all-reduce.2.cloned.1.call-update) | async-done | bytes 327696 | tf_op jit(solution)/shard_map/psum | solution.py:198
  814.1 2.6 fusion.72
  817.4 74.3 %pmax.7 = f32[4,4]{1,0:T(4,128)} all-reduce(f32[4,4]{1,0:T(4,128)S(1)} %reshape.445), channel_id=1, replica_groups=mesh['grp'=4,'tok'=8,'mdl'=8] {'grp','tok','mdl'}, use_global_device_ids=true, to_apply=%region_24.25 | all-reduce | flops 16 | bytes 128 | tf_op jit(solution)/shard_map/pmax | solution.py:206
  (91 shorter events, 20.3 us)
Async XLA Ops:
  8.0 806.1 %copy-start = (bf16[300,5120]{1,0:T(8,128)(2,1)S(1)}, bf16[300,5120]{1,0:T(8,128)(2,1)}, u32[]{:S(2)}) copy-start(bf16[300,5120]{1,0:T(8,128)(2,1)} %param.31) | copy-start | bytes 9216004
  8.0 53.1 %all-gather.6.cloned.1.call-start = ((), (), s32[]{:S(2)}) async-start(), calls=%async_computation.4 | async-start | bytes 1474560 | tf_op jit(solution)/shard_map/all_gather | solution.py:70
  25.9 82.0 %reduce-scatter.5.cloned.1.call-start = ((), (), s32[]{:S(2)}) async-start(), calls=%async_computation.5 | async-start | bytes 4128768 | tf_op jit(solution)/shard_map/reduce_scatter | solution.py:74
  66.2 0.7 copy-start.12
  66.3 66.8 %all-gather.8.cloned.1.call-start = ((), (), s32[]{:S(2)}) async-start(), calls=%async_computation.6 | async-start | bytes 4325376 | tf_op jit(solution)/shard_map/all_gather | solution.py:125
  66.8 136.1 %all-gather.10.cloned.1.call-start = ((), (), s32[]{:S(2)}) async-start(), calls=%async_computation.7 | async-start | bytes 1474560 | tf_op jit(solution)/shard_map/all_gather | solution.py:153
  133.1 13.0 %copy-start.5 = (bf16[1024,1,256]{0,2,1:T(8,128)(2,1)S(1)}, bf16[1024,1,256]{0,2,1:T(8,128)(2,1)}, u32[]{:S(2)}) copy-start(bf16[1024,1,256]{0,2,1:T(8,128)(2,1)} %all_gather.19) | copy-start | bytes 1572868
  133.1 13.0 %copy-start.7 = (pred[128,1024]{0,1:T(8,128)(4,1)S(1)}, pred[128,1024]{0,1:T(8,128)(4,1)}, u32[]{:S(2)}) copy-start(pred[128,1024]{0,1:T(8,128)(4,1)} %fusion.43) | copy-start | bytes 393220
  133.1 13.0 %copy-start.8 = (bf16[128,5,64]{2,0,1:T(8,128)(2,1)S(1)}, bf16[128,5,64]{2,0,1:T(8,128)(2,1)}, u32[]{:S(2)}) copy-start(bf16[128,5,64]{2,0,1:T(8,128)(2,1)} %get-tuple-element.16) | copy-start | bytes 245764
  133.1 13.0 %copy-start.9 = (bf16[128,5,64]{2,0,1:T(8,128)(2,1)S(1)}, bf16[128,5,64]{2,0,1:T(8,128)(2,1)}, u32[]{:S(2)}) copy-start(bf16[128,5,64]{2,0,1:T(8,128)(2,1)} %get-tuple-element.17) | copy-start | bytes 245764
  162.5 10.7 %copy-start.1 = (f32[1024,128,5]{1,0,2:T(8,128)S(1)}, f32[1024,128,5]{1,0,2:T(8,128)}, u32[]{:S(2)}) copy-start(f32[1024,128,5]{1,0,2:T(8,128)} %get-tuple-element.31) | copy-start | bytes 7864324
  173.2 1.0 copy-start.6
  173.2 1.1 copy-start.13
  175.8 67.4 %copy-start.2 = (bf16[1,128,640]{2,1,0:T(8,128)(2,1)S(1)}, bf16[1,128,640]{2,1,0:T(8,128)(2,1)}, u32[]{:S(2)}) copy-start(bf16[1,128,640]{2,1,0:T(8,128)(2,1)} %param.16) | copy-start | bytes 491524
  175.8 85.1 %copy-start.11 = (f32[640]{0:T(1024)S(1)}, f32[640]{0:T(1024)}, u32[]{:S(2)}) copy-start(f32[640]{0:T(1024)} %param.26) | copy-start | bytes 7684
  175.8 67.4 %reduce-scatter.7.cloned.1.call-start = ((), (), s32[]{:S(2)}) async-start(), calls=%async_computation.8 | async-start | bytes 1474560 | tf_op jit(solution)/shard_map/reduce_scatter | solution.py:157
  206.9 86.2 %all-gather.12.cloned.1.call-start = ((), (), s32[]{:S(2)}) async-start(), calls=%async_computation.9 | async-start | bytes 1474560 | tf_op jit(solution)/shard_map/all_gather | solution.py:167
  262.7 94.2 %reduce-scatter.9.cloned.1.call-start = ((), (), s32[]{:S(2)}) async-start(), calls=%async_computation.10 | async-start | bytes 8257536 | tf_op jit(solution)/shard_map/reduce_scatter | solution.py:171
  303.6 88.9 %all-gather.14.cloned.1.call-start = ((), (), s32[]{:S(2)}) async-start(), calls=%async_computation.11 | async-start | bytes 4128768 | tf_op jit(solution)/shard_map/all_gather | solution.py:176
  359.3 75.3 %copy-start.3 = (bf16[128,640]{1,0:T(8,128)(2,1)S(1)}, bf16[128,640]{1,0:T(8,128)(2,1)}, u32[]{:S(2)}) copy-start(bf16[128,640]{1,0:T(8,128)(2,1)} %reduce-scatter.7.cloned.1.call-done) | copy-start | bytes 491524
  359.3 75.3 %reduce-scatter.11.cloned.1.call-start = ((), (), s32[]{:S(2)}) async-start(), calls=%async_computation.12 | async-start | bytes 1474560 | tf_op jit(solution)/shard_map/reduce_scatter | solution.py:180
  399.3 414.8 %copy-start.10 = (f32[5120]{0:T(1024)S(1)}, f32[5120]{0:T(1024)}, u32[]{:S(2)}) copy-start(f32[5120]{0:T(1024)} %param.30) | copy-start | bytes 61444
  399.4 413.6 %all-reduce.2.cloned.1.call-start = ((), (), s32[]{:S(2)}) async-start(), calls=%async_computation.13 | async-start | bytes 655360 | tf_op jit(solution)/shard_map/psum | solution.py:198
  567.5 0.7 copy-start.4
Sparse Core Ops, SparseCore 0:
  26.1 35.0 all-gather.5
  66.4 41.5 reduce-scatter.4
  175.9 26.9 all-gather.9
  207.0 36.1 reduce-scatter.6
  262.8 30.2 all-gather.11
  303.7 53.1 reduce-scatter.8
  359.4 33.0 all-gather.13
  399.5 35.0 reduce-scatter.10
Sparse Core Ops, SparseCore 1:
  69.3 56.2 all-gather.7
  568.3 244.6 all-reduce.1
where the time goes:
time: 900 us; the launch traced here: 899 us
  waiting for transfers between devices  529 us (59%)
  blocking collectives  251 us (28%)
  matrix products  59.8 us (7%)
  other arithmetic  31.8 us (4%)
  between operations  15.8 us (2%)
  local copies, waits for them, and re-layouts  11.5 us (1%)
    psum x1, waiting for transfers between devices, on_device(): last_all = lax.psum(padded, ('grp', 'tok', 'mdl'))  243 us
    psum x1, blocking collectives, on_device(): req_total = lax.psum(req_squares, ('tok', 'mdl'))  128 us
    pmax x1, blocking collectives, on_device(): lax.pmax(jnp.max(logits, -1), ('grp', 'tok', 'mdl'))  74.3 us
    reduce_scatter x1, waiting for transfers between devices, on_device(): lax.psum_scatter(partial_ffn.astype(jnp.bfloat16), 'mdl', scatter_dimensi...  53.3 us
    reduce_scatter x1, waiting for transfers between devices, on_device(): lax.psum_scatter(partial_out.astype(jnp.bfloat16), 'tok', scatter_dimensi...  36.2 us
    all_gather x1, waiting for transfers between devices, on_device(): lax.all_gather(normed, 'tok', axis=0, tiled=True)  35.1 us
    reduce_scatter x1, waiting for transfers between devices, on_device(): lax.psum_scatter(partial_down.astype(jnp.bfloat16), 'tok', scatter_dimens...  35.1 us
    reduce_scatter x1, waiting for transfers between devices, on_device(): lax.psum_scatter(partial_qkv, 'mdl', scatter_dimension=0, tiled=True)  34.7 us
  transfers between devices with their start and end apart: 10, of which 9 were waited for; matrix products, arithmetic and copies ran while one was open for 2% of the time, Pallas kernels for 0%

commit v1 on v0

--- a/solution.py
+++ b/solution.py
@@ -190,22 +190,26 @@
     ends = offsets + counts - 1
     picked = ends[:, None] == my_tok_rows[None, :]
     last_part = jnp.sum(jnp.where(picked[:, :, None], final_rows[None, :, :], 0.0), 1)
-    padded = jnp.zeros((groups_total * req_count, model_width), jnp.float32)
-    padded = lax.dynamic_update_slice(
-        padded, last_part, (group_idx * req_count, mdl_idx * feat_dev)
-    )
-    req_total = lax.psum(req_squares, ("tok", "mdl"))
-    last_all = lax.psum(padded, ("grp", "tok", "mdl"))
+    last_squares = jnp.sum(last_part * last_part, -1)
+    packed = jnp.concatenate([last_part, req_squares[:, None], last_squares[:, None]], 1)
+    packed = lax.psum(packed, "tok")
+    blocks = lax.all_gather(packed, "mdl", axis=0, tiled=False)
+    mdl_count = blocks.shape[0]
+    last_rows = jnp.transpose(blocks[:, :, :feat_dev], (1, 0, 2)).reshape(req_count, model_width)
+    req_total = jnp.sum(blocks[:, :, feat_dev], 0)
+    last_total = jnp.sum(blocks[:, :, feat_dev + 1], 0)
     req_norm = jnp.sqrt(req_total / (counts.astype(jnp.float32) * model_width) + EPS)
-    last_normed = (
-        last_all * lax.rsqrt(jnp.mean(last_all * last_all, -1, keepdims=True) + EPS) * final_gain
+    last_own = (
+        last_rows * lax.rsqrt(last_total[:, None] / model_width + EPS) * final_gain
     ).astype(jnp.bfloat16)
+    last_normed = lax.all_gather(last_own, "grp", axis=0, tiled=True)
     logits = lax.dot_general(
         last_normed, lm_head, (((1,), (1,)), ((), ())), preferred_element_type=jnp.float32
     )
-    max_logit = lax.pmax(jnp.max(logits, -1), ("grp", "tok", "mdl")).reshape(
-        groups_total, req_count
-    )
+    local_max = jnp.max(logits, -1)
+    local_max = lax.pmax(local_max, "mdl")
+    local_max = lax.pmax(local_max, "tok")
+    max_logit = lax.pmax(local_max, "grp").reshape(groups_total, req_count)
     return (
         final_rows.astype(jnp.bfloat16)[None],
         appended[None],

time: 900 us -> 543 us (0.60)
  waiting for transfers between devices: 529 us -> 285 us
  blocking collectives: 251 us -> 138 us
    psum x1 -> x0, waiting for transfers between devices: 243 us -> none  [on_device(): last_all = lax.psum(padded, ('grp', 'tok', 'mdl'))]
    psum x1, blocking collectives: 128 us -> 21.7 us  [on_device(): packed = lax.psum(packed, 'tok')]
    pmax x1 -> x3, blocking collectives: 74.3 us -> 33.9 us  [the longest x1 14.4 us: on_device(): local_max = lax.pmax(local_max, 'mdl')]
    all_gather x0 -> x2, blocking collectives: none -> 34.2 us  [the longest x1 24.3 us: on_device(): blocks = lax.all_gather(packed, 'mdl', axis=0, tiled=False)]
  transfers between devices with their start and end apart: 10 -> 9, of which waited for: 9 -> 8; matrix products, arithmetic and copies ran while one was open for 2% -> 3% of each run, Pallas kernels for 0% -> 0%
where the time goes in v1:
time: 543 us; the launch traced here: 537 us
  waiting for transfers between devices  285 us (52%)
  blocking collectives  138 us (25%)
  matrix products  58.8 us (11%)
  other arithmetic  28.5 us (5%)
  between operations  15.8 us (3%)
  local copies, waits for them, and re-layouts  10.3 us (2%)
    reduce_scatter x1, waiting for transfers between devices, on_device(): lax.psum_scatter(partial_ffn.astype(jnp.bfloat16), 'mdl', scatter_dimensi...  53.3 us
    reduce_scatter x1, waiting for transfers between devices, on_device(): lax.psum_scatter(partial_out.astype(jnp.bfloat16), 'tok', scatter_dimensi...  36.2 us
    all_gather x1, waiting for transfers between devices, on_device(): lax.all_gather(normed, 'tok', axis=0, tiled=True)  35.1 us
    reduce_scatter x1, waiting for transfers between devices, on_device(): lax.psum_scatter(partial_qkv, 'mdl', scatter_dimension=0, tiled=True)  34.7 us
    reduce_scatter x1, waiting for transfers between devices, on_device(): lax.psum_scatter(partial_down.astype(jnp.bfloat16), 'tok', scatter_dimens...  34.4 us
    all_gather x1, waiting for transfers between devices, on_device(): lax.all_gather(activated, 'mdl', axis=0, tiled=True)  33.1 us
    all_gather x1, waiting for transfers between devices, on_device(): lax.all_gather(ffn_input, 'tok', axis=0, tiled=True)  30.4 us
    all_gather x1, waiting for transfers between devices, on_device(): lax.all_gather(attended, 'mdl', axis=0, tiled=True)  27 us
  transfers between devices with their start and end apart: 9, of which 8 were waited for; matrix products, arithmetic and copies ran while one was open for 3% of the time, Pallas kernels for 0%

profile of v1, /device:TPU:1, one launch (start us, length us, event | category | flops | bytes accessed | tf_op | source)
XLA Modules:
  0.0 537.0 jit_solution(11023597313740727375)
XLA Ops:
  9.2 15.0 %psum.21 = f32[128]{0:T(128)S(1)} all-reduce(f32[128]{0:T(128)S(1)} %fusion.44), channel_id=1, replica_groups=mesh['grp'=4,'tok'=8,'mdl'=8] {'mdl'}, use_global_device_ids=true, to_apply=%region_1.0 | all-reduce | flops 128 | bytes 1024 | tf_op jit(solution)/shard_map/psum | solution.py:64
  24.2 1.7 fusion.46
  26.0 35.1 %all-gather.7.cloned.1.call-done = bf16[1024,640]{1,0:T(8,128)(2,1)} async-done(((bf16[128,640]{1,0:T(8,128)(2,1)}), bf16[1024,640]{1,0:T(8,128)(2,1)}) %all-gather.7.cloned.1.call-update) | async-done | bytes 1310736 | tf_op jit(solution)/shard_map/all_gather | solution.py:70
  61.1 5.1 fusion.30
  71.6 1.6 broadcast_compare_fusion
  73.3 34.7 %reduce-scatter.5.cloned.1.call-done = f32[128,896]{0,1:T(8,128)} async-done(((f32[1024,896]{0,1:T(8,128)}), f32[128,896]{0,1:T(8,128)}) %reduce-scatter.5.cloned.1.call-update) | async-done | bytes 458768 | tf_op jit(solution)/shard_map/reduce_scatter | solution.py:74
  110.8 1.8 copy.67
  114.5 16.7 %all_gather.28 = bf16[1024,1,256]{0,2,1:T(8,128)(2,1)} all-gather(bf16[128,1,256]{0,2,1:T(8,128)(2,1)S(1)} %get-tuple-element.25), channel_id=1, replica_groups=mesh['grp'=4,'tok'=8,'mdl'=8] {'mdl'}, dimensions={0}, use_global_device_ids=true | all-gather | bytes 589824 | tf_op jit(solution)/shard_map/all_gather | solution.py:99
  131.3 1.8 subtract_convert_fusion
  133.1 13.0 %fusion = (f32[128,5]{0,1:T(8,128)S(1)}, f32[128,5,8192]{2,0,1:T(8,128)}) fusion(pred[128,8192]{1,0:T(8,128)(4,1)} %broadcast_compare_fusion, bf16[8192,1,256]{2,0,1:T(8,128)(2,1)} %bitcast.163, bf16[128,5,64]{2,0,1:T(8,128)(2,1)} %get-tuple-element.19, bf16[128,5,64]{2,0,1:T(8,128)(2,1)} %get-tuple-element.18), kind=kOutput, calls=%fused_computation.2 | convolution fusion | flops 1358232960 | bytes 24447488 | tf_op jit(solution)/shard_map/rcgd,kcd->rcgk/dot_general | solution.py:131
  146.1 2.2 fusion.10
  148.3 14.2 %fusion.21 = f32[1,128,128,5]{2,1,3,0:T(8,128)} fusion(bf16[8192,1,256]{2,0,1:T(8,128)(2,1)} %bitcast.164, f32[128,5,8192]{2,0,1:T(8,128)} %get-tuple-element.35, f32[128,5]{0,1:T(8,128)S(1)} %max.23, pred[128,8192]{1,0:T(8,128)(4,1)} %broadcast_compare_fusion), kind=kOutput, calls=%fused_computation.28 | convolution fusion | flops 1368391680 | bytes 24447488 | tf_op jit(solution)/shard_map/rcgk,kcd->rcgd/dot_general | solution.py:141
  162.5 10.7 %fusion.1 = f32[128,5]{0,1:T(8,128)S(1)} fusion(f32[128,5,8192]{2,0,1:T(8,128)} %get-tuple-element.35, f32[128,5]{0,1:T(8,128)S(1)} %max.23, pred[128,8192]{1,0:T(8,128)(4,1)} %broadcast_compare_fusion), kind=kLoop, calls=%fused_computation.3 | loop fusion | flops 26213760 | bytes 22025216 | tf_op jit(solution)/shard_map/reduce_sum | solution.py:140
  174.3 1.5 fusion.39
  175.9 27.0 %all-gather.11.cloned.1.call-done = bf16[1024,640]{0,1:T(8,128)(2,1)} async-done(((bf16[128,640]{0,1:T(8,128)(2,1)}), bf16[1024,640]{0,1:T(8,128)(2,1)}) %all-gather.11.cloned.1.call-update) | async-done | bytes 1310736 | tf_op jit(solution)/shard_map/all_gather | solution.py:153
  202.9 4.0 convolution_convert_fusion.2
  206.9 36.2 %reduce-scatter.7.cloned.1.call-done = bf16[128,640]{1,0:T(8,128)(2,1)} async-done(((bf16[1024,640]{1,0:T(8,128)(2,1)}), bf16[128,640]{1,0:T(8,128)(2,1)}) %reduce-scatter.7.cloned.1.call-update) | async-done | bytes 163856 | tf_op jit(solution)/shard_map/reduce_scatter | solution.py:157
  244.2 16.7 %psum.22 = f32[128]{0:T(128)S(1)} all-reduce(f32[128]{0:T(128)S(1)} %multiply_reduce_fusion.1), channel_id=1, replica_groups=mesh['grp'=4,'tok'=8,'mdl'=8] {'mdl'}, use_global_device_ids=true, to_apply=%region_14.15 | all-reduce | flops 128 | bytes 1024 | tf_op jit(solution)/shard_map/psum | solution.py:160
  260.9 1.7 multiply_convert_fusion
  262.7 30.4 %all-gather.13.cloned.1.call-done = bf16[1024,640]{1,0:T(8,128)(2,1)} async-done(((bf16[128,640]{1,0:T(8,128)(2,1)}), bf16[1024,640]{1,0:T(8,128)(2,1)}) %all-gather.13.cloned.1.call-update) | async-done | bytes 1310736 | tf_op jit(solution)/shard_map/all_gather | solution.py:167
  293.1 10.5 %convolution_convert_fusion = bf16[1024,3584]{1,0:T(8,128)(2,1)} fusion(bf16[1024,640]{1,0:T(8,128)(2,1)} %all-gather.13.cloned.1.call-done, bf16[640,1792]{1,0:T(8,128)(2,1)} %param.28, bf16[640,1792]{1,0:T(8,128)(2,1)} %param.27), kind=kOutput, calls=%fused_computation.8 | convolution fusion | flops 4710465536 | bytes 13238272 | tf_op jit(solution)/shard_map/dot_general | solution.py:166
  303.6 53.3 %reduce-scatter.9.cloned.1.call-done = bf16[128,3584]{1,0:T(8,128)(2,1)} async-done(((bf16[1024,3584]{1,0:T(8,128)(2,1)}), bf16[128,3584]{1,0:T(8,128)(2,1)}) %reduce-scatter.9.cloned.1.call-update) | async-done | bytes 917520 | tf_op jit(solution)/shard_map/reduce_scatter | solution.py:171
  359.4 33.1 %all-gather.15.cloned.1.call-done = bf16[1024,1792]{1,0:T(8,128)(2,1)} async-done(((bf16[128,1792]{1,0:T(8,128)(2,1)}), bf16[1024,1792]{1,0:T(8,128)(2,1)}) %all-gather.15.cloned.1.call-update) | async-done | bytes 3670032 | tf_op jit(solution)/shard_map/all_gather | solution.py:176
  392.5 6.8 %convolution_convert_fusion.1 = bf16[1024,640]{1,0:T(8,128)(2,1)} fusion(bf16[1024,1792]{1,0:T(8,128)(2,1)} %all-gather.15.cloned.1.call-done, bf16[1792,640]{1,0:T(8,128)(2,1)} %param.29), kind=kOutput, calls=%fused_computation.21 | convolution fusion | flops 2349465600 | bytes 7274496 | tf_op jit(solution)/shard_map/dot_general | solution.py:175
  400.2 34.4 %reduce-scatter.11.cloned.1.call-done = bf16[128,640]{1,0:T(8,128)(2,1)} async-done(((bf16[1024,640]{1,0:T(8,128)(2,1)}), bf16[128,640]{1,0:T(8,128)(2,1)}) %reduce-scatter.11.cloned.1.call-update) | async-done | bytes 163856 | tf_op jit(solution)/shard_map/reduce_scatter | solution.py:180
  437.1 21.7 %psum.23 = f32[1,4,642]{2,1,0:T(4,128)S(1)} all-reduce(f32[1,4,642]{2,1,0:T(4,128)S(1)} %maximum_bitcast_fusion), channel_id=1, replica_groups=mesh['grp'=4,'tok'=8,'mdl'=8] {'tok'}, use_global_device_ids=true, to_apply=%region_21.22 | all-reduce | flops 2568 | bytes 20544 | tf_op jit(solution)/shard_map/psum | solution.py:195
  458.8 24.3 %all_gather.34 = f32[8,4,642]{2,1,0:T(4,128)S(1)} all-gather(f32[1,4,642]{2,1,0:T(4,128)S(1)} %psum.23), channel_id=1, replica_groups=mesh['grp'=4,'tok'=8,'mdl'=8] {'mdl'}, dimensions={0}, use_global_device_ids=true | all-gather | bytes 92448 | tf_op jit(solution)/shard_map/all_gather | solution.py:196
  484.0 9.9 %all-gather = bf16[4,4,5120]{2,1,0:T(4,128)(2,1)S(1)} all-gather(bf16[1,4,5120]{2,1,0:T(4,128)(2,1)S(1)} %fusion.52), channel_id=1, replica_groups=mesh['grp'=4,'tok'=8,'mdl'=8] {'grp'}, dimensions={0}, use_global_device_ids=true | all-gather | bytes 204800 | tf_op jit(solution)/shard_map/all_gather | solution.py:205
  493.9 1.6 fusion.70
  495.6 14.4 %pmax.21 = f32[16]{0:T(128)S(1)} all-reduce(f32[16]{0:T(128)S(1)} %get-tuple-element.36), channel_id=1, replica_groups=mesh['grp'=4,'tok'=8,'mdl'=8] {'mdl'}, use_global_device_ids=true, to_apply=%region_25.26 | all-reduce | flops 16 | bytes 128 | tf_op jit(solution)/shard_map/pmax | solution.py:210
  510.0 10.7 %pmax.22 = f32[16]{0:T(128)S(1)} all-reduce(f32[16]{0:T(128)S(1)} %pmax.21), channel_id=1, replica_groups=mesh['grp'=4,'tok'=8,'mdl'=8] {'tok'}, use_global_device_ids=true, to_apply=%region_26.27 | all-reduce | flops 16 | bytes 128 | tf_op jit(solution)/shard_map/pmax | solution.py:211
  520.8 8.8 %pmax.23 = f32[4,4]{1,0:T(4,128)} all-reduce(f32[4,4]{1,0:T(4,128)S(1)} %reshape.478), channel_id=1, replica_groups=mesh['grp'=4,'tok'=8,'mdl'=8] {'grp'}, use_global_device_ids=true, to_apply=%region_27.28 | all-reduce | flops 16 | bytes 128 | tf_op jit(solution)/shard_map/pmax | solution.py:212
  (95 shorter events, 20.4 us)
Async XLA Ops:
  8.0 485.9 %copy-start = (bf16[300,5120]{1,0:T(8,128)(2,1)S(1)}, bf16[300,5120]{1,0:T(8,128)(2,1)}, u32[]{:S(2)}) copy-start(bf16[300,5120]{1,0:T(8,128)(2,1)} %param.31) | copy-start | bytes 9216004
  8.0 53.1 %all-gather.7.cloned.1.call-start = ((), (), s32[]{:S(2)}) async-start(), calls=%async_computation.4 | async-start | bytes 1474560 | tf_op jit(solution)/shard_map/all_gather | solution.py:70
  25.9 82.0 %reduce-scatter.5.cloned.1.call-start = ((), (), s32[]{:S(2)}) async-start(), calls=%async_computation.5 | async-start | bytes 4128768 | tf_op jit(solution)/shard_map/reduce_scatter | solution.py:74
  66.2 0.7 copy-start.11
  66.3 66.8 %all-gather.9.cloned.1.call-start = ((), (), s32[]{:S(2)}) async-start(), calls=%async_computation.6 | async-start | bytes 4325376 | tf_op jit(solution)/shard_map/all_gather | solution.py:125
  66.8 136.1 %all-gather.11.cloned.1.call-start = ((), (), s32[]{:S(2)}) async-start(), calls=%async_computation.7 | async-start | bytes 1474560 | tf_op jit(solution)/shard_map/all_gather | solution.py:153
  133.1 13.0 %copy-start.4 = (bf16[1024,1,256]{0,2,1:T(8,128)(2,1)S(1)}, bf16[1024,1,256]{0,2,1:T(8,128)(2,1)}, u32[]{:S(2)}) copy-start(bf16[1024,1,256]{0,2,1:T(8,128)(2,1)} %all_gather.28) | copy-start | bytes 1572868
  133.1 13.0 %copy-start.6 = (pred[128,1024]{0,1:T(8,128)(4,1)S(1)}, pred[128,1024]{0,1:T(8,128)(4,1)}, u32[]{:S(2)}) copy-start(pred[128,1024]{0,1:T(8,128)(4,1)} %fusion.43) | copy-start | bytes 393220
  133.1 13.0 %copy-start.7 = (bf16[128,5,64]{2,0,1:T(8,128)(2,1)S(1)}, bf16[128,5,64]{2,0,1:T(8,128)(2,1)}, u32[]{:S(2)}) copy-start(bf16[128,5,64]{2,0,1:T(8,128)(2,1)} %get-tuple-element.18) | copy-start | bytes 245764
  133.1 13.0 %copy-start.8 = (bf16[128,5,64]{2,0,1:T(8,128)(2,1)S(1)}, bf16[128,5,64]{2,0,1:T(8,128)(2,1)}, u32[]{:S(2)}) copy-start(bf16[128,5,64]{2,0,1:T(8,128)(2,1)} %get-tuple-element.19) | copy-start | bytes 245764
  162.5 10.7 %copy-start.1 = (f32[1024,128,5]{1,0,2:T(8,128)S(1)}, f32[1024,128,5]{1,0,2:T(8,128)}, u32[]{:S(2)}) copy-start(f32[1024,128,5]{1,0,2:T(8,128)} %get-tuple-element.33) | copy-start | bytes 7864324
  173.2 1.0 copy-start.5
  173.2 1.1 copy-start.12
  175.8 67.4 %copy-start.2 = (bf16[1,128,640]{2,1,0:T(8,128)(2,1)S(1)}, bf16[1,128,640]{2,1,0:T(8,128)(2,1)}, u32[]{:S(2)}) copy-start(bf16[1,128,640]{2,1,0:T(8,128)(2,1)} %param.16) | copy-start | bytes 491524
  175.8 85.1 %copy-start.10 = (f32[640]{0:T(1024)S(1)}, f32[640]{0:T(1024)}, u32[]{:S(2)}) copy-start(f32[640]{0:T(1024)} %param.26) | copy-start | bytes 7684
  175.8 67.4 %reduce-scatter.7.cloned.1.call-start = ((), (), s32[]{:S(2)}) async-start(), calls=%async_computation.8 | async-start | bytes 1474560 | tf_op jit(solution)/shard_map/reduce_scatter | solution.py:157
  206.9 86.2 %all-gather.13.cloned.1.call-start = ((), (), s32[]{:S(2)}) async-start(), calls=%async_computation.9 | async-start | bytes 1474560 | tf_op jit(solution)/shard_map/all_gather | solution.py:167
  262.7 94.2 %reduce-scatter.9.cloned.1.call-start = ((), (), s32[]{:S(2)}) async-start(), calls=%async_computation.10 | async-start | bytes 8257536 | tf_op jit(solution)/shard_map/reduce_scatter | solution.py:171
  303.6 88.9 %all-gather.15.cloned.1.call-start = ((), (), s32[]{:S(2)}) async-start(), calls=%async_computation.11 | async-start | bytes 4128768 | tf_op jit(solution)/shard_map/all_gather | solution.py:176
  359.3 75.3 %copy-start.3 = (bf16[128,640]{1,0:T(8,128)(2,1)S(1)}, bf16[128,640]{1,0:T(8,128)(2,1)}, u32[]{:S(2)}) copy-start(bf16[128,640]{1,0:T(8,128)(2,1)} %reduce-scatter.7.cloned.1.call-done) | copy-start | bytes 491524
  359.3 75.3 %reduce-scatter.11.cloned.1.call-start = ((), (), s32[]{:S(2)}) async-start(), calls=%async_computation.12 | async-start | bytes 1474560 | tf_op jit(solution)/shard_map/reduce_scatter | solution.py:180
  399.3 84.6 %copy-start.9 = (f32[5120]{0:T(1024)S(1)}, f32[5120]{0:T(1024)}, u32[]{:S(2)}) copy-start(f32[5120]{0:T(1024)} %param.30) | copy-start | bytes 61444
Sparse Core Ops, SparseCore 0:
  26.1 35.0 all-gather.6
  66.4 41.5 reduce-scatter.4
  175.9 26.9 all-gather.10
  207.0 36.1 reduce-scatter.6
  262.8 30.2 all-gather.12
  303.7 53.1 reduce-scatter.8
  359.4 33.0 all-gather.14
  399.5 35.0 reduce-scatter.10
Sparse Core Ops, SparseCore 1:
  69.3 56.2 all-gather.8

commit v2 on v1

--- a/solution.py
+++ b/solution.py
@@ -23,6 +23,13 @@
     return jnp.concatenate(
         [first_part * cosine - second * sine_part, second * cosine + first_part * sine_part], -1
     )
+
+
+def scatter_sum(partial, axis):
+    count = lax.axis_size(axis)
+    pieces = partial.reshape((count, partial.shape[0] // count) + partial.shape[1:])
+    pieces = lax.all_to_all(pieces, axis, 0, 0, tiled=False)
+    return jnp.sum(pieces.astype(jnp.float32), 0)
 
 
 def on_device(
@@ -61,16 +68,15 @@
     mdl_idx = lax.axis_index("mdl")
     score_scale = head_dim ** (-0.5)
     tokens = hidden_in[0].astype(jnp.float32)
+    hidden_all = lax.all_gather(hidden_in[0], "tok", axis=0, tiled=True)
     squares = lax.psum(jnp.sum(tokens * tokens, -1), "mdl")
-    normed = (tokens * lax.rsqrt(squares[:, None] / model_width + EPS) * attn_gain).astype(
-        jnp.bfloat16
-    )
+    squares_all = lax.all_gather(squares, "tok", axis=0, tiled=True)
+    hidden_all_f = hidden_all.astype(jnp.float32)
+    normed_all = (
+        hidden_all_f * lax.rsqrt(squares_all[:, None] / model_width + EPS) * attn_gain
+    ).astype(jnp.bfloat16)
     w_joined = jnp.concatenate([w_query, w_key, w_value], 1)
-    partial_qkv = jnp.dot(
-        lax.all_gather(normed, "tok", axis=0, tiled=True),
-        w_joined,
-        preferred_element_type=jnp.float32,
-    )
+    partial_qkv = jnp.dot(normed_all, w_joined, preferred_element_type=jnp.float32)
     qkv_rows = lax.psum_scatter(partial_qkv, "mdl", scatter_dimension=0, tiled=True)
     q_cols = heads_dev * head_dim
     kv_cols = kv_dev * head_dim
@@ -154,20 +160,18 @@
         w_out,
         preferred_element_type=jnp.float32,
     )
-    residual = tokens + lax.psum_scatter(
-        partial_out.astype(jnp.bfloat16), "tok", scatter_dimension=0, tiled=True
-    ).astype(jnp.float32)
+    out_sum = scatter_sum(partial_out.astype(jnp.bfloat16), "tok").astype(jnp.bfloat16)
+    residual = tokens + out_sum.astype(jnp.float32)
+    out_all = lax.all_gather(out_sum, "tok", axis=0, tiled=True)
     squares_ffn = lax.psum(jnp.sum(residual * residual, -1), "mdl")
-    ffn_input = (residual * lax.rsqrt(squares_ffn[:, None] / model_width + EPS) * ffn_gain).astype(
-        jnp.bfloat16
-    )
+    squares_ffn_all = lax.all_gather(squares_ffn, "tok", axis=0, tiled=True)
+    residual_all = hidden_all_f + out_all.astype(jnp.float32)
+    ffn_all = (
+        residual_all * lax.rsqrt(squares_ffn_all[:, None] / model_width + EPS) * ffn_gain
+    ).astype(jnp.bfloat16)
     w_pair = jnp.concatenate([w_gate, w_up], 1)
     ff_dev = w_gate.shape[1]
-    partial_ffn = jnp.dot(
-        lax.all_gather(ffn_input, "tok", axis=0, tiled=True),
-        w_pair,
-        preferred_element_type=jnp.float32,
-    )
+    partial_ffn = jnp.dot(ffn_all, w_pair, preferred_element_type=jnp.float32)
     summed = lax.psum_scatter(
         partial_ffn.astype(jnp.bfloat16), "mdl", scatter_dimension=0, tiled=True
     ).astype(jnp.float32)
@@ -177,9 +181,7 @@
         w_down,
         preferred_element_type=jnp.float32,
     )
-    final_rows = residual + lax.psum_scatter(
-        partial_down.astype(jnp.bfloat16), "tok", scatter_dimension=0, tiled=True
-    ).astype(jnp.float32)
+    final_rows = residual + scatter_sum(partial_down.astype(jnp.bfloat16), "tok")
     tok_start = tok_idx * tok_rows
     my_tok_rows = tok_start + jnp.arange(tok_rows, dtype=jnp.int32)
     tok_seg = lax.dynamic_slice_in_dim(seg_row, tok_start, tok_rows)

time: 543 us -> 518 us (0.954)
  waiting for transfers between devices: 285 us -> 199 us
  blocking collectives: 138 us -> 195 us
  starting transfers between devices: 0.37 us -> 7.15 us
    reduce_scatter x2 -> x0, waiting for transfers between devices: 70.7 us -> none  [the longest x1 36.2 us: on_device(): lax.psum_scatter(partial_out.astype(jnp.bfloat16), 'tok', scatter_dimensi...]
    all_gather x2, waiting for transfers between devices: 65.5 us -> 14.9 us  [the longest x1 9.13 us: on_device(): hidden_all = lax.all_gather(hidden_in[0], 'tok', axis=0, tiled=True)]
    all_to_all x0 -> x1, blocking collectives: none -> 41 us  [scatter_sum(): pieces = lax.all_to_all(pieces, axis, 0, 0, tiled=False)]
    all_to_all x0 -> x1, waiting for transfers between devices: none -> 34.1 us  [scatter_sum(): pieces = lax.all_to_all(pieces, axis, 0, 0, tiled=False)]
    all_gather x0 -> x2, blocking collectives: none -> 24.9 us  [the longest x1 14.3 us: on_device(): squares_all = lax.all_gather(squares, 'tok', axis=0, tiled=True)]
    all_to_all x0 -> x1, starting transfers between devices: none -> 6.87 us  [scatter_sum(): pieces = lax.all_to_all(pieces, axis, 0, 0, tiled=False)]
  transfers between devices with their start and end apart: 9 -> 8, of which waited for: 8 -> 7; matrix products, arithmetic and copies ran while one was open for 3% -> 3% of each run, Pallas kernels for 0% -> 0%
where the time goes in v2:
time: 518 us; the launch traced here: 513 us
  waiting for transfers between devices  199 us (38%)
  blocking collectives  195 us (38%)
  matrix products  58.3 us (11%)
  other arithmetic  28 us (5%)
  between operations  15.8 us (3%)
  local copies, waits for them, and re-layouts  10.3 us (2%)
  starting transfers between devices  7.15 us (1%)
    reduce_scatter x1, waiting for transfers between devices, on_device(): lax.psum_scatter(partial_ffn.astype(jnp.bfloat16), 'mdl', scatter_dimensi...  53.3 us
    all_to_all x1, blocking collectives, scatter_sum(): pieces = lax.all_to_all(pieces, axis, 0, 0, tiled=False)  41 us
    reduce_scatter x1, waiting for transfers between devices, on_device(): lax.psum_scatter(partial_qkv, 'mdl', scatter_dimension=0, tiled=True)  34.8 us
    all_to_all x1, waiting for transfers between devices, scatter_sum(): pieces = lax.all_to_all(pieces, axis, 0, 0, tiled=False)  34.1 us
    all_gather x1, waiting for transfers between devices, on_device(): lax.all_gather(activated, 'mdl', axis=0, tiled=True)  33.2 us
    all_gather x1, waiting for transfers between devices, on_device(): lax.all_gather(attended, 'mdl', axis=0, tiled=True)  27 us
    psum x1, blocking collectives, on_device(): packed = lax.psum(packed, 'tok')  20.3 us
    all_gather x1, blocking collectives, on_device(): blocks = lax.all_gather(packed, 'mdl', axis=0, tiled=False)  20.2 us
  transfers between devices with their start and end apart: 8, of which 7 were waited for; matrix products, arithmetic and copies ran while one was open for 3% of the time, Pallas kernels for 0%

profile of v2, /device:TPU:1, one launch (start us, length us, event | category | flops | bytes accessed | tf_op | source)
XLA Modules:
  0.0 512.6 jit_solution(6090198081249575781)
XLA Ops:
  10.0 15.0 %psum.21 = f32[128]{0:T(128)S(1)} all-reduce(f32[128]{0:T(128)S(1)} %fusion.58), channel_id=1, replica_groups=mesh['grp'=4,'tok'=8,'mdl'=8] {'mdl'}, use_global_device_ids=true, to_apply=%region_1.0 | all-reduce | flops 128 | bytes 1024 | tf_op jit(solution)/shard_map/psum | solution.py:72
  24.9 14.3 %all-gather.1 = f32[8,1,128]{2,1,0:T(1,128)S(1)} all-gather(f32[1,1,128]{2,1,0:T(1,128)S(1)} %bitcast.199), channel_id=1, replica_groups=mesh['grp'=4,'tok'=8,'mdl'=8] {'tok'}, dimensions={0}, use_global_device_ids=true | all-gather | bytes 4608 | tf_op jit(solution)/shard_map/all_gather | solution.py:73
  39.3 9.1 %all-gather.18.cloned.1.call-done = bf16[1,1024,640]{2,1,0:T(8,128)(2,1)} async-done(((bf16[1,128,640]{2,1,0:T(8,128)(2,1)}), bf16[1,1024,640]{2,1,0:T(8,128)(2,1)}) %all-gather.18.cloned.1.call-update) | async-done | bytes 1310736 | tf_op jit(solution)/shard_map/all_gather | solution.py:71
  48.4 5.2 %fusion.21 = f32[1024,896]{0,1:T(8,128)} fusion(bf16[1,1024,640]{2,1,0:T(8,128)(2,1)} %all-gather.18.cloned.1.call-done, f32[640]{0:T(1024)} %param.21, f32[1024]{0:T(1024)S(1)} %bitcast.195, bf16[640,128]{1,0:T(8,128)(2,1)} %param.24, bf16[640,128]{1,0:T(8,128)(2,1)} %param.23, bf16[640,640]{1,0:T(8,128)(2,1)} %param.22), kind=kOutput, calls=%fused_computation.32 | convolution fusion | flops 1180467200 | bytes 6134272 | tf_op jit(solution)/shard_map/dot_general | solution.py:79
  59.0 1.7 broadcast_compare_fusion
  60.7 34.8 %reduce-scatter.3.cloned.1.call-done = f32[128,896]{0,1:T(8,128)} async-done(((f32[1024,896]{0,1:T(8,128)}), f32[128,896]{0,1:T(8,128)}) %reduce-scatter.3.cloned.1.call-update) | async-done | bytes 458768 | tf_op jit(solution)/shard_map/reduce_scatter | solution.py:80
  98.3 1.8 copy.67
  102.1 16.6 %all_gather.35 = bf16[1024,1,256]{0,2,1:T(8,128)(2,1)} all-gather(bf16[128,1,256]{0,2,1:T(8,128)(2,1)S(1)} %get-tuple-element.25), channel_id=1, replica_groups=mesh['grp'=4,'tok'=8,'mdl'=8] {'mdl'}, dimensions={0}, use_global_device_ids=true | all-gather | bytes 589824 | tf_op jit(solution)/shard_map/all_gather | solution.py:105
  118.7 1.8 subtract_convert_fusion
  120.5 12.9 %fusion = (f32[128,5]{0,1:T(8,128)S(1)}, f32[128,5,8192]{2,0,1:T(8,128)}) fusion(pred[128,8192]{1,0:T(8,128)(4,1)} %broadcast_compare_fusion, bf16[8192,1,256]{2,0,1:T(8,128)(2,1)} %bitcast.201, bf16[128,5,64]{2,0,1:T(8,128)(2,1)} %get-tuple-element.17, bf16[128,5,64]{2,0,1:T(8,128)(2,1)} %get-tuple-element.16), kind=kOutput, calls=%fused_computation.2 | convolution fusion | flops 1358232960 | bytes 24447488 | tf_op jit(solution)/shard_map/rcgd,kcd->rcgk/dot_general | solution.py:137
  133.5 2.2 fusion.15
  135.7 14.1 %fusion.35 = f32[1,128,128,5]{2,1,3,0:T(8,128)} fusion(bf16[8192,1,256]{2,0,1:T(8,128)(2,1)} %bitcast.202, f32[128,5,8192]{2,0,1:T(8,128)} %get-tuple-element.35, f32[128,5]{0,1:T(8,128)S(1)} %max.23, pred[128,8192]{1,0:T(8,128)(4,1)} %broadcast_compare_fusion), kind=kOutput, calls=%fused_computation.43 | convolution fusion | flops 1368391680 | bytes 24447488 | tf_op jit(solution)/shard_map/rcgk,kcd->rcgd/dot_general | solution.py:147
  149.9 10.7 %fusion.1 = f32[128,5]{0,1:T(8,128)S(1)} fusion(f32[128,5,8192]{2,0,1:T(8,128)} %get-tuple-element.35, f32[128,5]{0,1:T(8,128)S(1)} %max.23, pred[128,8192]{1,0:T(8,128)(4,1)} %broadcast_compare_fusion), kind=kLoop, calls=%fused_computation.3 | loop fusion | flops 26213760 | bytes 22025216 | tf_op jit(solution)/shard_map/reduce_sum | solution.py:146
  163.2 27.0 %all-gather.12.cloned.1.call-done = bf16[1024,640]{0,1:T(8,128)(2,1)} async-done(((bf16[128,640]{0,1:T(8,128)(2,1)}), bf16[1024,640]{0,1:T(8,128)(2,1)}) %all-gather.12.cloned.1.call-update) | async-done | bytes 1310736 | tf_op jit(solution)/shard_map/all_gather | solution.py:159
  190.3 2.9 convolution_convert_fusion.2
  193.2 41.0 %all_to_all.10 = bf16[8,128,640]{2,1,0:T(8,128)(2,1)} all-to-all(bf16[8,128,640]{2,1,0:T(8,128)(2,1)S(1)} %bitcast.187), channel_id=1, replica_groups=mesh['grp'=4,'tok'=8,'mdl'=8] {'tok'}, dimensions={0} | all-to-all | bytes 2621440 | tf_op jit(solution)/shard_map/all_to_all | solution.py:31
  234.2 2.2 reduce_sum.156
  237.5 12.9 %psum.22 = f32[128]{0:T(128)S(1)} all-reduce(f32[128]{0:T(128)S(1)} %multiply_reduce_fusion.1), channel_id=1, replica_groups=mesh['grp'=4,'tok'=8,'mdl'=8] {'mdl'}, use_global_device_ids=true, to_apply=%region_14.15 | all-reduce | flops 128 | bytes 1024 | tf_op jit(solution)/shard_map/psum | solution.py:166
  250.4 10.6 %all-gather.2 = f32[8,1,128]{2,1,0:T(1,128)S(1)} all-gather(f32[1,1,128]{2,1,0:T(1,128)S(1)} %bitcast.200), channel_id=1, replica_groups=mesh['grp'=4,'tok'=8,'mdl'=8] {'tok'}, dimensions={0}, use_global_device_ids=true | all-gather | bytes 4608 | tf_op jit(solution)/shard_map/all_gather | solution.py:167
  260.9 5.8 %all-gather.14.cloned.1.call-done = bf16[1024,640]{1,0:T(8,128)(2,1)} async-done(((bf16[128,640]{1,0:T(8,128)(2,1)}), bf16[1024,640]{1,0:T(8,128)(2,1)}) %all-gather.14.cloned.1.call-update) | async-done | bytes 1310736 | tf_op jit(solution)/shard_map/all_gather | solution.py:165
  266.7 10.9 %convolution_convert_fusion = bf16[1024,3584]{1,0:T(8,128)(2,1)} fusion(bf16[640,1792]{1,0:T(8,128)(2,1)} %param.28, bf16[640,1792]{1,0:T(8,128)(2,1)} %param.27, bf16[1024,640]{1,0:T(8,128)(2,1)} %all-gather.14.cloned.1.call-done, bf16[1,1024,640]{2,1,0:T(8,128)(2,1)} %all-gather.18.cloned.1.call-done, f32[640]{0:T(1024)S(1)} %copy-done.10, ...), kind=kOutput, calls=%fused_computation.8 | convolution fusion | flops 4714397696 | bytes 14555648 | tf_op jit(solution)/shard_map/dot_general | solution.py:174
  277.7 53.3 %reduce-scatter.5.cloned.1.call-done = bf16[128,3584]{1,0:T(8,128)(2,1)} async-done(((bf16[1024,3584]{1,0:T(8,128)(2,1)}), bf16[128,3584]{1,0:T(8,128)(2,1)}) %reduce-scatter.5.cloned.1.call-update) | async-done | bytes 917520 | tf_op jit(solution)/shard_map/reduce_scatter | solution.py:175
  333.4 33.2 %all-gather.16.cloned.1.call-done = bf16[1024,1792]{1,0:T(8,128)(2,1)} async-done(((bf16[128,1792]{1,0:T(8,128)(2,1)}), bf16[1024,1792]{1,0:T(8,128)(2,1)}) %all-gather.16.cloned.1.call-update) | async-done | bytes 3670032 | tf_op jit(solution)/shard_map/all_gather | solution.py:180
  366.6 6.8 %convolution_convert_fusion.1 = bf16[1024,640]{1,0:T(8,128)(2,1)} fusion(bf16[1024,1792]{1,0:T(8,128)(2,1)} %all-gather.16.cloned.1.call-done, bf16[1792,640]{1,0:T(8,128)(2,1)} %param.29), kind=kOutput, calls=%fused_computation.29 | convolution fusion | flops 2349465600 | bytes 7274496 | tf_op jit(solution)/shard_map/dot_general | solution.py:179
  373.4 6.9 %all-to-all-start.1 = ((bf16[8,128,640]{2,1,0:T(8,128)(2,1)}), bf16[8,128,640]{2,1,0:T(8,128)(2,1)}, u32[]{:S(2)}, u32[]{:S(2)}) async-start(bf16[8,128,640]{2,1,0:T(8,128)(2,1)} %bitcast.186), calls=%async_computation.3 | async-start | bytes 2621440 | tf_op jit(solution)/shard_map/all_to_all | solution.py:31
  381.1 34.1 %all-to-all-done.1 = bf16[8,128,640]{2,1,0:T(8,128)(2,1)} async-done(((bf16[8,128,640]{2,1,0:T(8,128)(2,1)}), bf16[8,128,640]{2,1,0:T(8,128)(2,1)}, u32[]{:S(2)}, u32[]{:S(2)}) %all-to-all-start.1) | async-done | bytes 1310752 | tf_op jit(solution)/shard_map/all_to_all | solution.py:31
  418.3 20.3 %psum.23 = f32[1,4,642]{2,1,0:T(4,128)S(1)} all-reduce(f32[1,4,642]{2,1,0:T(4,128)S(1)} %maximum_bitcast_fusion), channel_id=1, replica_groups=mesh['grp'=4,'tok'=8,'mdl'=8] {'tok'}, use_global_device_ids=true, to_apply=%region_21.22 | all-reduce | flops 2568 | bytes 20544 | tf_op jit(solution)/shard_map/psum | solution.py:197
  438.6 20.2 %all_gather.42 = f32[8,4,642]{2,1,0:T(4,128)S(1)} all-gather(f32[1,4,642]{2,1,0:T(4,128)S(1)} %psum.23), channel_id=1, replica_groups=mesh['grp'=4,'tok'=8,'mdl'=8] {'mdl'}, dimensions={0}, use_global_device_ids=true | all-gather | bytes 92448 | tf_op jit(solution)/shard_map/all_gather | solution.py:198
  459.6 9.8 %all-gather.3 = bf16[4,4,5120]{2,1,0:T(4,128)(2,1)S(1)} all-gather(bf16[1,4,5120]{2,1,0:T(4,128)(2,1)S(1)} %fusion.67), channel_id=1, replica_groups=mesh['grp'=4,'tok'=8,'mdl'=8] {'grp'}, dimensions={0}, use_global_device_ids=true | all-gather | bytes 204800 | tf_op jit(solution)/shard_map/all_gather | solution.py:207
  471.2 14.5 %pmax.21 = f32[16]{0:T(128)S(1)} all-reduce(f32[16]{0:T(128)S(1)} %get-tuple-element.36), channel_id=1, replica_groups=mesh['grp'=4,'tok'=8,'mdl'=8] {'mdl'}, use_global_device_ids=true, to_apply=%region_25.26 | all-reduce | flops 16 | bytes 128 | tf_op jit(solution)/shard_map/pmax | solution.py:212
  485.7 10.7 %pmax.22 = f32[16]{0:T(128)S(1)} all-reduce(f32[16]{0:T(128)S(1)} %pmax.21), channel_id=1, replica_groups=mesh['grp'=4,'tok'=8,'mdl'=8] {'tok'}, use_global_device_ids=true, to_apply=%region_26.27 | all-reduce | flops 16 | bytes 128 | tf_op jit(solution)/shard_map/pmax | solution.py:213
  496.4 8.8 %pmax.23 = f32[4,4]{1,0:T(4,128)} all-reduce(f32[4,4]{1,0:T(4,128)S(1)} %reshape.495), channel_id=1, replica_groups=mesh['grp'=4,'tok'=8,'mdl'=8] {'grp'}, use_global_device_ids=true, to_apply=%region_27.28 | all-reduce | flops 16 | bytes 128 | tf_op jit(solution)/shard_map/pmax | solution.py:214
  (94 shorter events, 24.7 us)
Async XLA Ops:
  8.0 461.5 %copy-start = (bf16[300,5120]{1,0:T(8,128)(2,1)S(1)}, bf16[300,5120]{1,0:T(8,128)(2,1)}, u32[]{:S(2)}) copy-start(bf16[300,5120]{1,0:T(8,128)(2,1)} %param.31) | copy-start | bytes 9216004
  8.0 40.4 %all-gather.18.cloned.1.call-start = ((), (), s32[]{:S(2)}) async-start(), calls=%async_computation.10 | async-start | bytes 1474560 | tf_op jit(solution)/shard_map/all_gather | solution.py:71
  8.7 86.7 %reduce-scatter.3.cloned.1.call-start = ((), (), s32[]{:S(2)}) async-start(), calls=%async_computation.4 | async-start | bytes 4128768 | tf_op jit(solution)/shard_map/reduce_scatter | solution.py:80
  53.6 0.7 copy-start.11
  53.7 66.9 %all-gather.10.cloned.1.call-start = ((), (), s32[]{:S(2)}) async-start(), calls=%async_computation.5 | async-start | bytes 4325376 | tf_op jit(solution)/shard_map/all_gather | solution.py:131
  54.2 136.0 %all-gather.12.cloned.1.call-start = ((), (), s32[]{:S(2)}) async-start(), calls=%async_computation.6 | async-start | bytes 1474560 | tf_op jit(solution)/shard_map/all_gather | solution.py:159
  120.5 13.0 %copy-start.4 = (bf16[1024,1,256]{0,2,1:T(8,128)(2,1)S(1)}, bf16[1024,1,256]{0,2,1:T(8,128)(2,1)}, u32[]{:S(2)}) copy-start(bf16[1024,1,256]{0,2,1:T(8,128)(2,1)} %all_gather.35) | copy-start | bytes 1572868
  120.5 13.0 %copy-start.6 = (pred[128,1024]{0,1:T(8,128)(4,1)S(1)}, pred[128,1024]{0,1:T(8,128)(4,1)}, u32[]{:S(2)}) copy-start(pred[128,1024]{0,1:T(8,128)(4,1)} %fusion.56) | copy-start | bytes 393220
  120.5 13.0 %copy-start.7 = (bf16[128,5,64]{2,0,1:T(8,128)(2,1)S(1)}, bf16[128,5,64]{2,0,1:T(8,128)(2,1)}, u32[]{:S(2)}) copy-start(bf16[128,5,64]{2,0,1:T(8,128)(2,1)} %get-tuple-element.16) | copy-start | bytes 245764
  120.5 13.0 %copy-start.8 = (bf16[128,5,64]{2,0,1:T(8,128)(2,1)S(1)}, bf16[128,5,64]{2,0,1:T(8,128)(2,1)}, u32[]{:S(2)}) copy-start(bf16[128,5,64]{2,0,1:T(8,128)(2,1)} %get-tuple-element.17) | copy-start | bytes 245764
  149.9 10.7 %copy-start.1 = (f32[1024,128,5]{1,0,2:T(8,128)S(1)}, f32[1024,128,5]{1,0,2:T(8,128)}, u32[]{:S(2)}) copy-start(f32[1024,128,5]{1,0,2:T(8,128)} %get-tuple-element.33) | copy-start | bytes 7864324
  160.6 1.0 copy-start.5
  160.6 1.1 copy-start.12
  163.2 103.5 %all-gather.14.cloned.1.call-start = ((), (), s32[]{:S(2)}) async-start(), calls=%async_computation.7 | async-start | bytes 1474560 | tf_op jit(solution)/shard_map/all_gather | solution.py:165
  193.2 43.3 %copy-start.2 = (bf16[1,128,640]{2,1,0:T(8,128)(2,1)S(1)}, bf16[1,128,640]{2,1,0:T(8,128)(2,1)}, u32[]{:S(2)}) copy-start(bf16[1,128,640]{2,1,0:T(8,128)(2,1)} %param.16) | copy-start | bytes 491524
  193.2 73.5 %copy-start.10 = (f32[640]{0:T(1024)S(1)}, f32[640]{0:T(1024)}, u32[]{:S(2)}) copy-start(f32[640]{0:T(1024)} %param.26) | copy-start | bytes 7684
  236.4 94.6 %reduce-scatter.5.cloned.1.call-start = ((), (), s32[]{:S(2)}) async-start(), calls=%async_computation.8 | async-start | bytes 8257536 | tf_op jit(solution)/shard_map/reduce_scatter | solution.py:175
  277.7 88.9 %all-gather.16.cloned.1.call-start = ((), (), s32[]{:S(2)}) async-start(), calls=%async_computation.9 | async-start | bytes 4128768 | tf_op jit(solution)/shard_map/all_gather | solution.py:180
  373.4 43.3 %copy-start.3 = (bf16[128,640]{1,0:T(8,128)(2,1)S(1)}, bf16[128,640]{1,0:T(8,128)(2,1)}, u32[]{:S(2)}) copy-start(bf16[128,640]{1,0:T(8,128)(2,1)} %reduce_sum.156) | copy-start | bytes 491524
  373.4 41.8 %all-to-all-start.1 = ((bf16[8,128,640]{2,1,0:T(8,128)(2,1)}), bf16[8,128,640]{2,1,0:T(8,128)(2,1)}, u32[]{:S(2)}, u32[]{:S(2)}) async-start(bf16[8,128,640]{2,1,0:T(8,128)(2,1)} %bitcast.186), calls=%async_computation.3 | async-start | bytes 2621440 | tf_op jit(solution)/shard_map/all_to_all | solution.py:31
  380.3 79.3 %copy-start.9 = (f32[5120]{0:T(1024)S(1)}, f32[5120]{0:T(1024)}, u32[]{:S(2)}) copy-start(f32[5120]{0:T(1024)} %param.30) | copy-start | bytes 61444
Sparse Core Ops, SparseCore 0:
  10.6 37.7 all-gather.17
  53.8 41.6 reduce-scatter.2
  163.3 26.8 all-gather.11
  236.5 30.1 all-gather.13
  277.8 53.1 reduce-scatter.4
  333.5 33.0 all-gather.15
Sparse Core Ops, SparseCore 1:
  56.7 56.3 all-gather.9

commit v3 on v2

--- a/solution.py
+++ b/solution.py
@@ -1,7 +1,10 @@
+import functools
+
 import jax
 import jax.numpy as jnp
 from jax import lax
 from jax.sharding import PartitionSpec as P
+from jax.experimental import pallas as pl
 
 PREFIX = 4096
 PAGE = 256
@@ -10,6 +13,71 @@
 EPS = 1e-06
 THETA = 1000000.0
 NEG = -1e30
+BK = 512
+
+
+def attn_kernel(q_ref, pkv_ref, skv_ref, rp_ref, rs_ref, ri_ref, kp_ref, ks_ref, o_ref, *, scale, head_dim):
+    q = q_ref[...]
+    rows = q.shape[0]
+    row_prefix = rp_ref[...]
+    row_seg = rs_ref[...]
+    row_idx = ri_ref[...]
+    n_pre = pkv_ref.shape[0] // BK
+    n_suf = skv_ref.shape[0] // BK
+
+    def pre_block(b):
+        start = pl.multiple_of(b * BK, BK)
+        kv = pkv_ref[pl.ds(start, BK), :]
+        s = lax.dot_general(q, kv[:, :head_dim], (((1,), (1,)), ((), ())), preferred_element_type=jnp.float32) * scale
+        ok = row_prefix == kp_ref[:, pl.ds(start, BK)]
+        return s, ok, kv[:, head_dim:]
+
+    def suf_block(b):
+        start = pl.multiple_of(b * BK, BK)
+        kv = skv_ref[pl.ds(start, BK), :]
+        s = lax.dot_general(q, kv[:, :head_dim], (((1,), (1,)), ((), ())), preferred_element_type=jnp.float32) * scale
+        key_idx = start + lax.broadcasted_iota(jnp.int32, (1, BK), 1)
+        ok = (row_seg == ks_ref[:, pl.ds(start, BK)]) & (key_idx <= row_idx)
+        return s, ok, kv[:, head_dim:]
+
+    def max_step(block):
+        def step(b, m):
+            s, ok, _ = block(b)
+            return jnp.maximum(m, jnp.max(jnp.where(ok, s, NEG), -1, keepdims=True))
+        return step
+
+    m = jnp.full((rows, 1), NEG, jnp.float32)
+    m = lax.fori_loop(0, n_pre, max_step(pre_block), m)
+    m = lax.fori_loop(0, n_suf, max_step(suf_block), m)
+
+    def sum_step(block):
+        def step(b, carry):
+            total, acc = carry
+            s, ok, v = block(b)
+            p = jnp.where(ok, jnp.exp(s - m), 0.0)
+            total = total + jnp.sum(p, -1, keepdims=True)
+            acc = acc + jnp.dot(p.astype(jnp.bfloat16), v, preferred_element_type=jnp.float32)
+            return total, acc
+        return step
+
+    carry = (jnp.zeros((rows, 1), jnp.float32), jnp.zeros((rows, head_dim), jnp.float32))
+    carry = lax.fori_loop(0, n_pre, sum_step(pre_block), carry)
+    total, acc = lax.fori_loop(0, n_suf, sum_step(suf_block), carry)
+    o_ref[...] = (acc / total).astype(o_ref.dtype)
+
+
+def attention(q, pkv, skv, row_prefix, row_seg, row_idx, key_prefix, key_seg, *, scale, block_rows=128):
+    n_rows, head_dim = q.shape
+    kern = functools.partial(attn_kernel, scale=scale, head_dim=head_dim)
+    full = lambda shape: pl.BlockSpec(shape, lambda i: (0, 0))
+    rowb = lambda w: pl.BlockSpec((block_rows, w), lambda i: (i, 0))
+    return pl.pallas_call(
+        kern,
+        grid=(n_rows // block_rows,),
+        in_specs=[rowb(head_dim), full(pkv.shape), full(skv.shape), rowb(1), rowb(1), rowb(1), full(key_prefix.shape), full(key_seg.shape)],
+        out_specs=rowb(head_dim),
+        out_shape=jax.ShapeDtypeStruct((n_rows, head_dim), jnp.bfloat16),
+    )(q, pkv, skv, row_prefix, row_seg, row_idx, key_prefix, key_seg)
 
 
 def rotate(tensor, positions):
@@ -103,26 +171,6 @@
     k_rot = rotate(key_rows, positions).astype(jnp.bfloat16)
     appended = jnp.concatenate([k_rot, value_rows.astype(jnp.bfloat16)], -1)
     suffix = lax.all_gather(appended, "mdl", axis=0, tiled=True)
-    every_row = jnp.arange(seq_len, dtype=jnp.int32)
-    suffix_ok = ((seg_row[None, :] == my_seg[:, None]) & (every_row[None, :] <= my_rows[:, None]))[
-        :, None, None, :
-    ]
-    suffix_scores = (
-        jnp.einsum(
-            "rcgd,tcd->rcgt", q_rot, suffix[..., :head_dim], preferred_element_type=jnp.float32
-        )
-        * score_scale
-    )
-    suffix_scores = jnp.where(suffix_ok, suffix_scores, NEG)
-    row_max = jnp.max(suffix_scores, -1)
-    suffix_weights = jnp.where(suffix_ok, jnp.exp(suffix_scores - row_max[..., None]), 0.0)
-    row_total = jnp.sum(suffix_weights, -1)
-    mixed = jnp.einsum(
-        "rcgt,tcd->rcgd",
-        suffix_weights.astype(jnp.bfloat16),
-        suffix[..., head_dim:],
-        preferred_element_type=jnp.float32,
-    )
     slot_ids = jnp.arange(slot_total, dtype=jnp.int32)
     pages_each = PREFIX // PAGE
     slot_prefix = jnp.sum(
@@ -130,31 +178,23 @@
     )
     piece = lax.all_gather(prefix_cache, ("grp", "mdl"), axis=0, tiled=True)
     page_count = piece.shape[0]
-    key_prefix = jnp.repeat(slot_prefix, page_len)
-    allowed = (my_prefix[:, None] == key_prefix[None, :])[:, None, None, :]
-    flat_pages = piece.reshape(page_count * page_len, kv_dev, 2 * head_dim)
-    scores = (
-        jnp.einsum(
-            "rcgd,kcd->rcgk", q_rot, flat_pages[..., :head_dim], preferred_element_type=jnp.float32
-        )
-        * score_scale
-    )
-    scores = jnp.where(allowed, scores, NEG)
-    new_max = jnp.maximum(row_max, jnp.max(scores, -1))
-    factor = jnp.exp(row_max - new_max)
-    page_weights = jnp.where(allowed, jnp.exp(scores - new_max[..., None]), 0.0)
-    new_total = row_total * factor + jnp.sum(page_weights, -1)
-    new_mixed = mixed * factor[..., None] + jnp.einsum(
-        "rcgk,kcd->rcgd",
-        page_weights.astype(jnp.bfloat16),
-        flat_pages[..., head_dim:],
-        preferred_element_type=jnp.float32,
-    )
-    attended = (
-        (new_mixed / new_total[..., None])
-        .astype(jnp.bfloat16)
-        .reshape(rows_mdl, heads_dev * head_dim)
-    )
+    key_prefix = jnp.repeat(slot_prefix, page_len)[None, :]
+    flat_pages = piece.reshape(page_count * page_len, 2 * head_dim)
+    flat_suffix = suffix.reshape(seq_len, 2 * head_dim)
+    row_prefix = jnp.repeat(my_prefix, group_size)[:, None]
+    row_seg = jnp.repeat(my_seg, group_size)[:, None]
+    row_idx = jnp.repeat(my_rows, group_size)[:, None]
+    attended = attention(
+        q_rot.reshape(rows_mdl * heads_dev, head_dim),
+        flat_pages,
+        flat_suffix,
+        row_prefix,
+        row_seg,
+        row_idx,
+        key_prefix,
+        seg_row[None, :],
+        scale=score_scale,
+    ).reshape(rows_mdl, heads_dev * head_dim)
     partial_out = jnp.dot(
         lax.all_gather(attended, "mdl", axis=0, tiled=True),
         w_out,

time: 518 us -> 540 us (1.042)
  Pallas kernels: 0 us -> 59.9 us
  matrix products: 58.3 us -> 27.6 us
  other arithmetic: 28 us -> 18.5 us
  local copies, waits for them, and re-layouts: 10.3 us -> 16.9 us
  waiting for transfers between devices: 199 us -> 193 us
    pallas_call x0 -> x1, Pallas kernels: none -> 59.9 us  [attention(): pl.pallas_call(kern, grid=(n_rows // block_rows,), in_specs=[rowb(head_di...]
    dot_general x4 -> x0, matrix products: 30.8 us -> none  [the longest x1 14.1 us: on_device(): jnp.einsum('rcgk,kcd->rcgd', page_weights.astype(jnp.bfloat16), flat_page...]
    reduce_sum x2 -> x0, other arithmetic: 11.3 us -> none  [the longest x1 10.7 us: on_device(): new_total = row_total * factor + jnp.sum(page_weights, -1)]
  transfers between devices with their start and end apart: 8 -> 8, of which waited for: 7 -> 7; matrix products, arithmetic and copies ran while one was open for 3% -> 4% of each run, Pallas kernels for 0% -> 0%
where the time goes in v3:
time: 540 us; the launch traced here: 534 us
  blocking collectives  196 us (36%)
  waiting for transfers between devices  193 us (36%)
  Pallas kernels  59.9 us (11%)
  matrix products  27.6 us (5%)
  other arithmetic  18.5 us (3%)
  local copies, waits for them, and re-layouts  16.9 us (3%)
  between operations  15.8 us (3%)
  starting transfers between devices  7.34 us (1%)
    pallas_call x1, Pallas kernels, attention(): pl.pallas_call(kern, grid=(n_rows // block_rows,), in_specs=[rowb(head_di...  59.9 us
    reduce_scatter x1, waiting for transfers between devices, on_device(): lax.psum_scatter(partial_ffn.astype(jnp.bfloat16), 'mdl', scatter_dimensi...  53.1 us
    all_to_all x1, blocking collectives, scatter_sum(): pieces = lax.all_to_all(pieces, axis, 0, 0, tiled=False)  41 us
    all_to_all x1, waiting for transfers between devices, scatter_sum(): pieces = lax.all_to_all(pieces, axis, 0, 0, tiled=False)  34.1 us
    all_gather x1, waiting for transfers between devices, on_device(): lax.all_gather(activated, 'mdl', axis=0, tiled=True)  33.2 us
    reduce_scatter x1, waiting for transfers between devices, on_device(): lax.psum_scatter(partial_qkv, 'mdl', scatter_dimension=0, tiled=True)  31.2 us
    all_gather x1, waiting for transfers between devices, on_device(): lax.all_gather(attended, 'mdl', axis=0, tiled=True)  25.9 us
    psum x1, blocking collectives, on_device(): packed = lax.psum(packed, 'tok')  20.3 us
  transfers between devices with their start and end apart: 8, of which 7 were waited for; matrix products, arithmetic and copies ran while one was open for 4% of the time, Pallas kernels for 0%

profile of v3, /device:TPU:1, one launch (start us, length us, event | category | flops | bytes accessed | tf_op | source)
XLA Modules:
  0.0 534.2 jit_solution(2753886322939917879)
XLA Ops:
  10.0 15.0 %psum.21 = f32[128]{0:T(128)S(1)} all-reduce(f32[128]{0:T(128)S(1)} %fusion.24), channel_id=1, replica_groups=mesh['grp'=4,'tok'=8,'mdl'=8] {'mdl'}, use_global_device_ids=true, to_apply=%region_1.0 | all-reduce | flops 128 | bytes 1024 | tf_op jit(solution)/shard_map/psum | solution.py:140
  24.9 14.3 %all-gather.1 = f32[8,1,128]{2,1,0:T(1,128)S(1)} all-gather(f32[1,1,128]{2,1,0:T(1,128)S(1)} %bitcast.98), channel_id=1, replica_groups=mesh['grp'=4,'tok'=8,'mdl'=8] {'tok'}, dimensions={0}, use_global_device_ids=true | all-gather | bytes 4608 | tf_op jit(solution)/shard_map/all_gather | solution.py:141
  39.3 9.1 %all-gather.18.cloned.1.call-done = bf16[1,1024,640]{2,1,0:T(8,128)(2,1)} async-done(((bf16[1,128,640]{2,1,0:T(8,128)(2,1)}), bf16[1,1024,640]{2,1,0:T(8,128)(2,1)}) %all-gather.18.cloned.1.call-update) | async-done | bytes 1310736 | tf_op jit(solution)/shard_map/all_gather | solution.py:139
  48.4 5.3 fusion.9
  64.3 31.2 %reduce-scatter.3.cloned.1.call-done = f32[128,896]{1,0:T(8,128)} async-done(((f32[1024,896]{1,0:T(8,128)}), f32[128,896]{1,0:T(8,128)}) %reduce-scatter.3.cloned.1.call-update) | async-done | bytes 458768 | tf_op jit(solution)/shard_map/reduce_scatter | solution.py:148
  95.6 1.7 slice.49
  98.4 1.4 subtract_convert_fusion
  104.9 1.7 pad_maximum_fusion.q_ref
  106.6 17.6 %all_gather.36 = bf16[1024,1,256]{2,0,1:T(8,128)(2,1)} all-gather(bf16[128,1,256]{2,0,1:T(8,128)(2,1)S(1)} %pad_maximum_fusion.1), channel_id=1, replica_groups=mesh['grp'=4,'tok'=8,'mdl'=8] {'mdl'}, dimensions={0}, use_global_device_ids=true | all-gather | bytes 589824 | tf_op jit(solution)/shard_map/all_gather | solution.py:173
  124.1 59.9 %shard_map.191 = bf16[640,128]{1,0:T(8,128)(2,1)} custom-call(bf16[640,128]{1,0:T(8,128)(2,1)} %pad_maximum_fusion.q_ref, bf16[8192,256]{1,0:T(8,128)(2,1)} %bitcast.85, bf16[1024,256]{1,0:T(8,128)(2,1)} %bitcast.86, s32[640,1]{1,0:T(8,128)} %broadcast_in_dim_reshape.16.rp_ref, s32[640,1]{1,0:T(8,128)} %broadcast_in_dim_reshape.17.rs_ref, ...), custom_call_target="tpu_custom_call" | custom-call | tf_op jit(solution)/shard_map/pallas_call | solution.py:74
  184.0 1.7 reshape.325
  185.8 25.9 %all-gather.12.cloned.1.call-done = bf16[1024,640]{1,0:T(8,128)(2,1)} async-done(((bf16[128,640]{1,0:T(8,128)(2,1)}), bf16[1024,640]{1,0:T(8,128)(2,1)}) %all-gather.12.cloned.1.call-update) | async-done | bytes 1310736 | tf_op jit(solution)/shard_map/all_gather | solution.py:199
  211.6 2.8 convolution_convert_fusion.2
  214.5 41.0 %all_to_all.10 = bf16[8,128,640]{2,1,0:T(8,128)(2,1)} all-to-all(bf16[8,128,640]{2,1,0:T(8,128)(2,1)S(1)} %bitcast.88), channel_id=1, replica_groups=mesh['grp'=4,'tok'=8,'mdl'=8] {'tok'}, dimensions={0} | all-to-all | bytes 2621440 | tf_op jit(solution)/shard_map/all_to_all | solution.py:99
  255.5 2.2 reduce_sum.136
  258.8 12.9 %psum.22 = f32[128]{0:T(128)S(1)} all-reduce(f32[128]{0:T(128)S(1)} %multiply_reduce_fusion.1), channel_id=1, replica_groups=mesh['grp'=4,'tok'=8,'mdl'=8] {'mdl'}, use_global_device_ids=true, to_apply=%region_10.11 | all-reduce | flops 128 | bytes 1024 | tf_op jit(solution)/shard_map/psum | solution.py:206
  271.7 10.8 %all-gather.2 = f32[8,1,128]{2,1,0:T(1,128)S(1)} all-gather(f32[1,1,128]{2,1,0:T(1,128)S(1)} %bitcast.99), channel_id=1, replica_groups=mesh['grp'=4,'tok'=8,'mdl'=8] {'tok'}, dimensions={0}, use_global_device_ids=true | all-gather | bytes 4608 | tf_op jit(solution)/shard_map/all_gather | solution.py:207
  282.5 4.8 all-gather.14.cloned.1.call-done
  287.2 10.9 %convolution_convert_fusion = bf16[1024,3584]{1,0:T(8,128)(2,1)} fusion(bf16[640,1792]{1,0:T(8,128)(2,1)} %param.28, bf16[640,1792]{1,0:T(8,128)(2,1)} %param.27, bf16[1024,640]{1,0:T(8,128)(2,1)} %all-gather.14.cloned.1.call-done, bf16[1,1024,640]{2,1,0:T(8,128)(2,1)} %all-gather.18.cloned.1.call-done, f32[640]{0:T(1024)S(1)} %copy-done.17, f32[1024]{0:T(1024)S(1)} %bitcast.93), kind=kOutput, calls=%fused_computation | convolution fusion | flops 4714397696 | bytes 14555648 | tf_op jit(solution)/shard_map/dot_general | solution.py:214
  298.4 53.1 %reduce-scatter.5.cloned.1.call-done = bf16[128,3584]{1,0:T(8,128)(2,1)} async-done(((bf16[1024,3584]{1,0:T(8,128)(2,1)}), bf16[128,3584]{1,0:T(8,128)(2,1)}) %reduce-scatter.5.cloned.1.call-update) | async-done | bytes 917520 | tf_op jit(solution)/shard_map/reduce_scatter | solution.py:215
  353.9 33.2 %all-gather.16.cloned.1.call-done = bf16[1024,1792]{1,0:T(8,128)(2,1)} async-done(((bf16[128,1792]{1,0:T(8,128)(2,1)}), bf16[1024,1792]{1,0:T(8,128)(2,1)}) %all-gather.16.cloned.1.call-update) | async-done | bytes 3670032 | tf_op jit(solution)/shard_map/all_gather | solution.py:220
  387.1 6.8 %convolution_convert_fusion.1 = bf16[1024,640]{1,0:T(8,128)(2,1)} fusion(bf16[1024,1792]{1,0:T(8,128)(2,1)} %all-gather.16.cloned.1.call-done, bf16[1792,640]{1,0:T(8,128)(2,1)} %param.29), kind=kOutput, calls=%fused_computation.12 | convolution fusion | flops 2349465600 | bytes 7274496 | tf_op jit(solution)/shard_map/dot_general | solution.py:219
  394.0 6.9 %all-to-all-start.1 = ((bf16[8,128,640]{2,1,0:T(8,128)(2,1)}), bf16[8,128,640]{2,1,0:T(8,128)(2,1)}, u32[]{:S(2)}, u32[]{:S(2)}) async-start(bf16[8,128,640]{2,1,0:T(8,128)(2,1)} %bitcast.87), calls=%async_computation.3 | async-start | bytes 2621440 | tf_op jit(solution)/shard_map/all_to_all | solution.py:99
  401.7 34.1 %all-to-all-done.1 = bf16[8,128,640]{2,1,0:T(8,128)(2,1)} async-done(((bf16[8,128,640]{2,1,0:T(8,128)(2,1)}), bf16[8,128,640]{2,1,0:T(8,128)(2,1)}, u32[]{:S(2)}, u32[]{:S(2)}) %all-to-all-start.1) | async-done | bytes 1310752 | tf_op jit(solution)/shard_map/all_to_all | solution.py:99
  435.7 1.5 convert_reduce_fusion
  439.9 20.3 %psum.23 = f32[1,4,642]{2,1,0:T(4,128)S(1)} all-reduce(f32[1,4,642]{2,1,0:T(4,128)S(1)} %maximum_bitcast_fusion), channel_id=1, replica_groups=mesh['grp'=4,'tok'=8,'mdl'=8] {'tok'}, use_global_device_ids=true, to_apply=%region_17.18 | all-reduce | flops 2568 | bytes 20544 | tf_op jit(solution)/shard_map/psum | solution.py:237
  460.2 20.2 %all_gather.42 = f32[8,4,642]{2,1,0:T(4,128)S(1)} all-gather(f32[1,4,642]{2,1,0:T(4,128)S(1)} %psum.23), channel_id=1, replica_groups=mesh['grp'=4,'tok'=8,'mdl'=8] {'mdl'}, dimensions={0}, use_global_device_ids=true | all-gather | bytes 92448 | tf_op jit(solution)/shard_map/all_gather | solution.py:238
  480.7 9.8 %all-gather.3 = bf16[4,4,5120]{2,1,0:T(4,128)(2,1)S(1)} all-gather(bf16[1,4,5120]{2,1,0:T(4,128)(2,1)S(1)} %fusion.36), channel_id=1, replica_groups=mesh['grp'=4,'tok'=8,'mdl'=8] {'grp'}, dimensions={0}, use_global_device_ids=true | all-gather | bytes 204800 | tf_op jit(solution)/shard_map/all_gather | solution.py:247
  490.6 1.6 fusion.40
  492.3 14.5 %pmax.21 = f32[16]{0:T(128)S(1)} all-reduce(f32[16]{0:T(128)S(1)} %get-tuple-element.21), channel_id=1, replica_groups=mesh['grp'=4,'tok'=8,'mdl'=8] {'mdl'}, use_global_device_ids=true, to_apply=%region_21.22 | all-reduce | flops 16 | bytes 128 | tf_op jit(solution)/shard_map/pmax | solution.py:252
  506.7 10.7 %pmax.22 = f32[16]{0:T(128)S(1)} all-reduce(f32[16]{0:T(128)S(1)} %pmax.21), channel_id=1, replica_groups=mesh['grp'=4,'tok'=8,'mdl'=8] {'tok'}, use_global_device_ids=true, to_apply=%region_22.23 | all-reduce | flops 16 | bytes 128 | tf_op jit(solution)/shard_map/pmax | solution.py:253
  517.5 8.8 %pmax.23 = f32[4,4]{1,0:T(4,128)} all-reduce(f32[4,4]{1,0:T(4,128)S(1)} %reshape.329), channel_id=1, replica_groups=mesh['grp'=4,'tok'=8,'mdl'=8] {'grp'}, use_global_device_ids=true, to_apply=%region_23.24 | all-reduce | flops 16 | bytes 128 | tf_op jit(solution)/shard_map/pmax | solution.py:254
  (107 shorter events, 26.8 us)
Async XLA Ops:
  8.0 482.6 %copy-start = (bf16[300,5120]{1,0:T(8,128)(2,1)S(1)}, bf16[300,5120]{1,0:T(8,128)(2,1)}, u32[]{:S(2)}) copy-start(bf16[300,5120]{1,0:T(8,128)(2,1)} %param.31) | copy-start | bytes 9216004
  8.0 40.4 %all-gather.18.cloned.1.call-start = ((), (), s32[]{:S(2)}) async-start(), calls=%async_computation.10 | async-start | bytes 1474560 | tf_op jit(solution)/shard_map/all_gather | solution.py:139
  8.7 86.8 %reduce-scatter.3.cloned.1.call-start = ((), (), s32[]{:S(2)}) async-start(), calls=%async_computation.4 | async-start | bytes 4128768 | tf_op jit(solution)/shard_map/reduce_scatter | solution.py:148
  53.7 7.8 %copy-start.18 = (s32[32]{0:T(128)S(1)}, s32[32]{0:T(128)}, u32[]{:S(2)}) copy-start(s32[32]{0:T(128)} %param.19) | copy-start | bytes 388
  53.8 70.4 %all-gather.10.cloned.1.call-start = ((), (), s32[]{:S(2)}) async-start(), calls=%async_computation.5 | async-start | bytes 4325376 | tf_op jit(solution)/shard_map/all_gather | solution.py:179
  54.3 157.3 %all-gather.12.cloned.1.call-start = ((), (), s32[]{:S(2)}) async-start(), calls=%async_computation.6 | async-start | bytes 1474560 | tf_op jit(solution)/shard_map/all_gather | solution.py:199
  55.1 0.6 copy-start.9
  55.9 2.8 copy-start.13
  62.4 0.5 copy-start.11
  62.9 0.6 copy-start.12
  102.9 3.7 copy-start.3
  104.7 1.8 copy-start.5
  104.8 1.8 copy-start.7
  185.7 101.5 %all-gather.14.cloned.1.call-start = ((), (), s32[]{:S(2)}) async-start(), calls=%async_computation.7 | async-start | bytes 1474560 | tf_op jit(solution)/shard_map/all_gather | solution.py:205
  214.5 43.3 %copy-start.1 = (bf16[1,128,640]{2,1,0:T(8,128)(2,1)S(1)}, bf16[1,128,640]{2,1,0:T(8,128)(2,1)}, u32[]{:S(2)}) copy-start(bf16[1,128,640]{2,1,0:T(8,128)(2,1)} %param.16) | copy-start | bytes 491524
  214.5 72.7 %copy-start.17 = (f32[640]{0:T(1024)S(1)}, f32[640]{0:T(1024)}, u32[]{:S(2)}) copy-start(f32[640]{0:T(1024)} %param.26) | copy-start | bytes 7684
  257.7 93.8 %reduce-scatter.5.cloned.1.call-start = ((), (), s32[]{:S(2)}) async-start(), calls=%async_computation.8 | async-start | bytes 8257536 | tf_op jit(solution)/shard_map/reduce_scatter | solution.py:215
  298.2 88.9 %all-gather.16.cloned.1.call-start = ((), (), s32[]{:S(2)}) async-start(), calls=%async_computation.9 | async-start | bytes 4128768 | tf_op jit(solution)/shard_map/all_gather | solution.py:220
  393.9 6.9 %copy-start.16 = (s32[4]{0:T(128)S(1)}, s32[4]{0:T(128)}, u32[]{:S(2)}) copy-start(s32[4]{0:T(128)} %get-tuple-element.19) | copy-start | bytes 52
  393.9 7.0 %copy-start.4 = (bf16[128,1,128]{2,0,1:T(8,128)(2,1)S(1)}, bf16[128,1,128]{2,0,1:T(8,128)(2,1)}, u32[]{:S(2)}) copy-start(bf16[128,1,128]{2,0,1:T(8,128)(2,1)} %copy-done.3) | copy-start | bytes 98308
  393.9 7.0 %copy-start.6 = (bf16[128,1,64]{2,0,1:T(8,128)(2,1)S(1)}, bf16[128,1,64]{2,0,1:T(8,128)(2,1)}, u32[]{:S(2)}) copy-start(bf16[128,1,64]{2,0,1:T(8,128)(2,1)} %copy-done.5) | copy-start | bytes 49156
  393.9 7.0 %copy-start.8 = (bf16[128,1,64]{2,0,1:T(8,128)(2,1)S(1)}, bf16[128,1,64]{2,0,1:T(8,128)(2,1)}, u32[]{:S(2)}) copy-start(bf16[128,1,64]{2,0,1:T(8,128)(2,1)} %copy-done.7) | copy-start | bytes 49156
  393.9 43.3 %copy-start.2 = (bf16[128,640]{1,0:T(8,128)(2,1)S(1)}, bf16[128,640]{1,0:T(8,128)(2,1)}, u32[]{:S(2)}) copy-start(bf16[128,640]{1,0:T(8,128)(2,1)} %reduce_sum.136) | copy-start | bytes 491524
  394.0 41.8 %all-to-all-start.1 = ((bf16[8,128,640]{2,1,0:T(8,128)(2,1)}), bf16[8,128,640]{2,1,0:T(8,128)(2,1)}, u32[]{:S(2)}, u32[]{:S(2)}) async-start(bf16[8,128,640]{2,1,0:T(8,128)(2,1)} %bitcast.87), calls=%async_computation.3 | async-start | bytes 2621440 | tf_op jit(solution)/shard_map/all_to_all | solution.py:99
  400.8 37.4 %copy-start.15 = (s32[128]{0:T(128)S(1)}, s32[128]{0:T(128)}, u32[]{:S(2)}) copy-start(s32[128]{0:T(128)} %get-tuple-element.15) | copy-start | bytes 1540
  401.7 79.0 %copy-start.10 = (f32[5120]{0:T(1024)S(1)}, f32[5120]{0:T(1024)}, u32[]{:S(2)}) copy-start(f32[5120]{0:T(1024)} %param.30) | copy-start | bytes 61444
  438.5 87.8 %copy-start.14 = (s32[4]{0:T(128)S(1)}, s32[4]{0:T(128)}, u32[]{:S(2)}) copy-start(s32[4]{0:T(128)} %copy-done.13) | copy-start | bytes 52
Sparse Core Ops, SparseCore 0:
  10.6 37.7 all-gather.17
  53.9 41.6 reduce-scatter.2
  185.9 25.7 all-gather.11
  257.8 29.3 all-gather.13
  298.3 53.1 reduce-scatter.4
  354.0 33.0 all-gather.15
Sparse Core Ops, SparseCore 1:
  56.8 56.2 all-gather.9

commit v4 on v3

--- a/solution.py
+++ b/solution.py
@@ -5,6 +5,7 @@
 from jax import lax
 from jax.sharding import PartitionSpec as P
 from jax.experimental import pallas as pl
+from jax.experimental.pallas import tpu as pltpu
 
 PREFIX = 4096
 PAGE = 256
@@ -13,71 +14,75 @@
 EPS = 1e-06
 THETA = 1000000.0
 NEG = -1e30
-BK = 512
-
-
-def attn_kernel(q_ref, pkv_ref, skv_ref, rp_ref, rs_ref, ri_ref, kp_ref, ks_ref, o_ref, *, scale, head_dim):
-    q = q_ref[...]
-    rows = q.shape[0]
-    row_prefix = rp_ref[...]
-    row_seg = rs_ref[...]
-    row_idx = ri_ref[...]
-    n_pre = pkv_ref.shape[0] // BK
-    n_suf = skv_ref.shape[0] // BK
-
-    def pre_block(b):
-        start = pl.multiple_of(b * BK, BK)
-        kv = pkv_ref[pl.ds(start, BK), :]
-        s = lax.dot_general(q, kv[:, :head_dim], (((1,), (1,)), ((), ())), preferred_element_type=jnp.float32) * scale
-        ok = row_prefix == kp_ref[:, pl.ds(start, BK)]
-        return s, ok, kv[:, head_dim:]
-
-    def suf_block(b):
-        start = pl.multiple_of(b * BK, BK)
-        kv = skv_ref[pl.ds(start, BK), :]
-        s = lax.dot_general(q, kv[:, :head_dim], (((1,), (1,)), ((), ())), preferred_element_type=jnp.float32) * scale
-        key_idx = start + lax.broadcasted_iota(jnp.int32, (1, BK), 1)
-        ok = (row_seg == ks_ref[:, pl.ds(start, BK)]) & (key_idx <= row_idx)
-        return s, ok, kv[:, head_dim:]
-
-    def max_step(block):
-        def step(b, m):
-            s, ok, _ = block(b)
-            return jnp.maximum(m, jnp.max(jnp.where(ok, s, NEG), -1, keepdims=True))
-        return step
-
-    m = jnp.full((rows, 1), NEG, jnp.float32)
-    m = lax.fori_loop(0, n_pre, max_step(pre_block), m)
-    m = lax.fori_loop(0, n_suf, max_step(suf_block), m)
-
-    def sum_step(block):
-        def step(b, carry):
-            total, acc = carry
-            s, ok, v = block(b)
-            p = jnp.where(ok, jnp.exp(s - m), 0.0)
-            total = total + jnp.sum(p, -1, keepdims=True)
-            acc = acc + jnp.dot(p.astype(jnp.bfloat16), v, preferred_element_type=jnp.float32)
-            return total, acc
-        return step
-
-    carry = (jnp.zeros((rows, 1), jnp.float32), jnp.zeros((rows, head_dim), jnp.float32))
-    carry = lax.fori_loop(0, n_pre, sum_step(pre_block), carry)
-    total, acc = lax.fori_loop(0, n_suf, sum_step(suf_block), carry)
-    o_ref[...] = (acc / total).astype(o_ref.dtype)
-
-
-def attention(q, pkv, skv, row_prefix, row_seg, row_idx, key_prefix, key_seg, *, scale, block_rows=128):
+
+
+def attn_kernel(flags_ref, q_ref, pkv_ref, skv_ref, rp_ref, rs_ref, ri_ref, kp_ref, ks_ref, o_ref, m_ref, t_ref, a_ref, *, scale, head_dim, block_keys):
+    i = pl.program_id(0)
+    n_pre = pkv_ref.shape[0] // block_keys
+    n_suf = skv_ref.shape[0] // block_keys
+    m_ref[...] = jnp.full(m_ref.shape, NEG, jnp.float32)
+    t_ref[...] = jnp.zeros(t_ref.shape, jnp.float32)
+    a_ref[...] = jnp.zeros(a_ref.shape, jnp.float32)
+
+    def update(s, ok, v):
+        m_old = m_ref[...]
+        m_new = jnp.maximum(m_old, jnp.max(jnp.where(ok, s, NEG), -1, keepdims=True))
+        alpha = jnp.exp(m_old - m_new)
+        p = jnp.where(ok, jnp.exp(s - m_new), 0.0)
+        t_ref[...] = t_ref[...] * alpha + jnp.sum(p, -1, keepdims=True)
+        a_ref[...] = a_ref[...] * alpha + jnp.dot(p.astype(jnp.bfloat16), v, preferred_element_type=jnp.float32)
+        m_ref[...] = m_new
+
+    def pre_step(b, carry):
+        @pl.when(flags_ref[i, b] > 0)
+        def _():
+            start = pl.multiple_of(b * block_keys, block_keys)
+            kv = pkv_ref[pl.ds(start, block_keys), :]
+            s = lax.dot_general(q_ref[...], kv[:, :head_dim], (((1,), (1,)), ((), ())), preferred_element_type=jnp.float32) * scale
+            ok = rp_ref[...] == kp_ref[:, pl.ds(start, block_keys)]
+            update(s, ok, kv[:, head_dim:])
+        return carry
+
+    def suf_step(b, carry):
+        @pl.when(flags_ref[i, n_pre + b] > 0)
+        def _():
+            start = pl.multiple_of(b * block_keys, block_keys)
+            kv = skv_ref[pl.ds(start, block_keys), :]
+            s = lax.dot_general(q_ref[...], kv[:, :head_dim], (((1,), (1,)), ((), ())), preferred_element_type=jnp.float32) * scale
+            key_idx = start + lax.broadcasted_iota(jnp.int32, (1, block_keys), 1)
+            ok = (rs_ref[...] == ks_ref[:, pl.ds(start, block_keys)]) & (key_idx <= ri_ref[...])
+            update(s, ok, kv[:, head_dim:])
+        return carry
+
+    lax.fori_loop(0, n_pre, pre_step, 0)
+    lax.fori_loop(0, n_suf, suf_step, 0)
+    o_ref[...] = (a_ref[...] / t_ref[...]).astype(o_ref.dtype)
+
+
+def attention(q, pkv, skv, row_prefix, row_seg, row_idx, key_prefix, key_seg, *, scale, block_rows=128, block_keys=256):
     n_rows, head_dim = q.shape
-    kern = functools.partial(attn_kernel, scale=scale, head_dim=head_dim)
-    full = lambda shape: pl.BlockSpec(shape, lambda i: (0, 0))
-    rowb = lambda w: pl.BlockSpec((block_rows, w), lambda i: (i, 0))
+    n_blocks = n_rows // block_rows
+    pre_blocks = key_prefix.reshape(-1, block_keys)[:, 0]
+    rows_prefix = row_prefix.reshape(n_blocks, block_rows)
+    need_pre = jnp.any(rows_prefix[:, :, None] == pre_blocks[None, None, :], 1)
+    last_row = jnp.max(row_idx.reshape(n_blocks, block_rows), 1)
+    suf_starts = jnp.arange(skv.shape[0] // block_keys, dtype=jnp.int32) * block_keys
+    need_suf = suf_starts[None, :] <= last_row[:, None]
+    flags = jnp.concatenate([need_pre, need_suf], 1).astype(jnp.int32)
+    kern = functools.partial(attn_kernel, scale=scale, head_dim=head_dim, block_keys=block_keys)
+    full = lambda shape: pl.BlockSpec(shape, lambda i, f: (0, 0))
+    rowb = lambda w: pl.BlockSpec((block_rows, w), lambda i, f: (i, 0))
     return pl.pallas_call(
         kern,
-        grid=(n_rows // block_rows,),
-        in_specs=[rowb(head_dim), full(pkv.shape), full(skv.shape), rowb(1), rowb(1), rowb(1), full(key_prefix.shape), full(key_seg.shape)],
-        out_specs=rowb(head_dim),
+        grid_spec=pltpu.PrefetchScalarGridSpec(
+            num_scalar_prefetch=1,
+            grid=(n_blocks,),
+            in_specs=[rowb(head_dim), full(pkv.shape), full(skv.shape), rowb(1), rowb(1), rowb(1), full(key_prefix.shape), full(key_seg.shape)],
+            out_specs=rowb(head_dim),
+            scratch_shapes=[pltpu.VMEM((block_rows, 1), jnp.float32), pltpu.VMEM((block_rows, 1), jnp.float32), pltpu.VMEM((block_rows, head_dim), jnp.float32)],
+        ),
         out_shape=jax.ShapeDtypeStruct((n_rows, head_dim), jnp.bfloat16),
-    )(q, pkv, skv, row_prefix, row_seg, row_idx, key_prefix, key_seg)
+    )(flags, q, pkv, skv, row_prefix, row_seg, row_idx, key_prefix, key_seg)
 
 
 def rotate(tensor, positions):

time: 540 us -> 537 us (level)
  Pallas kernels: 59.9 us -> 45.3 us
  waiting for transfers between devices: 193 us -> 206 us
    pallas_call x1, Pallas kernels: 59.9 us -> 45.3 us  [attention(): pl.pallas_call(kern, grid_spec=pltpu.PrefetchScalarGridSpec(num_scalar_pr...]
    all_gather x1, waiting for transfers between devices: 25.9 us -> 39.1 us  [on_device(): lax.all_gather(attended, 'mdl', axis=0, tiled=True)]
where the time goes in v4:
time: 537 us; the launch traced here: 533 us
  waiting for transfers between devices  206 us (38%)
  blocking collectives  196 us (36%)
  Pallas kernels  45.3 us (8%)
  matrix products  27.6 us (5%)
  other arithmetic  19.6 us (4%)
  local copies, waits for them, and re-layouts  16.2 us (3%)
  between operations  15.8 us (3%)
  starting transfers between devices  7.35 us (1%)
    reduce_scatter x1, waiting for transfers between devices, on_device(): lax.psum_scatter(partial_ffn.astype(jnp.bfloat16), 'mdl', scatter_dimensi...  53.1 us
    pallas_call x1, Pallas kernels, attention(): pl.pallas_call(kern, grid_spec=pltpu.PrefetchScalarGridSpec(num_scalar_pr...  45.3 us
    all_to_all x1, blocking collectives, scatter_sum(): pieces = lax.all_to_all(pieces, axis, 0, 0, tiled=False)  40.9 us
    all_gather x1, waiting for transfers between devices, on_device(): lax.all_gather(attended, 'mdl', axis=0, tiled=True)  39.1 us
    all_to_all x1, waiting for transfers between devices, scatter_sum(): pieces = lax.all_to_all(pieces, axis, 0, 0, tiled=False)  34.1 us
    all_gather x1, waiting for transfers between devices, on_device(): lax.all_gather(activated, 'mdl', axis=0, tiled=True)  33.2 us
    reduce_scatter x1, waiting for transfers between devices, on_device(): lax.psum_scatter(partial_qkv, 'mdl', scatter_dimension=0, tiled=True)  31 us
    psum x1, blocking collectives, on_device(): packed = lax.psum(packed, 'tok')  20.3 us
  transfers between devices with their start and end apart: 8, of which 7 were waited for; matrix products, arithmetic and copies ran while one was open for 4% of the time, Pallas kernels for 0%

profile of v4, /device:TPU:1, one launch (start us, length us, event | category | flops | bytes accessed | tf_op | source)
XLA Modules:
  0.0 532.9 jit_solution(14826316527908550144)
XLA Ops:
  10.0 15.0 %psum.21 = f32[128]{0:T(128)S(1)} all-reduce(f32[128]{0:T(128)S(1)} %fusion.24), channel_id=1, replica_groups=mesh['grp'=4,'tok'=8,'mdl'=8] {'mdl'}, use_global_device_ids=true, to_apply=%region_5.6 | all-reduce | flops 128 | bytes 1024 | tf_op jit(solution)/shard_map/psum | solution.py:145
  24.9 14.3 %all-gather.1 = f32[8,1,128]{2,1,0:T(1,128)S(1)} all-gather(f32[1,1,128]{2,1,0:T(1,128)S(1)} %bitcast.98), channel_id=1, replica_groups=mesh['grp'=4,'tok'=8,'mdl'=8] {'tok'}, dimensions={0}, use_global_device_ids=true | all-gather | bytes 4608 | tf_op jit(solution)/shard_map/all_gather | solution.py:146
  39.3 9.1 %all-gather.18.cloned.1.call-done = bf16[1,1024,640]{2,1,0:T(8,128)(2,1)} async-done(((bf16[1,128,640]{2,1,0:T(8,128)(2,1)}), bf16[1,1024,640]{2,1,0:T(8,128)(2,1)}) %all-gather.18.cloned.1.call-update) | async-done | bytes 1310736 | tf_op jit(solution)/shard_map/all_gather | solution.py:144
  48.4 5.3 fusion.9
  64.8 31.0 %reduce-scatter.3.cloned.1.call-done = f32[128,896]{1,0:T(8,128)} async-done(((f32[1024,896]{1,0:T(8,128)}), f32[128,896]{1,0:T(8,128)}) %reduce-scatter.3.cloned.1.call-update) | async-done | bytes 458768 | tf_op jit(solution)/shard_map/reduce_scatter | solution.py:153
  95.7 1.7 slice.50
  98.6 1.4 subtract_convert_fusion
  105.0 1.7 pad_maximum_fusion.q_ref
  106.8 17.4 %all_gather.36 = bf16[1024,1,256]{2,0,1:T(8,128)(2,1)} all-gather(bf16[128,1,256]{2,0,1:T(8,128)(2,1)S(1)} %pad_maximum_fusion.1), channel_id=1, replica_groups=mesh['grp'=4,'tok'=8,'mdl'=8] {'mdl'}, dimensions={0}, use_global_device_ids=true | all-gather | bytes 589824 | tf_op jit(solution)/shard_map/all_gather | solution.py:178
  124.1 45.3 %shard_map.191 = bf16[640,128]{1,0:T(8,128)(2,1)} custom-call(s32[5,36]{1,0:T(8,128)} %add_convert_fusion.1.flags_ref, bf16[640,128]{1,0:T(8,128)(2,1)} %pad_maximum_fusion.q_ref, bf16[8192,256]{1,0:T(8,128)(2,1)} %bitcast.85, bf16[1024,256]{1,0:T(8,128)(2,1)} %bitcast.86, s32[640,1]{1,0:T(8,128)} %broadcast_in_dim_reshape.16.rp_ref, ...), custom_call_target="tpu_custom_call" | custom-call | tf_op jit(solution)/shard_map/pallas_call | solution.py:75
  169.4 1.7 reshape.333
  171.2 39.1 %all-gather.12.cloned.1.call-done = bf16[1024,640]{1,0:T(8,128)(2,1)} async-done(((bf16[128,640]{1,0:T(8,128)(2,1)}), bf16[1024,640]{1,0:T(8,128)(2,1)}) %all-gather.12.cloned.1.call-update) | async-done | bytes 1310736 | tf_op jit(solution)/shard_map/all_gather | solution.py:204
  210.3 2.8 convolution_convert_fusion.2
  213.1 40.9 %all_to_all.10 = bf16[8,128,640]{2,1,0:T(8,128)(2,1)} all-to-all(bf16[8,128,640]{2,1,0:T(8,128)(2,1)S(1)} %bitcast.88), channel_id=1, replica_groups=mesh['grp'=4,'tok'=8,'mdl'=8] {'tok'}, dimensions={0} | all-to-all | bytes 2621440 | tf_op jit(solution)/shard_map/all_to_all | solution.py:104
  254.1 2.2 reduce_sum.136
  257.4 12.9 %psum.22 = f32[128]{0:T(128)S(1)} all-reduce(f32[128]{0:T(128)S(1)} %multiply_reduce_fusion.1), channel_id=1, replica_groups=mesh['grp'=4,'tok'=8,'mdl'=8] {'mdl'}, use_global_device_ids=true, to_apply=%region_12.13 | all-reduce | flops 128 | bytes 1024 | tf_op jit(solution)/shard_map/psum | solution.py:211
  270.3 10.8 %all-gather.2 = f32[8,1,128]{2,1,0:T(1,128)S(1)} all-gather(f32[1,1,128]{2,1,0:T(1,128)S(1)} %bitcast.99), channel_id=1, replica_groups=mesh['grp'=4,'tok'=8,'mdl'=8] {'tok'}, dimensions={0}, use_global_device_ids=true | all-gather | bytes 4608 | tf_op jit(solution)/shard_map/all_gather | solution.py:212
  281.1 4.8 all-gather.14.cloned.1.call-done
  285.9 10.9 %convolution_convert_fusion = bf16[1024,3584]{1,0:T(8,128)(2,1)} fusion(bf16[640,1792]{1,0:T(8,128)(2,1)} %param.28, bf16[640,1792]{1,0:T(8,128)(2,1)} %param.27, bf16[1024,640]{1,0:T(8,128)(2,1)} %all-gather.14.cloned.1.call-done, bf16[1,1024,640]{2,1,0:T(8,128)(2,1)} %all-gather.18.cloned.1.call-done, f32[640]{0:T(1024)S(1)} %copy-done.17, f32[1024]{0:T(1024)S(1)} %bitcast.93), kind=kOutput, calls=%fused_computation | convolution fusion | flops 4714397696 | bytes 14555648 | tf_op jit(solution)/shard_map/dot_general | solution.py:219
  297.0 53.1 %reduce-scatter.5.cloned.1.call-done = bf16[128,3584]{1,0:T(8,128)(2,1)} async-done(((bf16[1024,3584]{1,0:T(8,128)(2,1)}), bf16[128,3584]{1,0:T(8,128)(2,1)}) %reduce-scatter.5.cloned.1.call-update) | async-done | bytes 917520 | tf_op jit(solution)/shard_map/reduce_scatter | solution.py:220
  352.5 33.2 %all-gather.16.cloned.1.call-done = bf16[1024,1792]{1,0:T(8,128)(2,1)} async-done(((bf16[128,1792]{1,0:T(8,128)(2,1)}), bf16[1024,1792]{1,0:T(8,128)(2,1)}) %all-gather.16.cloned.1.call-update) | async-done | bytes 3670032 | tf_op jit(solution)/shard_map/all_gather | solution.py:225
  385.7 6.8 %convolution_convert_fusion.1 = bf16[1024,640]{1,0:T(8,128)(2,1)} fusion(bf16[1024,1792]{1,0:T(8,128)(2,1)} %all-gather.16.cloned.1.call-done, bf16[1792,640]{1,0:T(8,128)(2,1)} %param.29), kind=kOutput, calls=%fused_computation.12 | convolution fusion | flops 2349465600 | bytes 7274496 | tf_op jit(solution)/shard_map/dot_general | solution.py:224
  392.6 6.9 %all-to-all-start.1 = ((bf16[8,128,640]{2,1,0:T(8,128)(2,1)}), bf16[8,128,640]{2,1,0:T(8,128)(2,1)}, u32[]{:S(2)}, u32[]{:S(2)}) async-start(bf16[8,128,640]{2,1,0:T(8,128)(2,1)} %bitcast.87), calls=%async_computation.3 | async-start | bytes 2621440 | tf_op jit(solution)/shard_map/all_to_all | solution.py:104
  400.3 34.1 %all-to-all-done.1 = bf16[8,128,640]{2,1,0:T(8,128)(2,1)} async-done(((bf16[8,128,640]{2,1,0:T(8,128)(2,1)}), bf16[8,128,640]{2,1,0:T(8,128)(2,1)}, u32[]{:S(2)}, u32[]{:S(2)}) %all-to-all-start.1) | async-done | bytes 1310752 | tf_op jit(solution)/shard_map/all_to_all | solution.py:104
  434.4 1.5 convert_reduce_fusion
  438.6 20.3 %psum.23 = f32[1,4,642]{2,1,0:T(4,128)S(1)} all-reduce(f32[1,4,642]{2,1,0:T(4,128)S(1)} %maximum_bitcast_fusion), channel_id=1, replica_groups=mesh['grp'=4,'tok'=8,'mdl'=8] {'tok'}, use_global_device_ids=true, to_apply=%region_19.20 | all-reduce | flops 2568 | bytes 20544 | tf_op jit(solution)/shard_map/psum | solution.py:242
  458.8 20.2 %all_gather.42 = f32[8,4,642]{2,1,0:T(4,128)S(1)} all-gather(f32[1,4,642]{2,1,0:T(4,128)S(1)} %psum.23), channel_id=1, replica_groups=mesh['grp'=4,'tok'=8,'mdl'=8] {'mdl'}, dimensions={0}, use_global_device_ids=true | all-gather | bytes 92448 | tf_op jit(solution)/shard_map/all_gather | solution.py:243
  479.4 9.8 %all-gather.3 = bf16[4,4,5120]{2,1,0:T(4,128)(2,1)S(1)} all-gather(bf16[1,4,5120]{2,1,0:T(4,128)(2,1)S(1)} %fusion.36), channel_id=1, replica_groups=mesh['grp'=4,'tok'=8,'mdl'=8] {'grp'}, dimensions={0}, use_global_device_ids=true | all-gather | bytes 204800 | tf_op jit(solution)/shard_map/all_gather | solution.py:252
  489.3 1.6 fusion.40
  490.9 14.5 %pmax.21 = f32[16]{0:T(128)S(1)} all-reduce(f32[16]{0:T(128)S(1)} %get-tuple-element.21), channel_id=1, replica_groups=mesh['grp'=4,'tok'=8,'mdl'=8] {'mdl'}, use_global_device_ids=true, to_apply=%region_23.24 | all-reduce | flops 16 | bytes 128 | tf_op jit(solution)/shard_map/pmax | solution.py:257
  505.4 10.7 %pmax.22 = f32[16]{0:T(128)S(1)} all-reduce(f32[16]{0:T(128)S(1)} %pmax.21), channel_id=1, replica_groups=mesh['grp'=4,'tok'=8,'mdl'=8] {'tok'}, use_global_device_ids=true, to_apply=%region_24.25 | all-reduce | flops 16 | bytes 128 | tf_op jit(solution)/shard_map/pmax | solution.py:258
  516.1 8.8 %pmax.23 = f32[4,4]{1,0:T(4,128)} all-reduce(f32[4,4]{1,0:T(4,128)S(1)} %reshape.337), channel_id=1, replica_groups=mesh['grp'=4,'tok'=8,'mdl'=8] {'grp'}, use_global_device_ids=true, to_apply=%region_25.26 | all-reduce | flops 16 | bytes 128 | tf_op jit(solution)/shard_map/pmax | solution.py:259
  (114 shorter events, 27.2 us)
Async XLA Ops:
  8.0 481.2 %copy-start = (bf16[300,5120]{1,0:T(8,128)(2,1)S(1)}, bf16[300,5120]{1,0:T(8,128)(2,1)}, u32[]{:S(2)}) copy-start(bf16[300,5120]{1,0:T(8,128)(2,1)} %param.31) | copy-start | bytes 9216004
  8.0 40.4 %all-gather.18.cloned.1.call-start = ((), (), s32[]{:S(2)}) async-start(), calls=%async_computation.10 | async-start | bytes 1474560 | tf_op jit(solution)/shard_map/all_gather | solution.py:144
  8.7 87.0 %reduce-scatter.3.cloned.1.call-start = ((), (), s32[]{:S(2)}) async-start(), calls=%async_computation.4 | async-start | bytes 4128768 | tf_op jit(solution)/shard_map/reduce_scatter | solution.py:153
  53.7 8.2 %copy-start.18 = (s32[32]{0:T(128)S(1)}, s32[32]{0:T(128)}, u32[]{:S(2)}) copy-start(s32[32]{0:T(128)} %param.19) | copy-start | bytes 388
  53.8 70.4 %all-gather.10.cloned.1.call-start = ((), (), s32[]{:S(2)}) async-start(), calls=%async_computation.5 | async-start | bytes 4325376 | tf_op jit(solution)/shard_map/all_gather | solution.py:184
  54.3 155.9 %all-gather.12.cloned.1.call-start = ((), (), s32[]{:S(2)}) async-start(), calls=%async_computation.6 | async-start | bytes 1474560 | tf_op jit(solution)/shard_map/all_gather | solution.py:204
  55.1 0.6 copy-start.9
  55.9 2.8 copy-start.13
  62.9 32.8 %copy-start.11 = (f32[64]{0:T(128)}, f32[64]{0:T(128)S(1)}, u32[]{:S(2)}) copy-start(f32[64]{0:T(128)S(1)} %negate_power_fusion) | copy-start | bytes 772
  64.0 31.8 %copy-start.12 = (f32[128]{0:T(128)}, f32[128]{0:T(128)S(1)}, u32[]{:S(2)}) copy-start(f32[128]{0:T(128)S(1)} %subtract_convert_fusion.1) | copy-start | bytes 1540
  103.0 3.7 copy-start.3
  104.9 1.8 copy-start.5
  104.9 1.8 copy-start.7
  171.2 114.7 %all-gather.14.cloned.1.call-start = ((), (), s32[]{:S(2)}) async-start(), calls=%async_computation.7 | async-start | bytes 1474560 | tf_op jit(solution)/shard_map/all_gather | solution.py:210
  213.1 43.2 %copy-start.1 = (bf16[1,128,640]{2,1,0:T(8,128)(2,1)S(1)}, bf16[1,128,640]{2,1,0:T(8,128)(2,1)}, u32[]{:S(2)}) copy-start(bf16[1,128,640]{2,1,0:T(8,128)(2,1)} %param.16) | copy-start | bytes 491524
  213.1 72.7 %copy-start.17 = (f32[640]{0:T(1024)S(1)}, f32[640]{0:T(1024)}, u32[]{:S(2)}) copy-start(f32[640]{0:T(1024)} %param.26) | copy-start | bytes 7684
  256.3 93.8 %reduce-scatter.5.cloned.1.call-start = ((), (), s32[]{:S(2)}) async-start(), calls=%async_computation.8 | async-start | bytes 8257536 | tf_op jit(solution)/shard_map/reduce_scatter | solution.py:220
  296.8 88.9 %all-gather.16.cloned.1.call-start = ((), (), s32[]{:S(2)}) async-start(), calls=%async_computation.9 | async-start | bytes 4128768 | tf_op jit(solution)/shard_map/all_gather | solution.py:225
  392.6 6.9 %copy-start.16 = (s32[4]{0:T(128)S(1)}, s32[4]{0:T(128)}, u32[]{:S(2)}) copy-start(s32[4]{0:T(128)} %get-tuple-element.19) | copy-start | bytes 52
  392.6 7.0 %copy-start.4 = (bf16[128,1,128]{2,0,1:T(8,128)(2,1)S(1)}, bf16[128,1,128]{2,0,1:T(8,128)(2,1)}, u32[]{:S(2)}) copy-start(bf16[128,1,128]{2,0,1:T(8,128)(2,1)} %copy-done.3) | copy-start | bytes 98308
  392.6 7.0 %copy-start.6 = (bf16[128,1,64]{2,0,1:T(8,128)(2,1)S(1)}, bf16[128,1,64]{2,0,1:T(8,128)(2,1)}, u32[]{:S(2)}) copy-start(bf16[128,1,64]{2,0,1:T(8,128)(2,1)} %copy-done.5) | copy-start | bytes 49156
  392.6 7.0 %copy-start.8 = (bf16[128,1,64]{2,0,1:T(8,128)(2,1)S(1)}, bf16[128,1,64]{2,0,1:T(8,128)(2,1)}, u32[]{:S(2)}) copy-start(bf16[128,1,64]{2,0,1:T(8,128)(2,1)} %copy-done.7) | copy-start | bytes 49156
  392.6 43.3 %copy-start.2 = (bf16[128,640]{1,0:T(8,128)(2,1)S(1)}, bf16[128,640]{1,0:T(8,128)(2,1)}, u32[]{:S(2)}) copy-start(bf16[128,640]{1,0:T(8,128)(2,1)} %reduce_sum.136) | copy-start | bytes 491524
  392.6 41.8 %all-to-all-start.1 = ((bf16[8,128,640]{2,1,0:T(8,128)(2,1)}), bf16[8,128,640]{2,1,0:T(8,128)(2,1)}, u32[]{:S(2)}, u32[]{:S(2)}) async-start(bf16[8,128,640]{2,1,0:T(8,128)(2,1)} %bitcast.87), calls=%async_computation.3 | async-start | bytes 2621440 | tf_op jit(solution)/shard_map/all_to_all | solution.py:104
  399.5 37.4 %copy-start.15 = (s32[128]{0:T(128)S(1)}, s32[128]{0:T(128)}, u32[]{:S(2)}) copy-start(s32[128]{0:T(128)} %get-tuple-element.15) | copy-start | bytes 1540
  400.3 79.0 %copy-start.10 = (f32[5120]{0:T(1024)S(1)}, f32[5120]{0:T(1024)}, u32[]{:S(2)}) copy-start(f32[5120]{0:T(1024)} %param.30) | copy-start | bytes 61444
  437.1 87.8 %copy-start.14 = (s32[4]{0:T(128)S(1)}, s32[4]{0:T(128)}, u32[]{:S(2)}) copy-start(s32[4]{0:T(128)} %copy-done.13) | copy-start | bytes 52
Sparse Core Ops, SparseCore 0:
  10.6 37.7 all-gather.17
  53.9 41.8 reduce-scatter.2
  171.3 38.9 all-gather.11
  256.4 29.3 all-gather.13
  296.9 53.1 reduce-scatter.4
  352.7 33.0 all-gather.15
Sparse Core Ops, SparseCore 1:
  56.8 56.3 all-gather.9

commit v5 on v2

--- a/solution.py
+++ b/solution.py
@@ -181,7 +181,10 @@
         w_down,
         preferred_element_type=jnp.float32,
     )
-    final_rows = residual + scatter_sum(partial_down.astype(jnp.bfloat16), "tok")
+    down_sum = lax.psum_scatter(
+        partial_down.astype(jnp.bfloat16), "tok", scatter_dimension=0, tiled=True
+    )
+    final_rows = residual + down_sum.astype(jnp.float32)
     tok_start = tok_idx * tok_rows
     my_tok_rows = tok_start + jnp.arange(tok_rows, dtype=jnp.int32)
     tok_seg = lax.dynamic_slice_in_dim(seg_row, tok_start, tok_rows)
@@ -191,15 +194,16 @@
     )
     ends = offsets + counts - 1
     picked = ends[:, None] == my_tok_rows[None, :]
-    last_part = jnp.sum(jnp.where(picked[:, :, None], final_rows[None, :, :], 0.0), 1)
+    last_res = jnp.sum(jnp.where(picked[:, :, None], residual[None, :, :], 0.0), 1)
+    last_down = jnp.take(partial_down, ends, axis=0, mode="clip")
+    last_part = lax.psum(last_res + last_down, "tok")
     last_squares = jnp.sum(last_part * last_part, -1)
-    packed = jnp.concatenate([last_part, req_squares[:, None], last_squares[:, None]], 1)
-    packed = lax.psum(packed, "tok")
+    packed = jnp.concatenate([last_part, last_squares[:, None]], 1)
     blocks = lax.all_gather(packed, "mdl", axis=0, tiled=False)
-    mdl_count = blocks.shape[0]
     last_rows = jnp.transpose(blocks[:, :, :feat_dev], (1, 0, 2)).reshape(req_count, model_width)
-    req_total = jnp.sum(blocks[:, :, feat_dev], 0)
-    last_total = jnp.sum(blocks[:, :, feat_dev + 1], 0)
+    last_total = jnp.sum(blocks[:, :, feat_dev], 0)
+    req_squares, _ = lax.optimization_barrier((req_squares, last_part))
+    req_total = lax.psum(lax.psum(req_squares, "tok"), "mdl")
     req_norm = jnp.sqrt(req_total / (counts.astype(jnp.float32) * model_width) + EPS)
     last_own = (
         last_rows * lax.rsqrt(last_total[:, None] / model_width + EPS) * final_gain

time: 518 us -> 515 us (level)
  blocking collectives: 195 us -> 232 us
  waiting for transfers between devices: 199 us -> 164 us
  starting transfers between devices: 7.15 us -> 0.33 us
    psum x1 -> x3, blocking collectives: 20.3 us -> 58.2 us  [the longest x2 34 us: on_device(): req_total = lax.psum(lax.psum(req_squares, 'tok'), 'mdl')]
    all_to_all x1 -> x0, waiting for transfers between devices: 34.1 us -> none  [scatter_sum(): pieces = lax.all_to_all(pieces, axis, 0, 0, tiled=False)]
    all_to_all x1 -> x0, starting transfers between devices: 6.87 us -> none  [scatter_sum(): pieces = lax.all_to_all(pieces, axis, 0, 0, tiled=False)]
  transfers between devices with their start and end apart: 8 -> 8, of which waited for: 7 -> 6; matrix products, arithmetic and copies ran while one was open for 3% -> 5% of each run, Pallas kernels for 0% -> 0%
where the time goes in v5:
time: 515 us; the launch traced here: 514 us
  blocking collectives  232 us (45%)
  waiting for transfers between devices  164 us (32%)
  matrix products  60 us (12%)
  other arithmetic  27.2 us (5%)
  between operations  15.8 us (3%)
  local copies, waits for them, and re-layouts  14.1 us (3%)
    reduce_scatter x1, waiting for transfers between devices, on_device(): lax.psum_scatter(partial_ffn.astype(jnp.bfloat16), 'mdl', scatter_dimensi...  53.3 us
    all_to_all x1, blocking collectives, scatter_sum(): pieces = lax.all_to_all(pieces, axis, 0, 0, tiled=False)  41 us
    reduce_scatter x1, waiting for transfers between devices, on_device(): lax.psum_scatter(partial_qkv, 'mdl', scatter_dimension=0, tiled=True)  34.8 us
    psum x2, blocking collectives, on_device(): req_total = lax.psum(lax.psum(req_squares, 'tok'), 'mdl')  34 us
    all_gather x1, waiting for transfers between devices, on_device(): lax.all_gather(activated, 'mdl', axis=0, tiled=True)  33.1 us
    all_gather x1, waiting for transfers between devices, on_device(): lax.all_gather(attended, 'mdl', axis=0, tiled=True)  27 us
    psum x1, blocking collectives, on_device(): last_part = lax.psum(last_res + last_down, 'tok')  24.1 us
    all_gather x1, blocking collectives, on_device(): blocks = lax.all_gather(packed, 'mdl', axis=0, tiled=False)  18.9 us
  transfers between devices with their start and end apart: 8, of which 6 were waited for; matrix products, arithmetic and copies ran while one was open for 5% of the time, Pallas kernels for 0%

profile of v5, /device:TPU:1, one launch (start us, length us, event | category | flops | bytes accessed | tf_op | source)
XLA Modules:
  0.0 513.6 jit_solution(5931888199886954794)
XLA Ops:
  10.0 15.0 %psum.35 = f32[128]{0:T(128)S(1)} all-reduce(f32[128]{0:T(128)S(1)} %fusion.59), channel_id=1, replica_groups=mesh['grp'=4,'tok'=8,'mdl'=8] {'mdl'}, use_global_device_ids=true, to_apply=%region_1.0 | all-reduce | flops 128 | bytes 1024 | tf_op jit(solution)/shard_map/psum | solution.py:72
  24.9 14.3 %all-gather.2 = f32[8,1,128]{2,1,0:T(1,128)S(1)} all-gather(f32[1,1,128]{2,1,0:T(1,128)S(1)} %bitcast.197), channel_id=1, replica_groups=mesh['grp'=4,'tok'=8,'mdl'=8] {'tok'}, dimensions={0}, use_global_device_ids=true | all-gather | bytes 4608 | tf_op jit(solution)/shard_map/all_gather | solution.py:73
  39.3 9.1 %all-gather.20.cloned.1.call-done = bf16[1,1024,640]{2,1,0:T(8,128)(2,1)} async-done(((bf16[1,128,640]{2,1,0:T(8,128)(2,1)}), bf16[1,1024,640]{2,1,0:T(8,128)(2,1)}) %all-gather.20.cloned.1.call-update) | async-done | bytes 1310736 | tf_op jit(solution)/shard_map/all_gather | solution.py:71
  48.4 5.2 %fusion.21 = f32[1024,896]{0,1:T(8,128)} fusion(bf16[1,1024,640]{2,1,0:T(8,128)(2,1)} %all-gather.20.cloned.1.call-done, f32[640]{0:T(1024)} %param.21, f32[1024]{0:T(1024)S(1)} %bitcast.194, bf16[640,128]{1,0:T(8,128)(2,1)} %param.24, bf16[640,128]{1,0:T(8,128)(2,1)} %param.23, bf16[640,640]{1,0:T(8,128)(2,1)} %param.22), kind=kOutput, calls=%fused_computation.31 | convolution fusion | flops 1180467200 | bytes 6134272 | tf_op jit(solution)/shard_map/dot_general | solution.py:79
  60.7 34.8 %reduce-scatter.4.cloned.1.call-done = f32[128,896]{0,1:T(8,128)} async-done(((f32[1024,896]{0,1:T(8,128)}), f32[128,896]{0,1:T(8,128)}) %reduce-scatter.4.cloned.1.call-update) | async-done | bytes 458768 | tf_op jit(solution)/shard_map/reduce_scatter | solution.py:80
  98.3 1.8 copy.62
  102.1 16.6 %all_gather.35 = bf16[1024,1,256]{0,2,1:T(8,128)(2,1)} all-gather(bf16[128,1,256]{0,2,1:T(8,128)(2,1)S(1)} %get-tuple-element.25), channel_id=1, replica_groups=mesh['grp'=4,'tok'=8,'mdl'=8] {'mdl'}, dimensions={0}, use_global_device_ids=true | all-gather | bytes 589824 | tf_op jit(solution)/shard_map/all_gather | solution.py:105
  120.5 12.9 %fusion = (f32[128,5]{0,1:T(8,128)S(1)}, f32[128,5,8192]{2,0,1:T(8,128)}) fusion(pred[128,8192]{1,0:T(8,128)(4,1)} %broadcast_compare_fusion, bf16[8192,1,256]{2,0,1:T(8,128)(2,1)} %bitcast.199, bf16[128,5,64]{2,0,1:T(8,128)(2,1)} %get-tuple-element.17, bf16[128,5,64]{2,0,1:T(8,128)(2,1)} %get-tuple-element.16), kind=kOutput, calls=%fused_computation.3 | convolution fusion | flops 1358232960 | bytes 24447488 | tf_op jit(solution)/shard_map/rcgd,kcd->rcgk/dot_general | solution.py:137
  133.5 2.2 fusion.15
  135.7 14.1 %fusion.35 = f32[1,128,128,5]{2,1,3,0:T(8,128)} fusion(bf16[8192,1,256]{2,0,1:T(8,128)(2,1)} %bitcast.200, f32[128,5,8192]{2,0,1:T(8,128)} %get-tuple-element.35, f32[128,5]{0,1:T(8,128)S(1)} %max.23, pred[128,8192]{1,0:T(8,128)(4,1)} %broadcast_compare_fusion), kind=kOutput, calls=%fused_computation.42 | convolution fusion | flops 1368391680 | bytes 24447488 | tf_op jit(solution)/shard_map/rcgk,kcd->rcgd/dot_general | solution.py:147
  149.9 10.7 %fusion.1 = f32[128,5]{0,1:T(8,128)S(1)} fusion(f32[128,5,8192]{2,0,1:T(8,128)} %get-tuple-element.35, f32[128,5]{0,1:T(8,128)S(1)} %max.23, pred[128,8192]{1,0:T(8,128)(4,1)} %broadcast_compare_fusion), kind=kLoop, calls=%fused_computation.4 | loop fusion | flops 26213760 | bytes 22025216 | tf_op jit(solution)/shard_map/reduce_sum | solution.py:146
  163.2 27.0 %all-gather.14.cloned.1.call-done = bf16[1024,640]{0,1:T(8,128)(2,1)} async-done(((bf16[128,640]{0,1:T(8,128)(2,1)}), bf16[1024,640]{0,1:T(8,128)(2,1)}) %all-gather.14.cloned.1.call-update) | async-done | bytes 1310736 | tf_op jit(solution)/shard_map/all_gather | solution.py:159
  190.3 2.9 convolution_convert_fusion.1
  193.2 41.0 %all_to_all.5 = bf16[8,128,640]{2,1,0:T(8,128)(2,1)} all-to-all(bf16[8,128,640]{2,1,0:T(8,128)(2,1)S(1)} %bitcast.186), channel_id=1, replica_groups=mesh['grp'=4,'tok'=8,'mdl'=8] {'tok'}, dimensions={0} | all-to-all | bytes 2621440 | tf_op jit(solution)/shard_map/all_to_all | solution.py:31
  234.2 2.2 reduce_sum.136
  237.5 12.9 %psum.36 = f32[128]{0:T(128)S(1)} all-reduce(f32[128]{0:T(128)S(1)} %multiply_reduce_fusion.1), channel_id=1, replica_groups=mesh['grp'=4,'tok'=8,'mdl'=8] {'mdl'}, use_global_device_ids=true, to_apply=%region_14.15 | all-reduce | flops 128 | bytes 1024 | tf_op jit(solution)/shard_map/psum | solution.py:166
  250.4 10.6 %all-gather.3 = f32[8,1,128]{2,1,0:T(1,128)S(1)} all-gather(f32[1,1,128]{2,1,0:T(1,128)S(1)} %bitcast.198), channel_id=1, replica_groups=mesh['grp'=4,'tok'=8,'mdl'=8] {'tok'}, dimensions={0}, use_global_device_ids=true | all-gather | bytes 4608 | tf_op jit(solution)/shard_map/all_gather | solution.py:167
  260.9 5.8 %all-gather.16.cloned.1.call-done = bf16[1024,640]{1,0:T(8,128)(2,1)} async-done(((bf16[128,640]{1,0:T(8,128)(2,1)}), bf16[1024,640]{1,0:T(8,128)(2,1)}) %all-gather.16.cloned.1.call-update) | async-done | bytes 1310736 | tf_op jit(solution)/shard_map/all_gather | solution.py:165
  266.7 10.9 %convolution_convert_fusion = bf16[1024,3584]{1,0:T(8,128)(2,1)} fusion(bf16[640,1792]{1,0:T(8,128)(2,1)} %param.28, bf16[640,1792]{1,0:T(8,128)(2,1)} %param.27, bf16[1024,640]{1,0:T(8,128)(2,1)} %all-gather.16.cloned.1.call-done, bf16[1,1024,640]{2,1,0:T(8,128)(2,1)} %all-gather.20.cloned.1.call-done, f32[640]{0:T(1024)S(1)} %copy-done.10, ...), kind=kOutput, calls=%fused_computation.9 | convolution fusion | flops 4714397696 | bytes 14555648 | tf_op jit(solution)/shard_map/dot_general | solution.py:174
  277.7 53.3 %reduce-scatter.6.cloned.1.call-done = bf16[128,3584]{1,0:T(8,128)(2,1)} async-done(((bf16[1024,3584]{1,0:T(8,128)(2,1)}), bf16[128,3584]{1,0:T(8,128)(2,1)}) %reduce-scatter.6.cloned.1.call-update) | async-done | bytes 917520 | tf_op jit(solution)/shard_map/reduce_scatter | solution.py:175
  333.5 33.1 %all-gather.18.cloned.1.call-done = bf16[1024,1792]{1,0:T(8,128)(2,1)} async-done(((bf16[128,1792]{1,0:T(8,128)(2,1)}), bf16[1024,1792]{1,0:T(8,128)(2,1)}) %all-gather.18.cloned.1.call-update) | async-done | bytes 3670032 | tf_op jit(solution)/shard_map/all_gather | solution.py:180
  366.6 7.7 %fusion.86 = (bf16[1024,640]{1,0:T(8,128)(2,1)}, f32[1024,640]{1,0:T(8,128)}) fusion(bf16[1024,1792]{1,0:T(8,128)(2,1)} %all-gather.18.cloned.1.call-done, bf16[1792,640]{1,0:T(8,128)(2,1)} %param.29), kind=kOutput, calls=%fused_computation.141 | convolution fusion | flops 2349465600 | bytes 9895936 | tf_op jit(solution)/shard_map/dot_general | solution.py:179
  375.3 2.3 gather_fusion
  377.6 24.1 %psum.37 = f32[4,640]{1,0:T(4,128)S(1)} all-reduce(f32[4,640]{1,0:T(4,128)S(1)} %add.160), channel_id=1, replica_groups=mesh['grp'=4,'tok'=8,'mdl'=8] {'tok'}, use_global_device_ids=true, to_apply=%region_20.21 | all-reduce | flops 2560 | bytes 20480 | tf_op jit(solution)/shard_map/psum | solution.py:199
  402.0 18.9 %all-gather.4 = f32[8,4,641]{2,1,0:T(4,128)S(1)} all-gather(f32[1,4,641]{2,1,0:T(4,128)S(1)} %maximum_bitcast_fusion), channel_id=3, replica_groups=mesh['grp'=4,'tok'=8,'mdl'=8] {'mdl'}, dimensions={0}, use_global_device_ids=true | all-gather | bytes 92304 | tf_op jit(solution)/shard_map/all_gather | solution.py:202
  421.2 10.2 %all-gather.5 = bf16[4,4,5120]{2,1,0:T(4,128)(2,1)} all-gather(bf16[1,4,5120]{2,1,0:T(4,128)(2,1)S(1)} %fusion.68), channel_id=1, replica_groups=mesh['grp'=4,'tok'=8,'mdl'=8] {'grp'}, dimensions={0}, use_global_device_ids=true | all-gather | bytes 204800 | tf_op jit(solution)/shard_map/all_gather | solution.py:211
  433.0 2.6 fusion.87
  435.6 14.8 %pmax.21 = f32[16]{0:T(128)S(1)} all-reduce(f32[16]{0:T(128)S(1)} %get-tuple-element.38), channel_id=1, replica_groups=mesh['grp'=4,'tok'=8,'mdl'=8] {'mdl'}, use_global_device_ids=true, to_apply=%region_26.27 | all-reduce | flops 16 | bytes 128 | tf_op jit(solution)/shard_map/pmax | solution.py:216
  450.4 10.7 %pmax.22 = f32[16]{0:T(128)S(1)} all-reduce(f32[16]{0:T(128)S(1)} %pmax.21), channel_id=1, replica_groups=mesh['grp'=4,'tok'=8,'mdl'=8] {'tok'}, use_global_device_ids=true, to_apply=%region_27.28 | all-reduce | flops 16 | bytes 128 | tf_op jit(solution)/shard_map/pmax | solution.py:217
  462.9 12.6 %psum.38 = f32[4]{0:T(128)S(1)} all-reduce(f32[4]{0:T(128)S(1)} %select_reduce_fusion.2), channel_id=1, replica_groups=mesh['grp'=4,'tok'=8,'mdl'=8] {'tok'}, use_global_device_ids=true, to_apply=%region_21.22 | all-reduce | flops 4 | bytes 32 | tf_op jit(solution)/shard_map/psum | solution.py:206
  475.5 8.6 %pmax.23 = f32[4,4]{1,0:T(4,128)} all-reduce(f32[4,4]{1,0:T(4,128)S(1)} %reshape.450), channel_id=1, replica_groups=mesh['grp'=4,'tok'=8,'mdl'=8] {'grp'}, use_global_device_ids=true, to_apply=%region_28.29 | all-reduce | flops 16 | bytes 128 | tf_op jit(solution)/shard_map/pmax | solution.py:218
  484.2 21.4 %psum.39 = f32[4]{0:T(128)S(1)} all-reduce(f32[4]{0:T(128)S(1)} %psum.38), channel_id=1, replica_groups=mesh['grp'=4,'tok'=8,'mdl'=8] {'mdl'}, use_global_device_ids=true, to_apply=%region_22.23 | all-reduce | flops 4 | bytes 32 | tf_op jit(solution)/shard_map/psum | solution.py:206
  (99 shorter events, 27.3 us)
Async XLA Ops:
  8.0 425.0 %copy-start = (bf16[300,5120]{1,0:T(8,128)(2,1)S(1)}, bf16[300,5120]{1,0:T(8,128)(2,1)}, u32[]{:S(2)}) copy-start(bf16[300,5120]{1,0:T(8,128)(2,1)} %param.31) | copy-start | bytes 9216004
  8.0 40.4 %all-gather.20.cloned.1.call-start = ((), (), s32[]{:S(2)}) async-start(), calls=%async_computation.11 | async-start | bytes 1474560 | tf_op jit(solution)/shard_map/all_gather | solution.py:71
  8.7 86.7 %reduce-scatter.4.cloned.1.call-start = ((), (), s32[]{:S(2)}) async-start(), calls=%async_computation.4 | async-start | bytes 4128768 | tf_op jit(solution)/shard_map/reduce_scatter | solution.py:80
  53.6 0.7 copy-start.11
  53.7 66.9 %all-gather.12.cloned.1.call-start = ((), (), s32[]{:S(2)}) async-start(), calls=%async_computation.5 | async-start | bytes 4325376 | tf_op jit(solution)/shard_map/all_gather | solution.py:131
  54.2 136.0 %all-gather.14.cloned.1.call-start = ((), (), s32[]{:S(2)}) async-start(), calls=%async_computation.6 | async-start | bytes 1474560 | tf_op jit(solution)/shard_map/all_gather | solution.py:159
  120.5 13.0 %copy-start.4 = (bf16[1024,1,256]{0,2,1:T(8,128)(2,1)S(1)}, bf16[1024,1,256]{0,2,1:T(8,128)(2,1)}, u32[]{:S(2)}) copy-start(bf16[1024,1,256]{0,2,1:T(8,128)(2,1)} %all_gather.35) | copy-start | bytes 1572868
  120.5 13.0 %copy-start.6 = (pred[128,1024]{0,1:T(8,128)(4,1)S(1)}, pred[128,1024]{0,1:T(8,128)(4,1)}, u32[]{:S(2)}) copy-start(pred[128,1024]{0,1:T(8,128)(4,1)} %fusion.56) | copy-start | bytes 393220
  120.5 13.0 %copy-start.7 = (bf16[128,5,64]{2,0,1:T(8,128)(2,1)S(1)}, bf16[128,5,64]{2,0,1:T(8,128)(2,1)}, u32[]{:S(2)}) copy-start(bf16[128,5,64]{2,0,1:T(8,128)(2,1)} %get-tuple-element.16) | copy-start | bytes 245764
  120.5 13.0 %copy-start.8 = (bf16[128,5,64]{2,0,1:T(8,128)(2,1)S(1)}, bf16[128,5,64]{2,0,1:T(8,128)(2,1)}, u32[]{:S(2)}) copy-start(bf16[128,5,64]{2,0,1:T(8,128)(2,1)} %get-tuple-element.17) | copy-start | bytes 245764
  149.9 10.7 %copy-start.1 = (f32[1024,128,5]{1,0,2:T(8,128)S(1)}, f32[1024,128,5]{1,0,2:T(8,128)}, u32[]{:S(2)}) copy-start(f32[1024,128,5]{1,0,2:T(8,128)} %get-tuple-element.33) | copy-start | bytes 7864324
  160.6 1.0 copy-start.5
  160.6 1.1 copy-start.12
  163.2 103.5 %all-gather.16.cloned.1.call-start = ((), (), s32[]{:S(2)}) async-start(), calls=%async_computation.7 | async-start | bytes 1474560 | tf_op jit(solution)/shard_map/all_gather | solution.py:165
  193.2 43.3 %copy-start.2 = (bf16[1,128,640]{2,1,0:T(8,128)(2,1)S(1)}, bf16[1,128,640]{2,1,0:T(8,128)(2,1)}, u32[]{:S(2)}) copy-start(bf16[1,128,640]{2,1,0:T(8,128)(2,1)} %param.16) | copy-start | bytes 491524
  193.2 73.5 %copy-start.10 = (f32[640]{0:T(1024)S(1)}, f32[640]{0:T(1024)}, u32[]{:S(2)}) copy-start(f32[640]{0:T(1024)} %param.26) | copy-start | bytes 7684
  236.4 94.6 %reduce-scatter.6.cloned.1.call-start = ((), (), s32[]{:S(2)}) async-start(), calls=%async_computation.8 | async-start | bytes 8257536 | tf_op jit(solution)/shard_map/reduce_scatter | solution.py:175
  277.7 88.9 %all-gather.18.cloned.1.call-start = ((), (), s32[]{:S(2)}) async-start(), calls=%async_computation.9 | async-start | bytes 4128768 | tf_op jit(solution)/shard_map/all_gather | solution.py:180
  333.4 127.7 %reduce-scatter.8.cloned.1.call-start = ((), (), s32[]{:S(2)}) async-start(), calls=%async_computation.10 | async-start | bytes 1474560 | tf_op jit(solution)/shard_map/reduce_scatter | solution.py:184
  333.5 41.5 %copy-start.3 = (bf16[128,640]{1,0:T(8,128)(2,1)S(1)}, bf16[128,640]{1,0:T(8,128)(2,1)}, u32[]{:S(2)}) copy-start(bf16[128,640]{1,0:T(8,128)(2,1)} %reduce_sum.136) | copy-start | bytes 491524
  374.3 46.8 %copy-start.9 = (f32[5120]{0:T(1024)S(1)}, f32[5120]{0:T(1024)}, u32[]{:S(2)}) copy-start(f32[5120]{0:T(1024)} %param.30) | copy-start | bytes 61444
Sparse Core Ops, SparseCore 0:
  10.6 37.7 all-gather.19
  53.8 41.6 reduce-scatter.3
  163.3 26.8 all-gather.13
  236.5 30.1 all-gather.15
  277.8 53.1 reduce-scatter.5
  333.5 33.0 all-gather.17
  374.4 35.2 reduce-scatter.7
Sparse Core Ops, SparseCore 1:
  56.7 56.3 all-gather.11

commit v6 on v5

--- a/solution.py
+++ b/solution.py
@@ -196,15 +196,12 @@
     picked = ends[:, None] == my_tok_rows[None, :]
     last_res = jnp.sum(jnp.where(picked[:, :, None], residual[None, :, :], 0.0), 1)
     last_down = jnp.take(partial_down, ends, axis=0, mode="clip")
-    last_part = lax.psum(last_res + last_down, "tok")
+    last_part = jnp.sum(lax.all_gather(last_res + last_down, "tok", axis=0, tiled=False), 0)
     last_squares = jnp.sum(last_part * last_part, -1)
     packed = jnp.concatenate([last_part, last_squares[:, None]], 1)
     blocks = lax.all_gather(packed, "mdl", axis=0, tiled=False)
     last_rows = jnp.transpose(blocks[:, :, :feat_dev], (1, 0, 2)).reshape(req_count, model_width)
     last_total = jnp.sum(blocks[:, :, feat_dev], 0)
-    req_squares, _ = lax.optimization_barrier((req_squares, last_part))
-    req_total = lax.psum(lax.psum(req_squares, "tok"), "mdl")
-    req_norm = jnp.sqrt(req_total / (counts.astype(jnp.float32) * model_width) + EPS)
     last_own = (
         last_rows * lax.rsqrt(last_total[:, None] / model_width + EPS) * final_gain
     ).astype(jnp.bfloat16)
@@ -213,9 +210,14 @@
         last_normed, lm_head, (((1,), (1,)), ((), ())), preferred_element_type=jnp.float32
     )
     local_max = jnp.max(logits, -1)
-    local_max = lax.pmax(local_max, "mdl")
-    local_max = lax.pmax(local_max, "tok")
-    max_logit = lax.pmax(local_max, "grp").reshape(groups_total, req_count)
+    rows_total = local_max.shape[0]
+    stats = jnp.concatenate([local_max, req_squares])
+    stats = lax.all_gather(stats, "tok", axis=0, tiled=False)
+    stats = jnp.concatenate([jnp.max(stats[:, :rows_total], 0), jnp.sum(stats[:, rows_total:], 0)])
+    stats = lax.all_gather(stats, "mdl", axis=0, tiled=False)
+    req_total = jnp.sum(stats[:, rows_total:], 0)
+    req_norm = jnp.sqrt(req_total / (counts.astype(jnp.float32) * model_width) + EPS)
+    max_logit = lax.pmax(jnp.max(stats[:, :rows_total], 0), "grp").reshape(groups_total, req_count)
     return (
         final_rows.astype(jnp.bfloat16)[None],
         appended[None],

time: 515 us -> 483 us (0.938)
  blocking collectives: 232 us -> 199 us
    psum x3 -> x0, blocking collectives: 58.2 us -> none  [the longest x2 34 us: on_device(): req_total = lax.psum(lax.psum(req_squares, 'tok'), 'mdl')]
    unnamed x0 -> x2, blocking collectives: none -> 30.8 us
    pmax x3 -> x1, blocking collectives: 34.1 us -> 8.64 us  [on_device(): lax.pmax(jnp.max(stats[:, :rows_total], 0), 'grp')]
    all_gather x0 -> x1, blocking collectives: none -> 20.8 us  [on_device(): lax.all_gather(last_res + last_down, 'tok', axis=0, tiled=False)]
  transfers between devices with their start and end apart: 8 -> 8, of which waited for: 6 -> 6; matrix products, arithmetic and copies ran while one was open for 5% -> 6% of each run, Pallas kernels for 0% -> 0%
where the time goes in v6:
time: 483 us; the launch traced here: 482 us
  blocking collectives  199 us (41%)
  waiting for transfers between devices  161 us (33%)
  matrix products  60 us (12%)
  other arithmetic  29.1 us (6%)
  between operations  17.2 us (4%)
  local copies, waits for them, and re-layouts  15.9 us (3%)
    reduce_scatter x1, waiting for transfers between devices, on_device(): lax.psum_scatter(partial_ffn.astype(jnp.bfloat16), 'mdl', scatter_dimensi...  53.2 us
    all_to_all x1, blocking collectives, scatter_sum(): pieces = lax.all_to_all(pieces, axis, 0, 0, tiled=False)  41 us
    reduce_scatter x1, waiting for transfers between devices, on_device(): lax.psum_scatter(partial_qkv, 'mdl', scatter_dimension=0, tiled=True)  34.3 us
    unnamed x2, blocking collectives  30.8 us
    all_gather x1, waiting for transfers between devices, on_device(): lax.all_gather(activated, 'mdl', axis=0, tiled=True)  29.8 us
    all_gather x1, waiting for transfers between devices, on_device(): lax.all_gather(attended, 'mdl', axis=0, tiled=True)  27 us
    all_gather x1, blocking collectives, on_device(): lax.all_gather(last_res + last_down, 'tok', axis=0, tiled=False)  20.8 us
    all_gather x1, blocking collectives, on_device(): blocks = lax.all_gather(packed, 'mdl', axis=0, tiled=False)  18.1 us
  transfers between devices with their start and end apart: 8, of which 6 were waited for; matrix products, arithmetic and copies ran while one was open for 6% of the time, Pallas kernels for 0%

profile of v6, /device:TPU:1, one launch (start us, length us, event | category | flops | bytes accessed | tf_op | source)
XLA Modules:
  0.0 482.0 jit_solution(3354644505176659271)
XLA Ops:
  10.0 15.0 %psum.14 = f32[128]{0:T(128)S(1)} all-reduce(f32[128]{0:T(128)S(1)} %fusion.59), channel_id=1, replica_groups=mesh['grp'=4,'tok'=8,'mdl'=8] {'mdl'}, use_global_device_ids=true, to_apply=%region_1.0 | all-reduce | flops 128 | bytes 1024 | tf_op jit(solution)/shard_map/psum | solution.py:72
  24.9 14.3 %all-gather.5 = f32[8,1,128]{2,1,0:T(1,128)S(1)} all-gather(f32[1,1,128]{2,1,0:T(1,128)S(1)} %bitcast.201), channel_id=1, replica_groups=mesh['grp'=4,'tok'=8,'mdl'=8] {'tok'}, dimensions={0}, use_global_device_ids=true | all-gather | bytes 4608 | tf_op jit(solution)/shard_map/all_gather | solution.py:73
  39.3 9.1 %all-gather.24.cloned.1.call-done = bf16[1,1024,640]{2,1,0:T(8,128)(2,1)} async-done(((bf16[1,128,640]{2,1,0:T(8,128)(2,1)}), bf16[1,1024,640]{2,1,0:T(8,128)(2,1)}) %all-gather.24.cloned.1.call-update) | async-done | bytes 1310736 | tf_op jit(solution)/shard_map/all_gather | solution.py:71
  48.4 5.2 %fusion.21 = f32[1024,896]{0,1:T(8,128)} fusion(bf16[1,1024,640]{2,1,0:T(8,128)(2,1)} %all-gather.24.cloned.1.call-done, f32[640]{0:T(1024)} %param.21, f32[1024]{0:T(1024)S(1)} %bitcast.198, bf16[640,128]{1,0:T(8,128)(2,1)} %param.24, bf16[640,128]{1,0:T(8,128)(2,1)} %param.23, bf16[640,640]{1,0:T(8,128)(2,1)} %param.22), kind=kOutput, calls=%fused_computation.31 | convolution fusion | flops 1180467200 | bytes 6134272 | tf_op jit(solution)/shard_map/dot_general | solution.py:79
  61.2 34.3 %reduce-scatter.4.cloned.1.call-done = f32[128,896]{0,1:T(8,128)} async-done(((f32[1024,896]{0,1:T(8,128)}), f32[128,896]{0,1:T(8,128)}) %reduce-scatter.4.cloned.1.call-update) | async-done | bytes 458768 | tf_op jit(solution)/shard_map/reduce_scatter | solution.py:80
  98.3 1.8 copy.77
  102.1 16.6 %all_gather.51 = bf16[1024,1,256]{0,2,1:T(8,128)(2,1)} all-gather(bf16[128,1,256]{0,2,1:T(8,128)(2,1)S(1)} %get-tuple-element.23), channel_id=1, replica_groups=mesh['grp'=4,'tok'=8,'mdl'=8] {'mdl'}, dimensions={0}, use_global_device_ids=true | all-gather | bytes 589824 | tf_op jit(solution)/shard_map/all_gather | solution.py:105
  118.7 1.8 subtract_convert_fusion
  120.5 12.9 %fusion = (f32[128,5]{0,1:T(8,128)S(1)}, f32[128,5,8192]{2,0,1:T(8,128)}) fusion(pred[128,8192]{1,0:T(8,128)(4,1)} %broadcast_compare_fusion, bf16[8192,1,256]{2,0,1:T(8,128)(2,1)} %bitcast.203, bf16[128,5,64]{2,0,1:T(8,128)(2,1)} %get-tuple-element.15, bf16[128,5,64]{2,0,1:T(8,128)(2,1)} %get-tuple-element.14), kind=kOutput, calls=%fused_computation.3 | convolution fusion | flops 1358232960 | bytes 24447488 | tf_op jit(solution)/shard_map/rcgd,kcd->rcgk/dot_general | solution.py:137
  133.5 2.2 fusion.15
  135.7 14.1 %fusion.35 = f32[1,128,128,5]{2,1,3,0:T(8,128)} fusion(bf16[8192,1,256]{2,0,1:T(8,128)(2,1)} %bitcast.204, f32[128,5,8192]{2,0,1:T(8,128)} %get-tuple-element.33, f32[128,5]{0,1:T(8,128)S(1)} %max.19, pred[128,8192]{1,0:T(8,128)(4,1)} %broadcast_compare_fusion), kind=kOutput, calls=%fused_computation.42 | convolution fusion | flops 1368391680 | bytes 24447488 | tf_op jit(solution)/shard_map/rcgk,kcd->rcgd/dot_general | solution.py:147
  149.9 10.7 %fusion.1 = f32[128,5]{0,1:T(8,128)S(1)} fusion(f32[128,5,8192]{2,0,1:T(8,128)} %get-tuple-element.33, f32[128,5]{0,1:T(8,128)S(1)} %max.19, pred[128,8192]{1,0:T(8,128)(4,1)} %broadcast_compare_fusion), kind=kLoop, calls=%fused_computation.4 | loop fusion | flops 26213760 | bytes 22025216 | tf_op jit(solution)/shard_map/reduce_sum | solution.py:146
  163.2 27.0 %all-gather.18.cloned.1.call-done = bf16[1024,640]{0,1:T(8,128)(2,1)} async-done(((bf16[128,640]{0,1:T(8,128)(2,1)}), bf16[1024,640]{0,1:T(8,128)(2,1)}) %all-gather.18.cloned.1.call-update) | async-done | bytes 1310736 | tf_op jit(solution)/shard_map/all_gather | solution.py:159
  190.3 2.9 convolution_convert_fusion.1
  193.2 41.0 %all_to_all.5 = bf16[8,128,640]{2,1,0:T(8,128)(2,1)} all-to-all(bf16[8,128,640]{2,1,0:T(8,128)(2,1)S(1)} %bitcast.190), channel_id=1, replica_groups=mesh['grp'=4,'tok'=8,'mdl'=8] {'tok'}, dimensions={0} | all-to-all | bytes 2621440 | tf_op jit(solution)/shard_map/all_to_all | solution.py:31
  234.2 2.2 reduce_sum.163
  237.5 12.9 %psum.15 = f32[128]{0:T(128)S(1)} all-reduce(f32[128]{0:T(128)S(1)} %multiply_reduce_fusion.1), channel_id=1, replica_groups=mesh['grp'=4,'tok'=8,'mdl'=8] {'mdl'}, use_global_device_ids=true, to_apply=%region_14.15 | all-reduce | flops 128 | bytes 1024 | tf_op jit(solution)/shard_map/psum | solution.py:166
  250.4 10.6 %all-gather.6 = f32[8,1,128]{2,1,0:T(1,128)S(1)} all-gather(f32[1,1,128]{2,1,0:T(1,128)S(1)} %bitcast.202), channel_id=1, replica_groups=mesh['grp'=4,'tok'=8,'mdl'=8] {'tok'}, dimensions={0}, use_global_device_ids=true | all-gather | bytes 4608 | tf_op jit(solution)/shard_map/all_gather | solution.py:167
  260.9 5.8 %all-gather.20.cloned.1.call-done = bf16[1024,640]{1,0:T(8,128)(2,1)} async-done(((bf16[128,640]{1,0:T(8,128)(2,1)}), bf16[1024,640]{1,0:T(8,128)(2,1)}) %all-gather.20.cloned.1.call-update) | async-done | bytes 1310736 | tf_op jit(solution)/shard_map/all_gather | solution.py:165
  266.7 10.9 %convolution_convert_fusion = bf16[1024,3584]{1,0:T(8,128)(2,1)} fusion(bf16[640,1792]{1,0:T(8,128)(2,1)} %param.28, bf16[640,1792]{1,0:T(8,128)(2,1)} %param.27, bf16[1024,640]{1,0:T(8,128)(2,1)} %all-gather.20.cloned.1.call-done, bf16[1,1024,640]{2,1,0:T(8,128)(2,1)} %all-gather.24.cloned.1.call-done, f32[640]{0:T(1024)S(1)} %copy-done.11, ...), kind=kOutput, calls=%fused_computation.9 | convolution fusion | flops 4714397696 | bytes 14555648 | tf_op jit(solution)/shard_map/dot_general | solution.py:174
  277.7 53.2 %reduce-scatter.6.cloned.1.call-done = bf16[128,3584]{1,0:T(8,128)(2,1)} async-done(((bf16[1024,3584]{1,0:T(8,128)(2,1)}), bf16[128,3584]{1,0:T(8,128)(2,1)}) %reduce-scatter.6.cloned.1.call-update) | async-done | bytes 917520 | tf_op jit(solution)/shard_map/reduce_scatter | solution.py:175
  336.8 29.8 %all-gather.22.cloned.1.call-done = bf16[1024,1792]{1,0:T(8,128)(2,1)} async-done(((bf16[128,1792]{1,0:T(8,128)(2,1)}), bf16[1024,1792]{1,0:T(8,128)(2,1)}) %all-gather.22.cloned.1.call-update) | async-done | bytes 3670032 | tf_op jit(solution)/shard_map/all_gather | solution.py:180
  366.6 7.7 %fusion.86 = (bf16[1024,640]{1,0:T(8,128)(2,1)}, f32[1024,640]{1,0:T(8,128)}) fusion(bf16[1024,1792]{1,0:T(8,128)(2,1)} %all-gather.22.cloned.1.call-done, bf16[1792,640]{1,0:T(8,128)(2,1)} %param.29), kind=kOutput, calls=%fused_computation.148 | convolution fusion | flops 2349465600 | bytes 9895936 | tf_op jit(solution)/shard_map/dot_general | solution.py:179
  374.6 2.3 gather_fusion
  376.9 20.8 %all-gather.7 = f32[8,4,640]{2,1,0:T(4,128)S(1)} all-gather(f32[1,4,640]{2,1,0:T(4,128)S(1)} %add_bitcast_fusion), channel_id=3, replica_groups=mesh['grp'=4,'tok'=8,'mdl'=8] {'tok'}, dimensions={0}, use_global_device_ids=true | all-gather | bytes 92160 | tf_op jit(solution)/shard_map/all_gather | solution.py:199
  397.9 18.1 %all-gather.8 = f32[8,4,641]{2,1,0:T(4,128)S(1)} all-gather(f32[1,4,641]{2,1,0:T(4,128)S(1)} %maximum_bitcast_fusion), channel_id=4, replica_groups=mesh['grp'=4,'tok'=8,'mdl'=8] {'mdl'}, dimensions={0}, use_global_device_ids=true | all-gather | bytes 92304 | tf_op jit(solution)/shard_map/all_gather | solution.py:202
  416.3 10.2 %all-gather.9 = bf16[4,4,5120]{2,1,0:T(4,128)(2,1)} all-gather(bf16[1,4,5120]{2,1,0:T(4,128)(2,1)S(1)} %fusion.68), channel_id=1, replica_groups=mesh['grp'=4,'tok'=8,'mdl'=8] {'grp'}, dimensions={0}, use_global_device_ids=true | all-gather | bytes 204800 | tf_op jit(solution)/shard_map/all_gather | solution.py:208
  428.1 2.6 fusion.87
  430.7 1.7 multiply_reduce_fusion
  433.3 12.2 %all-reduce = f32[160]{0:T(256)S(1)} all-reduce(f32[160]{0:T(256)S(1)} %maximum_dynamic-update-slice_fusion), channel_id=5, replica_groups=mesh['grp'=4,'tok'=8,'mdl'=8] {'tok'}, use_global_device_ids=true, to_apply=%add | all-reduce | flops 160 | bytes 1280
  445.9 18.5 %all-reduce.1 = f32[160]{0:T(256)S(1)} all-reduce(f32[160]{0:T(256)S(1)} %maximum_dynamic-update-slice_fusion.1), channel_id=6, replica_groups=mesh['grp'=4,'tok'=8,'mdl'=8] {'mdl'}, use_global_device_ids=true, to_apply=%add.1 | all-reduce | flops 160 | bytes 1280
  465.9 8.6 %pmax.7 = f32[4,4]{1,0:T(4,128)} all-reduce(f32[4,4]{1,0:T(4,128)S(1)} %reshape.491), channel_id=1, replica_groups=mesh['grp'=4,'tok'=8,'mdl'=8] {'grp'}, use_global_device_ids=true, to_apply=%region_28.29 | all-reduce | flops 16 | bytes 128 | tf_op jit(solution)/shard_map/pmax | solution.py:220
  (116 shorter events, 27.5 us)
Async XLA Ops:
  8.0 420.1 %copy-start = (bf16[300,5120]{1,0:T(8,128)(2,1)S(1)}, bf16[300,5120]{1,0:T(8,128)(2,1)}, u32[]{:S(2)}) copy-start(bf16[300,5120]{1,0:T(8,128)(2,1)} %param.31) | copy-start | bytes 9216004
  8.0 40.4 %all-gather.24.cloned.1.call-start = ((), (), s32[]{:S(2)}) async-start(), calls=%async_computation.11 | async-start | bytes 1474560 | tf_op jit(solution)/shard_map/all_gather | solution.py:71
  8.7 86.7 %reduce-scatter.4.cloned.1.call-start = ((), (), s32[]{:S(2)}) async-start(), calls=%async_computation.4 | async-start | bytes 4128768 | tf_op jit(solution)/shard_map/reduce_scatter | solution.py:80
  53.6 0.7 copy-start.12
  53.7 66.9 %all-gather.16.cloned.1.call-start = ((), (), s32[]{:S(2)}) async-start(), calls=%async_computation.5 | async-start | bytes 4325376 | tf_op jit(solution)/shard_map/all_gather | solution.py:131
  54.2 136.0 %all-gather.18.cloned.1.call-start = ((), (), s32[]{:S(2)}) async-start(), calls=%async_computation.6 | async-start | bytes 1474560 | tf_op jit(solution)/shard_map/all_gather | solution.py:159
  55.4 2.2 copy-start.10
  120.5 13.0 %copy-start.4 = (bf16[1024,1,256]{0,2,1:T(8,128)(2,1)S(1)}, bf16[1024,1,256]{0,2,1:T(8,128)(2,1)}, u32[]{:S(2)}) copy-start(bf16[1024,1,256]{0,2,1:T(8,128)(2,1)} %all_gather.51) | copy-start | bytes 1572868
  120.5 13.0 %copy-start.6 = (pred[128,1024]{0,1:T(8,128)(4,1)S(1)}, pred[128,1024]{0,1:T(8,128)(4,1)}, u32[]{:S(2)}) copy-start(pred[128,1024]{0,1:T(8,128)(4,1)} %fusion.56) | copy-start | bytes 393220
  120.5 13.0 %copy-start.7 = (bf16[128,5,64]{2,0,1:T(8,128)(2,1)S(1)}, bf16[128,5,64]{2,0,1:T(8,128)(2,1)}, u32[]{:S(2)}) copy-start(bf16[128,5,64]{2,0,1:T(8,128)(2,1)} %get-tuple-element.14) | copy-start | bytes 245764
  120.5 13.0 %copy-start.8 = (bf16[128,5,64]{2,0,1:T(8,128)(2,1)S(1)}, bf16[128,5,64]{2,0,1:T(8,128)(2,1)}, u32[]{:S(2)}) copy-start(bf16[128,5,64]{2,0,1:T(8,128)(2,1)} %get-tuple-element.15) | copy-start | bytes 245764
  149.9 10.7 %copy-start.1 = (f32[1024,128,5]{1,0,2:T(8,128)S(1)}, f32[1024,128,5]{1,0,2:T(8,128)}, u32[]{:S(2)}) copy-start(f32[1024,128,5]{1,0,2:T(8,128)} %get-tuple-element.31) | copy-start | bytes 7864324
  160.6 1.0 copy-start.5
  160.6 1.1 copy-start.15
  163.2 103.5 %all-gather.20.cloned.1.call-start = ((), (), s32[]{:S(2)}) async-start(), calls=%async_computation.7 | async-start | bytes 1474560 | tf_op jit(solution)/shard_map/all_gather | solution.py:165
  193.2 43.3 %copy-start.2 = (bf16[1,128,640]{2,1,0:T(8,128)(2,1)S(1)}, bf16[1,128,640]{2,1,0:T(8,128)(2,1)}, u32[]{:S(2)}) copy-start(bf16[1,128,640]{2,1,0:T(8,128)(2,1)} %param.16) | copy-start | bytes 491524
  193.2 73.5 %copy-start.11 = (f32[640]{0:T(1024)S(1)}, f32[640]{0:T(1024)}, u32[]{:S(2)}) copy-start(f32[640]{0:T(1024)} %param.26) | copy-start | bytes 7684
  236.4 94.6 %reduce-scatter.6.cloned.1.call-start = ((), (), s32[]{:S(2)}) async-start(), calls=%async_computation.8 | async-start | bytes 8257536 | tf_op jit(solution)/shard_map/reduce_scatter | solution.py:175
  277.7 55.8 %copy-start.14 = (u32[256]{0:T(256)S(1)}, u32[256]{0:T(256)}, u32[]{:S(2)}) copy-start(u32[256]{0:T(256)} %constant.117) | copy-start | bytes 3076
  277.7 56.4 %copy-start.13 = (u32[256]{0:T(256)S(1)}, u32[256]{0:T(256)}, u32[]{:S(2)}) copy-start(u32[256]{0:T(256)} %constant.112) | copy-start | bytes 3076
  277.7 88.9 %all-gather.22.cloned.1.call-start = ((), (), s32[]{:S(2)}) async-start(), calls=%async_computation.9 | async-start | bytes 4128768 | tf_op jit(solution)/shard_map/all_gather | solution.py:180
  333.4 97.3 %reduce-scatter.8.cloned.1.call-start = ((), (), s32[]{:S(2)}) async-start(), calls=%async_computation.10 | async-start | bytes 1474560 | tf_op jit(solution)/shard_map/reduce_scatter | solution.py:184
  336.8 37.5 %copy-start.3 = (bf16[128,640]{1,0:T(8,128)(2,1)S(1)}, bf16[128,640]{1,0:T(8,128)(2,1)}, u32[]{:S(2)}) copy-start(bf16[128,640]{1,0:T(8,128)(2,1)} %reduce_sum.163) | copy-start | bytes 491524
  374.3 41.9 %copy-start.9 = (f32[5120]{0:T(1024)S(1)}, f32[5120]{0:T(1024)}, u32[]{:S(2)}) copy-start(f32[5120]{0:T(1024)} %param.30) | copy-start | bytes 61444
Sparse Core Ops, SparseCore 0:
  10.6 37.7 all-gather.23
  53.8 41.6 reduce-scatter.3
  163.3 26.8 all-gather.17
  236.5 30.1 all-gather.19
  277.8 53.1 reduce-scatter.5
  333.5 33.0 all-gather.21
  374.4 35.1 reduce-scatter.7
Sparse Core Ops, SparseCore 1:
  56.7 56.3 all-gather.15

commit v7 on v6

--- a/solution.py
+++ b/solution.py
@@ -196,12 +196,10 @@
     picked = ends[:, None] == my_tok_rows[None, :]
     last_res = jnp.sum(jnp.where(picked[:, :, None], residual[None, :, :], 0.0), 1)
     last_down = jnp.take(partial_down, ends, axis=0, mode="clip")
-    last_part = jnp.sum(lax.all_gather(last_res + last_down, "tok", axis=0, tiled=False), 0)
-    last_squares = jnp.sum(last_part * last_part, -1)
-    packed = jnp.concatenate([last_part, last_squares[:, None]], 1)
-    blocks = lax.all_gather(packed, "mdl", axis=0, tiled=False)
-    last_rows = jnp.transpose(blocks[:, :, :feat_dev], (1, 0, 2)).reshape(req_count, model_width)
-    last_total = jnp.sum(blocks[:, :, feat_dev], 0)
+    by_mdl = lax.all_gather(last_res + last_down, "mdl", axis=0, tiled=False)
+    wide = jnp.transpose(by_mdl, (1, 0, 2)).reshape(req_count, model_width)
+    last_rows = jnp.sum(lax.all_gather(wide, "tok", axis=0, tiled=False), 0)
+    last_total = jnp.sum(last_rows * last_rows, -1)
     last_own = (
         last_rows * lax.rsqrt(last_total[:, None] / model_width + EPS) * final_gain
     ).astype(jnp.bfloat16)

time: 483 us -> 486 us (level)
  no operation moved by 1% of the time
where the time goes in v7:
time: 486 us; the launch traced here: 485 us
  blocking collectives  203 us (42%)
  waiting for transfers between devices  161 us (33%)
  matrix products  60 us (12%)
  other arithmetic  28.9 us (6%)
  between operations  17.2 us (4%)
  local copies, waits for them, and re-layouts  15.3 us (3%)
    reduce_scatter x1, waiting for transfers between devices, on_device(): lax.psum_scatter(partial_ffn.astype(jnp.bfloat16), 'mdl', scatter_dimensi...  53.2 us
    all_to_all x1, blocking collectives, scatter_sum(): pieces = lax.all_to_all(pieces, axis, 0, 0, tiled=False)  41 us
    unnamed x2, blocking collectives  35.4 us
    reduce_scatter x1, waiting for transfers between devices, on_device(): lax.psum_scatter(partial_qkv, 'mdl', scatter_dimension=0, tiled=True)  34.8 us
    all_gather x1, waiting for transfers between devices, on_device(): lax.all_gather(activated, 'mdl', axis=0, tiled=True)  29.8 us
    all_gather x1, waiting for transfers between devices, on_device(): lax.all_gather(attended, 'mdl', axis=0, tiled=True)  27 us
    all_gather x1, blocking collectives, on_device(): last_rows = jnp.sum(lax.all_gather(wide, 'tok', axis=0, tiled=False), 0)  24.6 us
    all_gather x1, blocking collectives, on_device(): suffix = lax.all_gather(appended, 'mdl', axis=0, tiled=True)  16.6 us
  transfers between devices with their start and end apart: 8, of which 6 were waited for; matrix products, arithmetic and copies ran while one was open for 6% of the time, Pallas kernels for 0%

profile of v7, /device:TPU:1, one launch (start us, length us, event | category | flops | bytes accessed | tf_op | source)
XLA Modules:
  0.0 485.4 jit_solution(625136463208839590)
XLA Ops:
  10.0 15.0 %psum.14 = f32[128]{0:T(128)S(1)} all-reduce(f32[128]{0:T(128)S(1)} %fusion.59), channel_id=1, replica_groups=mesh['grp'=4,'tok'=8,'mdl'=8] {'mdl'}, use_global_device_ids=true, to_apply=%region_1.0 | all-reduce | flops 128 | bytes 1024 | tf_op jit(solution)/shard_map/psum | solution.py:72
  24.9 14.3 %all-gather.4 = f32[8,1,128]{2,1,0:T(1,128)S(1)} all-gather(f32[1,1,128]{2,1,0:T(1,128)S(1)} %bitcast.197), channel_id=1, replica_groups=mesh['grp'=4,'tok'=8,'mdl'=8] {'tok'}, dimensions={0}, use_global_device_ids=true | all-gather | bytes 4608 | tf_op jit(solution)/shard_map/all_gather | solution.py:73
  39.3 9.1 %all-gather.22.cloned.1.call-done = bf16[1,1024,640]{2,1,0:T(8,128)(2,1)} async-done(((bf16[1,128,640]{2,1,0:T(8,128)(2,1)}), bf16[1,1024,640]{2,1,0:T(8,128)(2,1)}) %all-gather.22.cloned.1.call-update) | async-done | bytes 1310736 | tf_op jit(solution)/shard_map/all_gather | solution.py:71
  48.4 5.2 %fusion.21 = f32[1024,896]{0,1:T(8,128)} fusion(bf16[1,1024,640]{2,1,0:T(8,128)(2,1)} %all-gather.22.cloned.1.call-done, f32[640]{0:T(1024)} %param.21, f32[1024]{0:T(1024)S(1)} %bitcast.195, bf16[640,128]{1,0:T(8,128)(2,1)} %param.24, bf16[640,128]{1,0:T(8,128)(2,1)} %param.23, bf16[640,640]{1,0:T(8,128)(2,1)} %param.22), kind=kOutput, calls=%fused_computation.31 | convolution fusion | flops 1180467200 | bytes 6134272 | tf_op jit(solution)/shard_map/dot_general | solution.py:79
  60.7 34.8 %reduce-scatter.4.cloned.1.call-done = f32[128,896]{0,1:T(8,128)} async-done(((f32[1024,896]{0,1:T(8,128)}), f32[128,896]{0,1:T(8,128)}) %reduce-scatter.4.cloned.1.call-update) | async-done | bytes 458768 | tf_op jit(solution)/shard_map/reduce_scatter | solution.py:80
  98.3 1.8 copy.71
  102.1 16.6 %all_gather.48 = bf16[1024,1,256]{0,2,1:T(8,128)(2,1)} all-gather(bf16[128,1,256]{0,2,1:T(8,128)(2,1)S(1)} %get-tuple-element.23), channel_id=1, replica_groups=mesh['grp'=4,'tok'=8,'mdl'=8] {'mdl'}, dimensions={0}, use_global_device_ids=true | all-gather | bytes 589824 | tf_op jit(solution)/shard_map/all_gather | solution.py:105
  118.7 1.8 subtract_convert_fusion
  120.5 12.9 %fusion = (f32[128,5]{0,1:T(8,128)S(1)}, f32[128,5,8192]{2,0,1:T(8,128)}) fusion(pred[128,8192]{1,0:T(8,128)(4,1)} %broadcast_compare_fusion, bf16[8192,1,256]{2,0,1:T(8,128)(2,1)} %bitcast.199, bf16[128,5,64]{2,0,1:T(8,128)(2,1)} %get-tuple-element.15, bf16[128,5,64]{2,0,1:T(8,128)(2,1)} %get-tuple-element.14), kind=kOutput, calls=%fused_computation.3 | convolution fusion | flops 1358232960 | bytes 24447488 | tf_op jit(solution)/shard_map/rcgd,kcd->rcgk/dot_general | solution.py:137
  133.5 2.2 fusion.15
  135.7 14.1 %fusion.35 = f32[1,128,128,5]{2,1,3,0:T(8,128)} fusion(bf16[8192,1,256]{2,0,1:T(8,128)(2,1)} %bitcast.200, f32[128,5,8192]{2,0,1:T(8,128)} %get-tuple-element.33, f32[128,5]{0,1:T(8,128)S(1)} %max.19, pred[128,8192]{1,0:T(8,128)(4,1)} %broadcast_compare_fusion), kind=kOutput, calls=%fused_computation.42 | convolution fusion | flops 1368391680 | bytes 24447488 | tf_op jit(solution)/shard_map/rcgk,kcd->rcgd/dot_general | solution.py:147
  149.9 10.7 %fusion.1 = f32[128,5]{0,1:T(8,128)S(1)} fusion(f32[128,5,8192]{2,0,1:T(8,128)} %get-tuple-element.33, f32[128,5]{0,1:T(8,128)S(1)} %max.19, pred[128,8192]{1,0:T(8,128)(4,1)} %broadcast_compare_fusion), kind=kLoop, calls=%fused_computation.4 | loop fusion | flops 26213760 | bytes 22025216 | tf_op jit(solution)/shard_map/reduce_sum | solution.py:146
  163.2 27.0 %all-gather.16.cloned.1.call-done = bf16[1024,640]{0,1:T(8,128)(2,1)} async-done(((bf16[128,640]{0,1:T(8,128)(2,1)}), bf16[1024,640]{0,1:T(8,128)(2,1)}) %all-gather.16.cloned.1.call-update) | async-done | bytes 1310736 | tf_op jit(solution)/shard_map/all_gather | solution.py:159
  190.3 2.9 convolution_convert_fusion.1
  193.2 41.0 %all_to_all.5 = bf16[8,128,640]{2,1,0:T(8,128)(2,1)} all-to-all(bf16[8,128,640]{2,1,0:T(8,128)(2,1)S(1)} %bitcast.187), channel_id=1, replica_groups=mesh['grp'=4,'tok'=8,'mdl'=8] {'tok'}, dimensions={0} | all-to-all | bytes 2621440 | tf_op jit(solution)/shard_map/all_to_all | solution.py:31
  234.2 2.2 reduce_sum.154
  237.5 12.9 %psum.15 = f32[128]{0:T(128)S(1)} all-reduce(f32[128]{0:T(128)S(1)} %multiply_reduce_fusion.1), channel_id=1, replica_groups=mesh['grp'=4,'tok'=8,'mdl'=8] {'mdl'}, use_global_device_ids=true, to_apply=%region_14.15 | all-reduce | flops 128 | bytes 1024 | tf_op jit(solution)/shard_map/psum | solution.py:166
  250.4 10.6 %all-gather.5 = f32[8,1,128]{2,1,0:T(1,128)S(1)} all-gather(f32[1,1,128]{2,1,0:T(1,128)S(1)} %bitcast.198), channel_id=1, replica_groups=mesh['grp'=4,'tok'=8,'mdl'=8] {'tok'}, dimensions={0}, use_global_device_ids=true | all-gather | bytes 4608 | tf_op jit(solution)/shard_map/all_gather | solution.py:167
  260.9 5.8 %all-gather.18.cloned.1.call-done = bf16[1024,640]{1,0:T(8,128)(2,1)} async-done(((bf16[128,640]{1,0:T(8,128)(2,1)}), bf16[1024,640]{1,0:T(8,128)(2,1)}) %all-gather.18.cloned.1.call-update) | async-done | bytes 1310736 | tf_op jit(solution)/shard_map/all_gather | solution.py:165
  266.7 10.9 %convolution_convert_fusion = bf16[1024,3584]{1,0:T(8,128)(2,1)} fusion(bf16[640,1792]{1,0:T(8,128)(2,1)} %param.28, bf16[640,1792]{1,0:T(8,128)(2,1)} %param.27, bf16[1024,640]{1,0:T(8,128)(2,1)} %all-gather.18.cloned.1.call-done, bf16[1,1024,640]{2,1,0:T(8,128)(2,1)} %all-gather.22.cloned.1.call-done, f32[640]{0:T(1024)S(1)} %copy-done.10, ...), kind=kOutput, calls=%fused_computation.9 | convolution fusion | flops 4714397696 | bytes 14555648 | tf_op jit(solution)/shard_map/dot_general | solution.py:174
  277.7 53.2 %reduce-scatter.6.cloned.1.call-done = bf16[128,3584]{1,0:T(8,128)(2,1)} async-done(((bf16[1024,3584]{1,0:T(8,128)(2,1)}), bf16[128,3584]{1,0:T(8,128)(2,1)}) %reduce-scatter.6.cloned.1.call-update) | async-done | bytes 917520 | tf_op jit(solution)/shard_map/reduce_scatter | solution.py:175
  336.8 29.8 %all-gather.20.cloned.1.call-done = bf16[1024,1792]{1,0:T(8,128)(2,1)} async-done(((bf16[128,1792]{1,0:T(8,128)(2,1)}), bf16[1024,1792]{1,0:T(8,128)(2,1)}) %all-gather.20.cloned.1.call-update) | async-done | bytes 3670032 | tf_op jit(solution)/shard_map/all_gather | solution.py:180
  366.6 7.7 %fusion.86 = (bf16[1024,640]{1,0:T(8,128)(2,1)}, f32[1024,640]{1,0:T(8,128)}) fusion(bf16[1024,1792]{1,0:T(8,128)(2,1)} %all-gather.20.cloned.1.call-done, bf16[1792,640]{1,0:T(8,128)(2,1)} %param.29), kind=kOutput, calls=%fused_computation.146 | convolution fusion | flops 2349465600 | bytes 9895936 | tf_op jit(solution)/shard_map/dot_general | solution.py:179
  374.6 2.3 gather_fusion
  376.9 12.9 %all-gather.6 = f32[8,4,640]{2,1,0:T(4,128)S(1)} all-gather(f32[1,4,640]{2,1,0:T(4,128)S(1)} %add_bitcast_fusion), channel_id=3, replica_groups=mesh['grp'=4,'tok'=8,'mdl'=8] {'mdl'}, dimensions={0}, use_global_device_ids=true | all-gather | bytes 92160 | tf_op jit(solution)/shard_map/all_gather | solution.py:199
  389.8 24.6 %all_gather.55 = f32[8,4,5120]{2,1,0:T(4,128)} all-gather(f32[1,4,5120]{2,1,0:T(4,128)S(1)} %bitcast.189), channel_id=1, replica_groups=mesh['grp'=4,'tok'=8,'mdl'=8] {'tok'}, dimensions={0}, use_global_device_ids=true | all-gather | bytes 737280 | tf_op jit(solution)/shard_map/all_gather | solution.py:201
  415.9 10.8 %all-gather.7 = bf16[4,4,5120]{2,1,0:T(4,128)(2,1)} all-gather(bf16[1,4,5120]{2,1,0:T(4,128)(2,1)S(1)} %fusion.68), channel_id=1, replica_groups=mesh['grp'=4,'tok'=8,'mdl'=8] {'grp'}, dimensions={0}, use_global_device_ids=true | all-gather | bytes 204800 | tf_op jit(solution)/shard_map/all_gather | solution.py:206
  428.2 2.6 fusion.87
  430.8 1.7 multiply_reduce_fusion
  432.8 12.5 %all-reduce = f32[160]{0:T(256)S(1)} all-reduce(f32[160]{0:T(256)S(1)} %maximum_dynamic-update-slice_fusion), channel_id=4, replica_groups=mesh['grp'=4,'tok'=8,'mdl'=8] {'tok'}, use_global_device_ids=true, to_apply=%add | all-reduce | flops 160 | bytes 1280
  445.6 23.0 %all-reduce.1 = f32[160]{0:T(256)S(1)} all-reduce(f32[160]{0:T(256)S(1)} %maximum_dynamic-update-slice_fusion.1), channel_id=5, replica_groups=mesh['grp'=4,'tok'=8,'mdl'=8] {'mdl'}, use_global_device_ids=true, to_apply=%add.1 | all-reduce | flops 160 | bytes 1280
  469.4 8.6 %pmax.7 = f32[4,4]{1,0:T(4,128)} all-reduce(f32[4,4]{1,0:T(4,128)S(1)} %reshape.487), channel_id=1, replica_groups=mesh['grp'=4,'tok'=8,'mdl'=8] {'grp'}, use_global_device_ids=true, to_apply=%region_27.28 | all-reduce | flops 16 | bytes 128 | tf_op jit(solution)/shard_map/pmax | solution.py:218
  (110 shorter events, 26.8 us)
Async XLA Ops:
  8.0 420.2 %copy-start = (bf16[300,5120]{1,0:T(8,128)(2,1)S(1)}, bf16[300,5120]{1,0:T(8,128)(2,1)}, u32[]{:S(2)}) copy-start(bf16[300,5120]{1,0:T(8,128)(2,1)} %param.31) | copy-start | bytes 9216004
  8.0 40.4 %all-gather.22.cloned.1.call-start = ((), (), s32[]{:S(2)}) async-start(), calls=%async_computation.11 | async-start | bytes 1474560 | tf_op jit(solution)/shard_map/all_gather | solution.py:71
  8.7 86.7 %reduce-scatter.4.cloned.1.call-start = ((), (), s32[]{:S(2)}) async-start(), calls=%async_computation.4 | async-start | bytes 4128768 | tf_op jit(solution)/shard_map/reduce_scatter | solution.py:80
  53.6 0.7 copy-start.11
  53.7 66.9 %all-gather.14.cloned.1.call-start = ((), (), s32[]{:S(2)}) async-start(), calls=%async_computation.5 | async-start | bytes 4325376 | tf_op jit(solution)/shard_map/all_gather | solution.py:131
  54.2 136.0 %all-gather.16.cloned.1.call-start = ((), (), s32[]{:S(2)}) async-start(), calls=%async_computation.6 | async-start | bytes 1474560 | tf_op jit(solution)/shard_map/all_gather | solution.py:159
  120.5 13.0 %copy-start.4 = (bf16[1024,1,256]{0,2,1:T(8,128)(2,1)S(1)}, bf16[1024,1,256]{0,2,1:T(8,128)(2,1)}, u32[]{:S(2)}) copy-start(bf16[1024,1,256]{0,2,1:T(8,128)(2,1)} %all_gather.48) | copy-start | bytes 1572868
  120.5 13.0 %copy-start.6 = (pred[128,1024]{0,1:T(8,128)(4,1)S(1)}, pred[128,1024]{0,1:T(8,128)(4,1)}, u32[]{:S(2)}) copy-start(pred[128,1024]{0,1:T(8,128)(4,1)} %fusion.56) | copy-start | bytes 393220
  120.5 13.0 %copy-start.7 = (bf16[128,5,64]{2,0,1:T(8,128)(2,1)S(1)}, bf16[128,5,64]{2,0,1:T(8,128)(2,1)}, u32[]{:S(2)}) copy-start(bf16[128,5,64]{2,0,1:T(8,128)(2,1)} %get-tuple-element.14) | copy-start | bytes 245764
  120.5 13.0 %copy-start.8 = (bf16[128,5,64]{2,0,1:T(8,128)(2,1)S(1)}, bf16[128,5,64]{2,0,1:T(8,128)(2,1)}, u32[]{:S(2)}) copy-start(bf16[128,5,64]{2,0,1:T(8,128)(2,1)} %get-tuple-element.15) | copy-start | bytes 245764
  149.9 10.7 %copy-start.1 = (f32[1024,128,5]{1,0,2:T(8,128)S(1)}, f32[1024,128,5]{1,0,2:T(8,128)}, u32[]{:S(2)}) copy-start(f32[1024,128,5]{1,0,2:T(8,128)} %get-tuple-element.31) | copy-start | bytes 7864324
  160.6 1.0 copy-start.5
  160.6 1.1 copy-start.14
  163.2 103.5 %all-gather.18.cloned.1.call-start = ((), (), s32[]{:S(2)}) async-start(), calls=%async_computation.7 | async-start | bytes 1474560 | tf_op jit(solution)/shard_map/all_gather | solution.py:165
  193.2 43.3 %copy-start.2 = (bf16[1,128,640]{2,1,0:T(8,128)(2,1)S(1)}, bf16[1,128,640]{2,1,0:T(8,128)(2,1)}, u32[]{:S(2)}) copy-start(bf16[1,128,640]{2,1,0:T(8,128)(2,1)} %param.16) | copy-start | bytes 491524
  193.2 73.5 %copy-start.10 = (f32[640]{0:T(1024)S(1)}, f32[640]{0:T(1024)}, u32[]{:S(2)}) copy-start(f32[640]{0:T(1024)} %param.26) | copy-start | bytes 7684
  236.4 94.6 %reduce-scatter.6.cloned.1.call-start = ((), (), s32[]{:S(2)}) async-start(), calls=%async_computation.8 | async-start | bytes 8257536 | tf_op jit(solution)/shard_map/reduce_scatter | solution.py:175
  277.7 55.8 %copy-start.13 = (u32[256]{0:T(256)S(1)}, u32[256]{0:T(256)}, u32[]{:S(2)}) copy-start(u32[256]{0:T(256)} %constant.117) | copy-start | bytes 3076
  277.7 56.4 %copy-start.12 = (u32[256]{0:T(256)S(1)}, u32[256]{0:T(256)}, u32[]{:S(2)}) copy-start(u32[256]{0:T(256)} %constant.112) | copy-start | bytes 3076
  277.7 88.9 %all-gather.20.cloned.1.call-start = ((), (), s32[]{:S(2)}) async-start(), calls=%async_computation.9 | async-start | bytes 4128768 | tf_op jit(solution)/shard_map/all_gather | solution.py:180
  333.4 97.4 %reduce-scatter.8.cloned.1.call-start = ((), (), s32[]{:S(2)}) async-start(), calls=%async_computation.10 | async-start | bytes 1474560 | tf_op jit(solution)/shard_map/reduce_scatter | solution.py:184
  336.8 37.5 %copy-start.3 = (bf16[128,640]{1,0:T(8,128)(2,1)S(1)}, bf16[128,640]{1,0:T(8,128)(2,1)}, u32[]{:S(2)}) copy-start(bf16[128,640]{1,0:T(8,128)(2,1)} %reduce_sum.154) | copy-start | bytes 491524
  374.3 41.5 %copy-start.9 = (f32[5120]{0:T(1024)S(1)}, f32[5120]{0:T(1024)}, u32[]{:S(2)}) copy-start(f32[5120]{0:T(1024)} %param.30) | copy-start | bytes 61444
Sparse Core Ops, SparseCore 0:
  10.6 37.7 all-gather.21
  53.8 41.6 reduce-scatter.3
  163.3 26.8 all-gather.15
  236.5 30.1 all-gather.17
  277.8 53.1 reduce-scatter.5
  333.5 33.0 all-gather.19
  374.4 35.6 reduce-scatter.7
Sparse Core Ops, SparseCore 1:
  56.7 56.3 all-gather.13
